TPU v7x, 32 devices: a whole 2x2x4 slice. The times are simulated.
32 devices in a mesh: groups: 2 (over y), ctx: 4 (over z), head: 2 (over x), rep: 2 (over core).
Axes of the slice: x: 2, y: 2, z: 4, core: 2. Of those that a mesh axis runs over, the one named last changes fastest.
Arguments:
- queries: bfloat16 [4, 512, 1024], P(('groups', 'rep'), 'ctx', 'head'), parts along dimension 0, may hold values from -6 to 6
- per_head_keys: bfloat16 [4, 512, 1024], P(('groups', 'rep'), 'ctx', 'head'), parts along dimension 0, may hold values from -6 to 6
- value_rows: bfloat16 [4, 512, 1024], P(('groups', 'rep'), 'ctx', 'head'), parts along dimension 0, may hold values from -6 to 6
- gate_logits: bfloat16 [4, 512, 1024], P(('groups', 'rep'), 'ctx', 'head'), parts along dimension 0, may hold values from -16 to 4
- gate_bias: float32 [1024], P('head'), may hold values from -1 to 13
- value_weight: float32 [1024], P('head'), may hold values from -0.1875 to 0.1875
- targets: float32 [4, 512], P(('groups', 'rep'), 'ctx'), parts along dimension 0, may hold values from -6 to 6
- mask_ids: int32 [4, 4], P(('groups', 'rep'), 'ctx'), parts along dimension 0, may hold values from 0 to 3
- segment_starts: int32 [4, 512], P(('groups', 'rep'), 'ctx'), parts along dimension 0, may hold values 0 or 1
Outputs:
- value_pred: float32 [4, 512], P(('groups', 'rep'), 'ctx'), parts along dimension 0
- query_gradient_rows: bfloat16 [4, 512, 1024], P(('groups', 'rep'), 'ctx', 'head'), parts along dimension 0
- grad_keys: bfloat16 [4, 512, 1024], P(('groups', 'rep'), 'ctx', 'head'), parts along dimension 0
- grad_values: bfloat16 [4, 512, 1024], P(('groups', 'rep'), 'ctx', 'head'), parts along dimension 0
- grad_gate_logits: bfloat16 [4, 512, 1024], P(('groups', 'rep'), 'ctx', 'head'), parts along dimension 0
- grad_gate_bias: float32 [2048], P(('groups', 'head')), parts along dimension 0
- grad_value_weight: float32 [2048], P(('groups', 'head')), parts along dimension 0
There are 2 independent parts, one for each index of `groups`. A program takes and returns all parts, laid end to end along the dimension named above; an argument that names none is the same for every part. Nothing has to cross between parts.
Inputs may be any that keep to these rules, and one draw needn't show every extreme that they name: `mask_ids`: the window kind of each block of 128 positions. `segment_starts`: flags of segment starts.
All inputs are finite; a program needn't handle non-finite values. No bound on the sum of `segment_starts` on one device may be relied on, other than what follows from the above.
Results may differ from a plain program's by a relative error of at most 0.013.
Values sent between devices are 32-bit elements; how exact they have to be, the bound alone decides.
No kernel may reach another device: no remote copies, remote signals or barrier semaphores. Data moves between devices by JAX's collectives and lax.ppermute only.
A program may use at most 64 MiB of HBM per device.

v0:
```python
import jax
import jax.numpy as jnp
from jax import lax
from jax.sharding import PartitionSpec as P

DK = 128
DV = 128


epsilon = 1.0
gate_scale = 16.0
highest = lax.Precision.HIGHEST


def from_behind(value, axis, by):
    length = lax.axis_size(axis)
    pairs = [(i, i + by) for i in range(length) if 0 <= i + by < length]
    return lax.ppermute(value, axis, pairs)


def block_pass(query_in, key_in, value_in, decay, start_flags, kind_ids):
    blocks = kind_ids.shape[0]
    block_len = query_in.shape[0] // blocks
    head_count = query_in.shape[1]
    channels = query_in.shape[2]
    value_width = value_in.shape[2]
    query_f = query_in.astype(jnp.float32).reshape(blocks, block_len, head_count, channels)
    key_f = key_in.astype(jnp.float32).reshape(blocks, block_len, head_count, channels)
    value_bf = value_in.reshape(blocks, block_len, head_count, value_width)
    value_f = value_bf.astype(jnp.float32)
    log_cum = jnp.cumsum(decay.reshape(blocks, block_len, head_count, channels), axis=1)
    log_last = log_cum[:, -1]
    segment = jnp.cumsum(start_flags.reshape(blocks, block_len), axis=1, dtype=jnp.int32)
    alive_mask = (segment == 0).astype(jnp.float32)
    offsets = jnp.arange(block_len, dtype=jnp.int32)
    distance = offsets[:, None] - offsets[None, :]
    window = block_len // jnp.left_shift(jnp.ones_like(kind_ids), kind_ids)
    live_pairs = (
        (segment[:, :, None] == segment[:, None, :])
        & (distance[None] >= 0)
        & (distance[None] < window[:, None, None])
    )
    query_dec = query_f * jnp.exp(log_cum) * channels ** (-0.5)
    key_dec = key_f * jnp.exp(-log_cum)
    scores = jnp.einsum("bihc,bjhc->bhij", query_dec, key_dec, precision=highest)
    block_probs = jnp.where(live_pairs[:, None], scores, 0.0).astype(jnp.bfloat16)
    inner_part = jnp.einsum(
        "bhij,bjhd->bihd", block_probs, value_bf, preferred_element_type=jnp.float32
    )
    tail_mask = (segment == segment[:, -1:]).astype(jnp.float32)
    key_tail = key_f * jnp.exp(log_last[:, None] - log_cum) * tail_mask[:, :, None, None]
    block_state = jnp.einsum("bjhc,bjhd->bhcd", key_tail, value_f, precision=highest)
    block_decay = jnp.exp(log_last) * alive_mask[:, -1][:, None, None]

    def advance(carried_in, block_items):
        state_now, factor = carried_in
        new_state = state_now * block_items[1][..., None] + block_items[0]
        return ((new_state, factor * block_items[1]), (state_now, factor))

    initial = (
        jnp.zeros((head_count, channels, value_width), jnp.float32),
        jnp.ones((head_count, channels), jnp.float32),
    )
    finals, befores = lax.scan(advance, initial, (block_state, block_decay))
    query_live = query_dec * alive_mask[:, :, None, None]
    outer_part = jnp.einsum("bihc,bhcd->bihd", query_live, befores[0], precision=highest)
    carried = query_live * befores[1][:, None]
    attended = (inner_part + outer_part).reshape(blocks * block_len, head_count, value_width)
    return (
        attended,
        finals[0],
        finals[1],
        carried.reshape(blocks * block_len, head_count, channels),
    )


def on_device(
    queries,
    per_head_keys,
    value_rows,
    gate_logits,
    gate_bias,
    value_weight,
    targets,
    mask_ids,
    segment_starts,
):
    token_count = queries.shape[1]
    head_count = gate_bias.shape[0] // DK

    def to_heads(array):
        return array[0].reshape(token_count, head_count, -1)

    start_flags = segment_starts[0]
    kind_ids = mask_ids[0]

    def local_terms(query_in, key_in, value_in, logit_in, bias_in):
        decay = jax.nn.log_sigmoid(logit_in.astype(jnp.float32) + bias_in) / gate_scale
        return block_pass(query_in, key_in, value_in, decay, start_flags, kind_ids)

    local_out, pull_local = jax.vjp(
        local_terms,
        to_heads(queries),
        to_heads(per_head_keys),
        to_heads(value_rows),
        to_heads(gate_logits),
        gate_bias.reshape(head_count, DK),
    )
    attended_local, state_local, decay_local, carried = local_out

    def pass_state(position, incoming):
        return from_behind(incoming * decay_local[..., None] + state_local, "ctx", 1)

    state_in = lax.fori_loop(0, lax.axis_size("ctx") - 1, pass_state, jnp.zeros_like(state_local))
    attended = attended_local + jnp.einsum("thc,hcd->thd", carried, state_in, precision=highest)

    def value_head(attended_in, weight_in):
        normed = attended_in * lax.rsqrt(
            jnp.mean(attended_in * attended_in, axis=-1, keepdims=True) + epsilon
        )
        return jnp.einsum("thd,hd->t", normed, weight_in, precision=highest)

    partial_value, pull_value = jax.vjp(value_head, attended, value_weight.reshape(head_count, DV))
    value_pred = lax.psum(partial_value, "head")
    residual = value_pred - targets[0]
    grad_attended, grad_weight = pull_value(residual)
    grad_carried = jnp.einsum("thd,hcd->thc", grad_attended, state_in, precision=highest)
    grad_direct = jnp.einsum("thc,thd->hcd", carried, grad_attended, precision=highest)

    def pass_grad(position, incoming):
        return from_behind(grad_direct + decay_local[..., None] * incoming, "ctx", -1)

    grad_state = lax.fori_loop(0, lax.axis_size("ctx") - 1, pass_grad, jnp.zeros_like(grad_direct))
    grad_decay = jnp.sum(state_in * grad_state, axis=-1)
    grad_query, grad_key, grad_value, grad_logit, grad_bias = pull_local(
        (grad_attended, grad_state, grad_decay, grad_carried)
    )
    token_total = token_count * lax.axis_size("ctx") * lax.axis_size("rep")
    bias_total, weight_total = lax.psum(
        (grad_bias.reshape(-1), grad_weight.reshape(-1)), ("ctx", "rep")
    )
    return (
        value_pred[None],
        grad_query.reshape(1, token_count, -1),
        grad_key.reshape(1, token_count, -1),
        grad_value.reshape(1, token_count, -1),
        grad_logit.reshape(1, token_count, -1),
        bias_total / token_total,
        weight_total / token_total,
    )


def solution(mesh):
    in_specs = (
        P(("groups", "rep"), "ctx", "head"),
        P(("groups", "rep"), "ctx", "head"),
        P(("groups", "rep"), "ctx", "head"),
        P(("groups", "rep"), "ctx", "head"),
        P("head"),
        P("head"),
        P(("groups", "rep"), "ctx"),
        P(("groups", "rep"), "ctx"),
        P(("groups", "rep"), "ctx"),
    )
    out_specs = (
        P(("groups", "rep"), "ctx"),
        P(("groups", "rep"), "ctx", "head"),
        P(("groups", "rep"), "ctx", "head"),
        P(("groups", "rep"), "ctx", "head"),
        P(("groups", "rep"), "ctx", "head"),
        P(("groups", "head")),
        P(("groups", "head")),
    )
    return jax.shard_map(
        on_device, mesh=mesh, in_specs=in_specs, out_specs=out_specs, check_vma=False
    )
```

profile of v0, /device:TPU:0, one launch (start us, length us, event | category | flops | bytes accessed | tf_op | source)
XLA Modules:
  0.0 105.6 jit_solution(13447743507898511805)
XLA Ops:
  0.6 1.0 reshape.486
  1.7 0.4 fusion.9
  2.0 0.6 copy-done.13
  3.0 0.6 slice.11
  4.2 0.6 slice.12
  4.8 1.2 %compare_convert_fusion.1 = (f32[128]{0:T(128)}, f32[128]{0:T(128)S(1)}) fusion(s32[1,128]{1,0:T(1,128)S(1)} %reduce_window_sum.35, s32[]{:T(128)} %bitcast.14), kind=kLoop, calls=%fused_computation.129 | loop fusion | flops 512 | bytes 1540 | tf_op jit(solution)/shard_map/jvp()/convert_element_type | solution.py:34
  6.3 0.8 copy-done.2
  7.1 0.5 convolution_add_fusion
  7.6 28.2 %while.4 = (s32[]{:T(128)}, f32[4,128,128]{2,1,0:T(8,128)S(1)}, f32[4,128]{1,0:T(4,128)S(1)}, f32[4,128,128]{2,1,0:T(8,128)S(1)}, s32[]{:T(128)}) while((s32[]{:T(128)}, f32[4,128,128]{2,1,0:T(8,128)S(1)}, f32[4,128]{1,0:T(4,128)S(1)}, f32[4,128,128]{2,1,0:T(8,128)S(1)}, s32[]{:T(128)}) %tuple.61), condition=%wide.region_3.4_spmd, body=%wide.region_2.3_spmd.sunk | while | flops 131074 | bytes 1837157 | solution.py:114
  7.8 4.9 %collective-permute-start = (f32[4,128,128]{2,1,0:T(8,128)S(1)}, f32[4,128,128]{2,1,0:T(8,128)S(1)}, u32[]{:S(2)}, u32[]{:S(2)}) collective-permute-start(f32[4,128,128]{2,1,0:T(8,128)S(1)} %multiply_add_fusion.5), channel_id=1, source_target_pairs={{0,4},{4,8},{8,12},{1,5},{5,9},{9,13},{2,6},{6,10},{10,14},{3,7},{... | collective-permute-start | bytes 786440 | tf_op jit(solution)/shard_map/while/body/eval_jaxpr/ppermute | solution.py:18
  12.7 5.5 %collective-permute-done = f32[4,128,128]{2,1,0:T(8,128)S(1)} collective-permute-done((f32[4,128,128]{2,1,0:T(8,128)S(1)}, f32[4,128,128]{2,1,0:T(8,128)S(1)}, u32[]{:S(2)}, u32[]{:S(2)}) %collective-permute-start) | collective-permute-done | bytes 262176 | tf_op jit(solution)/shard_map/while/body/eval_jaxpr/ppermute | solution.py:18
  18.4 4.4 %collective-permute-start = (f32[4,128,128]{2,1,0:T(8,128)S(1)}, f32[4,128,128]{2,1,0:T(8,128)S(1)}, u32[]{:S(2)}, u32[]{:S(2)}) collective-permute-start(f32[4,128,128]{2,1,0:T(8,128)S(1)} %multiply_add_fusion.5), channel_id=1, source_target_pairs={{0,4},{4,8},{8,12},{1,5},{5,9},{9,13},{2,6},{6,10},{10,14},{3,7},{... | collective-permute-start | bytes 786440 | tf_op jit(solution)/shard_map/while/body/eval_jaxpr/ppermute | solution.py:18
  22.8 4.7 %collective-permute-done = f32[4,128,128]{2,1,0:T(8,128)S(1)} collective-permute-done((f32[4,128,128]{2,1,0:T(8,128)S(1)}, f32[4,128,128]{2,1,0:T(8,128)S(1)}, u32[]{:S(2)}, u32[]{:S(2)}) %collective-permute-start) | collective-permute-done | bytes 262176 | tf_op jit(solution)/shard_map/while/body/eval_jaxpr/ppermute | solution.py:18
  27.6 4.4 %collective-permute-start = (f32[4,128,128]{2,1,0:T(8,128)S(1)}, f32[4,128,128]{2,1,0:T(8,128)S(1)}, u32[]{:S(2)}, u32[]{:S(2)}) collective-permute-start(f32[4,128,128]{2,1,0:T(8,128)S(1)} %multiply_add_fusion.5), channel_id=1, source_target_pairs={{0,4},{4,8},{8,12},{1,5},{5,9},{9,13},{2,6},{6,10},{10,14},{3,7},{... | collective-permute-start | bytes 786440 | tf_op jit(solution)/shard_map/while/body/eval_jaxpr/ppermute | solution.py:18
  32.0 3.9 %collective-permute-done = f32[4,128,128]{2,1,0:T(8,128)S(1)} collective-permute-done((f32[4,128,128]{2,1,0:T(8,128)S(1)}, f32[4,128,128]{2,1,0:T(8,128)S(1)}, u32[]{:S(2)}, u32[]{:S(2)}) %collective-permute-start) | collective-permute-done | bytes 262176 | tf_op jit(solution)/shard_map/while/body/eval_jaxpr/ppermute | solution.py:18
  37.0 0.7 fusion.2
  37.9 0.7 fusion.1
  38.6 0.7 multiply_reduce_fusion.2
  39.4 0.6 copy-done.4
  40.3 4.9 %psum.21 = f32[128]{0:T(128)S(1)} all-reduce(f32[128]{0:T(128)S(1)} %convolution_bitcast_fusion.2), channel_id=1, replica_groups=mesh['groups'=2,'ctx'=4,'head'=2,'rep'=2] {'head'}, use_global_device_ids=true, to_apply=%region_5.6 | all-reduce | flops 128 | bytes 1024 | tf_op jit(solution)/shard_map/psum | solution.py:124
  45.2 0.5 copy-done.15
  45.9 0.7 fusion.60
  46.6 28.3 %while.5 = (s32[]{:T(128)}, f32[4,128,128]{2,1,0:T(8,128)S(1)}, f32[4,128]{1,0:T(4,128)S(1)}, f32[4,128,128]{2,1,0:T(8,128)S(1)}, s32[]{:T(128)}) while((s32[]{:T(128)}, f32[4,128,128]{2,1,0:T(8,128)S(1)}, f32[4,128]{1,0:T(4,128)S(1)}, f32[4,128,128]{2,1,0:T(8,128)S(1)}, s32[]{:T(128)}) %tuple.67), condition=%wide.region_8.9_spmd, body=%wide.region_7.8_spmd.sunk | while | flops 131074 | bytes 1837157 | solution.py:133
  46.8 1.3 %collective-permute-start.1 = (f32[4,128,128]{2,1,0:T(8,128)S(1)}, f32[4,128,128]{2,1,0:T(8,128)S(1)}, u32[]{:S(2)}, u32[]{:S(2)}) collective-permute-start(f32[4,128,128]{2,1,0:T(8,128)S(1)} %multiply_add_fusion.6), channel_id=1, source_target_pairs={{4,0},{8,4},{12,8},{5,1},{9,5},{13,9},{6,2},{10,6},{14,10},{7,3},{... | collective-permute-start | bytes 786440 | tf_op jit(solution)/shard_map/while/body/eval_jaxpr/ppermute | solution.py:18
  48.1 7.9 %collective-permute-done.1 = f32[4,128,128]{2,1,0:T(8,128)S(1)} collective-permute-done((f32[4,128,128]{2,1,0:T(8,128)S(1)}, f32[4,128,128]{2,1,0:T(8,128)S(1)}, u32[]{:S(2)}, u32[]{:S(2)}) %collective-permute-start.1) | collective-permute-done | bytes 262176 | tf_op jit(solution)/shard_map/while/body/eval_jaxpr/ppermute | solution.py:18
  56.1 1.3 %collective-permute-start.1 = (f32[4,128,128]{2,1,0:T(8,128)S(1)}, f32[4,128,128]{2,1,0:T(8,128)S(1)}, u32[]{:S(2)}, u32[]{:S(2)}) collective-permute-start(f32[4,128,128]{2,1,0:T(8,128)S(1)} %multiply_add_fusion.6), channel_id=1, source_target_pairs={{4,0},{8,4},{12,8},{5,1},{9,5},{13,9},{6,2},{10,6},{14,10},{7,3},{... | collective-permute-start | bytes 786440 | tf_op jit(solution)/shard_map/while/body/eval_jaxpr/ppermute | solution.py:18
  57.4 8.8 %collective-permute-done.1 = f32[4,128,128]{2,1,0:T(8,128)S(1)} collective-permute-done((f32[4,128,128]{2,1,0:T(8,128)S(1)}, f32[4,128,128]{2,1,0:T(8,128)S(1)}, u32[]{:S(2)}, u32[]{:S(2)}) %collective-permute-start.1) | collective-permute-done | bytes 262176 | tf_op jit(solution)/shard_map/while/body/eval_jaxpr/ppermute | solution.py:18
  66.3 1.3 %collective-permute-start.1 = (f32[4,128,128]{2,1,0:T(8,128)S(1)}, f32[4,128,128]{2,1,0:T(8,128)S(1)}, u32[]{:S(2)}, u32[]{:S(2)}) collective-permute-start(f32[4,128,128]{2,1,0:T(8,128)S(1)} %multiply_add_fusion.6), channel_id=1, source_target_pairs={{4,0},{8,4},{12,8},{5,1},{9,5},{13,9},{6,2},{10,6},{14,10},{7,3},{... | collective-permute-start | bytes 786440 | tf_op jit(solution)/shard_map/while/body/eval_jaxpr/ppermute | solution.py:18
  67.6 7.3 %collective-permute-done.1 = f32[4,128,128]{2,1,0:T(8,128)S(1)} collective-permute-done((f32[4,128,128]{2,1,0:T(8,128)S(1)}, f32[4,128,128]{2,1,0:T(8,128)S(1)}, u32[]{:S(2)}, u32[]{:S(2)}) %collective-permute-start.1) | collective-permute-done | bytes 262176 | tf_op jit(solution)/shard_map/while/body/eval_jaxpr/ppermute | solution.py:18
  74.9 0.8 multiply_reduce_fusion
  75.7 0.5 fusion.100
  76.3 0.5 fusion.33
  77.3 0.6 fusion.79
  77.9 0.8 copy.145
  78.8 0.6 fusion.56
  79.5 0.4 fusion.75
  80.2 1.4 %fusion.98 = (f32[4,128]{1,0:T(4,128)S(1)}, bf16[1,128,4,128]{3,2,1,0:T(4,128)(2,1)S(1)}, bf16[1,128,4,128]{3,2,1,0:T(4,128)(2,1)S(1)}, f32[1,128,4,128]{3,2,1,0:T(4,128)S(1)}) fusion(f32[1,128,4,128]{3,2,1,0:T(4,128)S(1)} %fusion.9, f32[4,128]{1,0:T(4,128)S(1)} %slice_bitcast_fusion, f32[1,128,4,128]{3,2,1,0:T(4,128)S(1)} %copy.167, f32[128]{0:T(128)} %copy-done.9, ...), kind=kLoop, calls=%fused_computation.145 | loop fusion | flops 1048064 | bytes 2364416 | tf_op jit(solution)/shard_map/transpose(jvp())/reduce_sum | solution.py:51
  81.8 0.7 copy-done
  82.6 0.8 reshape.491
  83.4 2.9 %fusion.55 = (f32[4,128]{1,0:T(4,128)S(1)}, f32[1,128,4,128]{3,2,1,0:T(4,128)S(1)}) fusion(f32[128,4,128]{2,1,0:T(4,128)} %reshape.491, f32[4,128]{1,0:T(4,128)S(1)} %bitcast.191, f32[1,128,4,128]{3,2,1,0:T(4,128)S(1)} %copy.167, f32[4,128,128]{2,0,1:T(4,128)S(1)} %copy.151, f32[1,1,4,128]{3,2,1,0:T(4,128)S(1)} %bitcast_add_fusion.2, ...), kind=kOutput, calls=%fused_computation.89 | output fusion | flops 10354176 | bytes 2105856 | tf_op jit(solution)/shard_map/transpose(jvp(jit(cumsum)))/reduce_window_sum | solution.py:31
  86.3 0.6 copy-done.6
  87.3 13.6 %all-reduce.1 = (f32[512]{0:T(512)S(1)}, f32[512]{0:T(512)S(1)}) all-reduce(f32[512]{0:T(512)S(1)} %negate_bitcast_fusion, f32[512]{0:T(512)S(1)} %bitcast.192), channel_id=1, replica_groups=mesh['groups'=2,'ctx'=4,'head'=2,'rep'=2] {'ctx','rep'}, use_global_device_ids=true, to_apply=%region_14.15 | all-reduce | flops 1024 | bytes 8192 | tf_op jit(solution)/shard_map/psum | solution.py:139
  100.9 0.6 broadcast_multiply_fusion.1
  101.6 0.9 fusion.15
  102.5 0.6 convolution_convert_fusion
  103.4 0.8 copy.155
  104.1 0.7 convert_element_type.156
  104.9 0.7 convert_element_type.158
  (67 shorter events, 4.5 us)
Async XLA Ops:
  0.6 1.0 copy-start.7
  1.6 4.3 %copy-start.1 = (bf16[1,128,512]{2,1,0:T(8,128)(2,1)S(1)}, bf16[1,128,512]{2,1,0:T(8,128)(2,1)}, u32[]{:S(2)}) copy-start(bf16[1,128,512]{2,1,0:T(8,128)(2,1)} %param.14) | copy-start | bytes 393220
  2.0 0.7 copy-start.13
  6.0 1.1 %copy-start.9 = (f32[128]{0:T(128)}, f32[128]{0:T(128)S(1)}, u32[]{:S(2)}) copy-start(f32[128]{0:T(128)S(1)} %get-tuple-element.174) | copy-start | bytes 1540
  6.1 0.9 copy-start.2
  7.6 29.0 %copy-start.3 = (bf16[1,128,512]{2,1,0:T(8,128)(2,1)S(1)}, bf16[1,128,512]{2,1,0:T(8,128)(2,1)}, u32[]{:S(2)}) copy-start(bf16[1,128,512]{2,1,0:T(8,128)(2,1)} %param.13) | copy-start | bytes 393220
  7.8 10.5 %collective-permute-start = (f32[4,128,128]{2,1,0:T(8,128)S(1)}, f32[4,128,128]{2,1,0:T(8,128)S(1)}, u32[]{:S(2)}, u32[]{:S(2)}) collective-permute-start(f32[4,128,128]{2,1,0:T(8,128)S(1)} %multiply_add_fusion.5), channel_id=1, source_target_pairs={{0,4},{4,8},{8,12},{1,5},{5,9},{9,13},{2,6},{6,10},{10,14},{3,7},{... | collective-permute-start | bytes 786440 | tf_op jit(solution)/shard_map/while/body/eval_jaxpr/ppermute | solution.py:18
  18.4 9.1 %collective-permute-start = (f32[4,128,128]{2,1,0:T(8,128)S(1)}, f32[4,128,128]{2,1,0:T(8,128)S(1)}, u32[]{:S(2)}, u32[]{:S(2)}) collective-permute-start(f32[4,128,128]{2,1,0:T(8,128)S(1)} %multiply_add_fusion.5), channel_id=1, source_target_pairs={{0,4},{4,8},{8,12},{1,5},{5,9},{9,13},{2,6},{6,10},{10,14},{3,7},{... | collective-permute-start | bytes 786440 | tf_op jit(solution)/shard_map/while/body/eval_jaxpr/ppermute | solution.py:18
  27.6 8.3 %collective-permute-start = (f32[4,128,128]{2,1,0:T(8,128)S(1)}, f32[4,128,128]{2,1,0:T(8,128)S(1)}, u32[]{:S(2)}, u32[]{:S(2)}) collective-permute-start(f32[4,128,128]{2,1,0:T(8,128)S(1)} %multiply_add_fusion.5), channel_id=1, source_target_pairs={{0,4},{4,8},{8,12},{1,5},{5,9},{9,13},{2,6},{6,10},{10,14},{3,7},{... | collective-permute-start | bytes 786440 | tf_op jit(solution)/shard_map/while/body/eval_jaxpr/ppermute | solution.py:18
  39.3 0.7 copy-start.4
  40.2 5.0 %copy-start.14 = (f32[1,128]{1,0:T(1,128)S(1)}, f32[1,128]{1,0:T(1,128)}, u32[]{:S(2)}) copy-start(f32[1,128]{1,0:T(1,128)} %param.19) | copy-start | bytes 1540
  45.2 0.5 copy-start.15
  45.7 31.3 %copy-start.5 = (f32[128]{0:T(128)}, f32[128]{0:T(128)S(1)}, u32[]{:S(2)}) copy-start(f32[128]{0:T(128)S(1)} %bitcast_subtract_fusion.1) | copy-start | bytes 1540
  46.8 9.2 %collective-permute-start.1 = (f32[4,128,128]{2,1,0:T(8,128)S(1)}, f32[4,128,128]{2,1,0:T(8,128)S(1)}, u32[]{:S(2)}, u32[]{:S(2)}) collective-permute-start(f32[4,128,128]{2,1,0:T(8,128)S(1)} %multiply_add_fusion.6), channel_id=1, source_target_pairs={{4,0},{8,4},{12,8},{5,1},{9,5},{13,9},{6,2},{10,6},{14,10},{7,3},{... | collective-permute-start | bytes 786440 | tf_op jit(solution)/shard_map/while/body/eval_jaxpr/ppermute | solution.py:18
  56.1 10.1 %collective-permute-start.1 = (f32[4,128,128]{2,1,0:T(8,128)S(1)}, f32[4,128,128]{2,1,0:T(8,128)S(1)}, u32[]{:S(2)}, u32[]{:S(2)}) collective-permute-start(f32[4,128,128]{2,1,0:T(8,128)S(1)} %multiply_add_fusion.6), channel_id=1, source_target_pairs={{4,0},{8,4},{12,8},{5,1},{9,5},{13,9},{6,2},{10,6},{14,10},{7,3},{... | collective-permute-start | bytes 786440 | tf_op jit(solution)/shard_map/while/body/eval_jaxpr/ppermute | solution.py:18
  66.3 8.6 %collective-permute-start.1 = (f32[4,128,128]{2,1,0:T(8,128)S(1)}, f32[4,128,128]{2,1,0:T(8,128)S(1)}, u32[]{:S(2)}, u32[]{:S(2)}) collective-permute-start(f32[4,128,128]{2,1,0:T(8,128)S(1)} %multiply_add_fusion.6), channel_id=1, source_target_pairs={{4,0},{8,4},{12,8},{5,1},{9,5},{13,9},{6,2},{10,6},{14,10},{7,3},{... | collective-permute-start | bytes 786440 | tf_op jit(solution)/shard_map/while/body/eval_jaxpr/ppermute | solution.py:18
  80.2 1.4 %copy-start.11 = (f32[4,128]{1,0:T(4,128)S(1)}, f32[4,128]{1,0:T(4,128)}, u32[]{:S(2)}) copy-start(f32[4,128]{1,0:T(4,128)} %get-tuple-element.145) | copy-start | bytes 6148
  80.2 1.4 %copy-start.12 = (f32[4,128]{1,0:T(4,128)S(1)}, f32[4,128]{1,0:T(4,128)}, u32[]{:S(2)}) copy-start(f32[4,128]{1,0:T(4,128)} %get-tuple-element.146) | copy-start | bytes 6148
  81.7 0.9 copy-start
  82.6 0.8 copy-start.8
  82.6 0.8 copy-start.10
  86.3 0.7 copy-start.6
where the time goes:
time: 106 us
  waiting for transfers between devices  38 us (36%)
  blocking collectives  18.5 us (17%)
  starting transfers between devices  17.6 us (17%)
  local copies, waits for them, and re-layouts  11.5 us (11%)
  other arithmetic  9.63 us (9%)
  matrix products  7.78 us (7%)
  between operations  2.37 us (2%)
    ppermute x6, waiting for transfers between devices, from_behind(): return lax.ppermute(value, axis, pairs)  38 us
    ppermute x6, starting transfers between devices, from_behind(): return lax.ppermute(value, axis, pairs)  17.6 us
    psum x1, blocking collectives, on_device(): lax.psum((grad_bias.reshape(-1), grad_weight.reshape(-1)), ('ctx', 'rep'))  13.6 us
    unnamed x35, local copies, waits for them, and re-layouts  5.02 us
    psum x1, blocking collectives, on_device(): value_pred = lax.psum(partial_value, 'head')  4.94 us
    another operation x2, other arithmetic, block_pass(): jnp.cumsum(decay.reshape(blocks, block_len, head_count, channels), axis=1)  3.28 us
  transfers between devices with their start and end apart: 6, of which 6 were waited for; matrix products, arithmetic and copies ran while one was open for 0% of the time, Pallas kernels for 0%

commit v1 on v0

--- a/solution.py
+++ b/solution.py
@@ -16,6 +16,28 @@
     length = lax.axis_size(axis)
     pairs = [(i, i + by) for i in range(length) if 0 <= i + by < length]
     return lax.ppermute(value, axis, pairs)
+
+
+def pack_state(state, factor):
+    rows = jnp.zeros((state.shape[0], 8, state.shape[2]), state.dtype)
+    rows = rows.at[:, 0, :].set(factor)
+    return jnp.concatenate([state, rows], axis=1)
+
+
+def gather_scan(state, factor, span_count, direction):
+    if span_count == 1:
+        return jnp.zeros_like(state)
+    channels = state.shape[1]
+    packed = pack_state(state, factor)
+    received = []
+    for shift in range(1, span_count):
+        payload = packed if shift < span_count - 1 else state
+        received.append(from_behind(payload, "ctx", direction * shift))
+    total = received[-1][:, :channels]
+    for shift in range(span_count - 2, 0, -1):
+        part = received[shift - 1]
+        total = total * part[:, channels, :][..., None] + part[:, :channels]
+    return total
 
 
 def block_pass(query_in, key_in, value_in, decay, start_flags, kind_ids):
@@ -108,10 +130,8 @@
     )
     attended_local, state_local, decay_local, carried = local_out
 
-    def pass_state(position, incoming):
-        return from_behind(incoming * decay_local[..., None] + state_local, "ctx", 1)
-
-    state_in = lax.fori_loop(0, lax.axis_size("ctx") - 1, pass_state, jnp.zeros_like(state_local))
+    span_count = lax.axis_size("ctx")
+    state_in = gather_scan(state_local, decay_local, span_count, 1)
     attended = attended_local + jnp.einsum("thc,hcd->thd", carried, state_in, precision=highest)
 
     def value_head(attended_in, weight_in):
@@ -127,10 +147,7 @@
     grad_carried = jnp.einsum("thd,hcd->thc", grad_attended, state_in, precision=highest)
     grad_direct = jnp.einsum("thc,thd->hcd", carried, grad_attended, precision=highest)
 
-    def pass_grad(position, incoming):
-        return from_behind(grad_direct + decay_local[..., None] * incoming, "ctx", -1)
-
-    grad_state = lax.fori_loop(0, lax.axis_size("ctx") - 1, pass_grad, jnp.zeros_like(grad_direct))
+    grad_state = gather_scan(grad_direct, decay_local, span_count, -1)
     grad_decay = jnp.sum(state_in * grad_state, axis=-1)
     grad_query, grad_key, grad_value, grad_logit, grad_bias = pull_local(
         (grad_attended, grad_state, grad_decay, grad_carried)

time: 106 us -> 102 us (0.962)
  waiting for transfers between devices: 38 us -> 27.1 us
  local copies, waits for them, and re-layouts: 11.5 us -> 15.7 us
  matrix products: 7.78 us -> 10.4 us
  other arithmetic: 9.63 us -> 11.7 us
  starting transfers between devices: 17.6 us -> 15.6 us
    ppermute x6, waiting for transfers between devices: 38 us -> 27.1 us  [from_behind(): return lax.ppermute(value, axis, pairs)]
    slice x0 -> x4, local copies, waits for them, and re-layouts: none -> 2.88 us  [gather_scan(): total = total * part[:, channels, :][..., None] + part[:, :channels]]
    unnamed x35 -> x53, local copies, waits for them, and re-layouts: 5.02 us -> 7.74 us
    ppermute x6, starting transfers between devices: 17.6 us -> 15.6 us  [from_behind(): return lax.ppermute(value, axis, pairs)]
    concatenate x0 -> x2, other arithmetic: none -> 1.71 us  [pack_state(): return jnp.concatenate([state, rows], axis=1)]
  transfers between devices with their start and end apart: 6 -> 6, of which waited for: 6 -> 4; matrix products, arithmetic and copies ran while one was open for 0% -> 11% of each run, Pallas kernels for 0% -> 0%
where the time goes in v1:
time: 102 us
  waiting for transfers between devices  27.1 us (27%)
  blocking collectives  18.5 us (18%)
  local copies, waits for them, and re-layouts  15.7 us (15%)
  starting transfers between devices  15.6 us (15%)
  other arithmetic  11.7 us (11%)
  matrix products  10.4 us (10%)
  between operations  2.46 us (2%)
    ppermute x6, waiting for transfers between devices, from_behind(): return lax.ppermute(value, axis, pairs)  27.1 us
    ppermute x6, starting transfers between devices, from_behind(): return lax.ppermute(value, axis, pairs)  15.6 us
    psum x1, blocking collectives, on_device(): lax.psum((grad_bias.reshape(-1), grad_weight.reshape(-1)), ('ctx', 'rep'))  13.6 us
    unnamed x53, local copies, waits for them, and re-layouts  7.74 us
    psum x1, blocking collectives, on_device(): value_pred = lax.psum(partial_value, 'head')  4.94 us
    slice x4, local copies, waits for them, and re-layouts, gather_scan(): total = total * part[:, channels, :][..., None] + part[:, :channels]  2.88 us
    another operation x2, other arithmetic, block_pass(): jnp.cumsum(decay.reshape(blocks, block_len, head_count, channels), axis=1)  2.36 us
  transfers between devices with their start and end apart: 6, of which 4 were waited for; matrix products, arithmetic and copies ran while one was open for 11% of the time, Pallas kernels for 0%

profile of v1, /device:TPU:0, one launch (start us, length us, event | category | flops | bytes accessed | tf_op | source)
XLA Modules:
  0.0 101.6 jit_solution(3680128129844914448)
XLA Ops:
  0.6 1.0 reshape.552
  2.0 0.6 slice.65
  3.7 0.6 slice.66
  4.5 0.8 copy-done.6
  5.3 1.2 %compare_convert_fusion.1 = (f32[128]{0:T(128)}, f32[128]{0:T(128)S(1)}) fusion(s32[1,128]{1,0:T(1,128)S(1)} %reduce_window_sum.35, s32[]{:T(128)} %bitcast.14), kind=kLoop, calls=%fused_computation.139 | loop fusion | flops 512 | bytes 1540 | tf_op jit(solution)/shard_map/jvp()/convert_element_type | solution.py:56
  6.5 0.5 copy-done.15
  7.6 5.8 %collective-permute-start.2 = (f32[4,136,128]{2,1,0:T(8,128)S(1)}, f32[4,136,128]{2,1,0:T(8,128)}, u32[]{:S(2)}, u32[]{:S(2)}) collective-permute-start(f32[4,136,128]{2,1,0:T(8,128)S(1)} %fusion.6), channel_id=1, source_target_pairs={{0,4},{4,8},{8,12},{1,5},{5,9},{9,13},{2,6},{6,10},{10,14},{3,7},{... | collective-permute-start | bytes 835592 | tf_op jit(solution)/shard_map/ppermute | solution.py:18
  13.3 4.5 %collective-permute-start.1 = (f32[4,136,128]{2,1,0:T(8,128)S(1)}, f32[4,136,128]{2,1,0:T(8,128)}, u32[]{:S(2)}, u32[]{:S(2)}) collective-permute-start(f32[4,136,128]{2,1,0:T(8,128)S(1)} %fusion.6), channel_id=1, source_target_pairs={{0,8},{4,12},{1,9},{5,13},{2,10},{6,14},{3,11},{7,15},{16,24},{20,... | collective-permute-start | bytes 835592 | tf_op jit(solution)/shard_map/ppermute | solution.py:18
  17.8 1.3 %collective-permute-start = (f32[4,128,128]{2,1,0:T(8,128)S(1)}, f32[4,128,128]{2,1,0:T(8,128)S(1)}, u32[]{:S(2)}, u32[]{:S(2)}) collective-permute-start(f32[4,128,128]{2,1,0:T(8,128)S(1)} %convolution_add_fusion), channel_id=1, source_target_pairs={{0,12},{1,13},{2,14},{3,15},{16,28},{17,29},{18,30},{19,31}} | collective-permute-start | bytes 786440 | tf_op jit(solution)/shard_map/ppermute | solution.py:18
  20.3 0.6 copy-done.3
  20.9 0.7 fusion.2
  21.8 0.5 compare_select_fusion.7
  23.3 0.7 fusion.1
  24.1 0.7 slice.78
  24.8 0.9 collective-permute-done.1
  25.7 0.7 slice.76
  26.4 3.8 %collective-permute-done = f32[4,128,128]{2,1,0:T(8,128)S(1)} collective-permute-done((f32[4,128,128]{2,1,0:T(8,128)S(1)}, f32[4,128,128]{2,1,0:T(8,128)S(1)}, u32[]{:S(2)}, u32[]{:S(2)}) %collective-permute-start) | collective-permute-done | bytes 262176 | tf_op jit(solution)/shard_map/ppermute | solution.py:18
  30.2 1.2 %slice_add_fusion.2 = f32[4,128,128]{2,1,0:T(8,128)S(1)} fusion(f32[4,136,128]{2,1,0:T(8,128)} %collective-permute-done.2, f32[4,136,128]{2,1,0:T(8,128)} %collective-permute-done.1, f32[4,128,128]{2,1,0:T(8,128)S(1)} %collective-permute-done, f32[4,128]{1,0:T(4,128)S(1)} %bitcast.200, f32[4,128]{1,0:T(4,128)S(1)} %bitcast.202), kind=kLoop, calls=%fused_computation.44 | loop fusion | flops 262144 | bytes 1052672 | tf_op jit(solution)/shard_map/add | solution.py:39
  31.4 0.7 multiply_reduce_fusion.2
  32.1 0.6 copy-done.8
  33.0 4.9 %psum.21 = f32[128]{0:T(128)S(1)} all-reduce(f32[128]{0:T(128)S(1)} %convolution_bitcast_fusion.2), channel_id=1, replica_groups=mesh['groups'=2,'ctx'=4,'head'=2,'rep'=2] {'head'}, use_global_device_ids=true, to_apply=%region_3.4 | all-reduce | flops 128 | bytes 1024 | tf_op jit(solution)/shard_map/psum | solution.py:144
  38.6 1.4 %fusion.64 = f32[4,128,128]{2,1,0:T(8,128)} fusion(f32[128,4,128]{2,0,1:T(8,128)S(1)} %fusion.39, f32[128]{0:T(128)S(1)} %copy-done.20, f32[128,4,128]{0,2,1:T(8,128)S(1)} %get-tuple-element.121, f32[128,4]{0,1:T(4,128)S(1)} %multiply_multiply_fusion.2, f32[4,128]{1,0:T(4,128)S(1)} %bitcast.189, f32[128]{0:T(128)S(1)} %bitcast_subtract_fusion.1, ...), kind=kOutput, calls=%fused_computation.102 | convolution fusion | flops 101056512 | bytes 793600 | tf_op jit(solution)/shard_map/thc,thd->hcd/dot_general | solution.py:148
  40.0 1.7 %fusion.7 = f32[4,136,128]{2,1,0:T(8,128)} fusion(f32[4,1,128]{2,1,0:T(1,128)S(1)} %bitcast.197, f32[4,128,128]{2,1,0:T(8,128)} %fusion.64), kind=kLoop, calls=%fused_computation.28 | loop fusion | flops 208896 | bytes 542720 | tf_op jit(solution)/shard_map/concatenate | solution.py:24
  41.7 1.3 %collective-permute-start.5 = (f32[4,136,128]{2,1,0:T(8,128)}, f32[4,136,128]{2,1,0:T(8,128)}, u32[]{:S(2)}, u32[]{:S(2)}) collective-permute-start(f32[4,136,128]{2,1,0:T(8,128)} %fusion.7), channel_id=1, source_target_pairs={{4,0},{8,4},{12,8},{5,1},{9,5},{13,9},{6,2},{10,6},{14,10},{7,3},{... | collective-permute-start | bytes 835592 | tf_op jit(solution)/shard_map/ppermute | solution.py:18
  43.0 1.3 %collective-permute-start.4 = (f32[4,136,128]{2,1,0:T(8,128)}, f32[4,136,128]{2,1,0:T(8,128)}, u32[]{:S(2)}, u32[]{:S(2)}) collective-permute-start(f32[4,136,128]{2,1,0:T(8,128)} %fusion.7), channel_id=1, source_target_pairs={{8,0},{12,4},{9,1},{13,5},{10,2},{14,6},{11,3},{15,7},{24,16},{28,... | collective-permute-start | bytes 835592 | tf_op jit(solution)/shard_map/ppermute | solution.py:18
  44.3 1.5 %collective-permute-start.3 = (f32[4,128,128]{2,1,0:T(8,128)}, f32[4,128,128]{2,1,0:T(8,128)}, u32[]{:S(2)}, u32[]{:S(2)}) collective-permute-start(f32[4,128,128]{2,1,0:T(8,128)} %fusion.64), channel_id=1, source_target_pairs={{12,0},{13,1},{14,2},{15,3},{28,16},{29,17},{30,18},{31,19}} | collective-permute-start | bytes 786440 | tf_op jit(solution)/shard_map/ppermute | solution.py:18
  46.1 0.6 fusion.60
  46.7 0.6 fusion.83
  47.9 1.2 %fusion.105 = f32[4,128,128]{2,1,0:T(8,128)} fusion(f32[4,128,128]{2,1,0:T(8,128)S(1)} %slice_add_fusion.2, f32[128,4,128]{0,2,1:T(8,128)S(1)} %get-tuple-element.121, f32[128,4]{0,1:T(4,128)S(1)} %multiply_multiply_fusion.2, f32[4,128]{1,0:T(4,128)S(1)} %bitcast.192, f32[128]{0:T(128)S(1)} %bitcast_subtract_fusion.1, f32[128,4]{0,1:T(4,128)S(1)} %fusion.91), kind=kOutput, calls=%fused_computation.155 | convolution fusion | flops 100990976 | bytes 793088 | tf_op jit(solution)/shard_map/thd,hcd->thc/dot_general | solution.py:147
  49.0 0.9 fusion.92
  50.4 0.8 copy-done.1
  51.4 0.9 convolution_convert_fusion.1
  52.3 5.7 %collective-permute-done.5 = f32[4,136,128]{2,1,0:T(8,128)} collective-permute-done((f32[4,136,128]{2,1,0:T(8,128)}, f32[4,136,128]{2,1,0:T(8,128)}, u32[]{:S(2)}, u32[]{:S(2)}) %collective-permute-start.5) | collective-permute-done | bytes 278560 | tf_op jit(solution)/shard_map/ppermute | solution.py:18
  57.9 0.7 slice.82
  58.7 16.9 %collective-permute-done.4 = f32[4,136,128]{2,1,0:T(8,128)} collective-permute-done((f32[4,136,128]{2,1,0:T(8,128)}, f32[4,136,128]{2,1,0:T(8,128)}, u32[]{:S(2)}, u32[]{:S(2)}) %collective-permute-start.4) | collective-permute-done | bytes 278560 | tf_op jit(solution)/shard_map/ppermute | solution.py:18
  75.5 0.7 slice.80
  76.2 1.5 %multiply_reduce_fusion = (f32[4,128]{1,0:T(4,128)S(1)}, f32[4,128]{1,0:T(4,128)S(1)}, f32[4,128,128]{2,1,0:T(8,128)S(1)}) fusion(f32[4,128,128]{2,1,0:T(8,128)S(1)} %slice_add_fusion.2, f32[4,136,128]{2,1,0:T(8,128)} %collective-permute-done.5, f32[4,128]{1,0:T(4,128)S(1)} %bitcast.199, f32[4,136,128]{2,1,0:T(8,128)} %collective-permute-done.4, ...), kind=kLoop, calls=%fused_computation.80 | loop fusion | flops 523264 | bytes 1318912 | tf_op jit(solution)/shard_map/transpose(jvp())/while/body/eval_jaxpr/reduce_sum | solution.py:79
  79.0 1.0 fusion.103
  80.0 0.7 convert_element_type.156
  80.7 0.7 convert_element_type.158
  81.6 0.6 fusion.5
  82.2 0.8 copy.89
  83.0 0.7 copy-done.18
  83.7 2.0 %fusion.59 = (f32[4,128]{1,0:T(4,128)S(1)}, f32[1,128,4,128]{3,2,1,0:T(4,128)S(1)}) fusion(f32[128,4,128]{2,1,0:T(4,128)S(1)} %reshape.557, f32[4,128]{1,0:T(4,128)S(1)} %bitcast.195, f32[1,128,4,128]{3,2,1,0:T(4,128)S(1)} %copy.101, f32[4,128,128]{2,0,1:T(4,128)S(1)} %copy.85, f32[1,1,4,128]{3,2,1,0:T(4,128)S(1)} %bitcast_add_fusion.2, ...), kind=kOutput, calls=%fused_computation.97 | output fusion | flops 10354176 | bytes 2105856 | tf_op jit(solution)/shard_map/transpose(jvp(jit(cumsum)))/reduce_window_sum | solution.py:53
  85.8 0.9 fusion.17
  86.7 0.7 copy-done.17
  87.4 13.6 %all-reduce.2 = (f32[512]{0:T(512)S(1)}, f32[512]{0:T(512)S(1)}) all-reduce(f32[512]{0:T(512)S(1)} %negate_bitcast_fusion, f32[512]{0:T(512)S(1)} %bitcast.198), channel_id=1, replica_groups=mesh['groups'=2,'ctx'=4,'head'=2,'rep'=2] {'ctx','rep'}, use_global_device_ids=true, to_apply=%region_10.11 | all-reduce | flops 1024 | bytes 8192 | tf_op jit(solution)/shard_map/psum | solution.py:156
  101.0 0.6 broadcast_multiply_fusion.1
  (82 shorter events, 7.1 us)
Async XLA Ops:
  0.6 1.0 copy-start.22
  2.6 0.7 copy-start.11
  3.2 1.0 copy-start.5
  3.6 2.9 %copy-start.9 = (f32[4,128]{1,0:T(4,128)}, f32[4,128]{1,0:T(4,128)S(1)}, u32[]{:S(2)}) copy-start(f32[4,128]{1,0:T(4,128)S(1)} %get-tuple-element.116) | copy-start | bytes 6148
  3.6 3.9 %copy-start.13 = (f32[1,1,4,128]{3,2,1,0:T(4,128)}, f32[1,1,4,128]{3,2,1,0:T(4,128)S(1)}, u32[]{:S(2)}) copy-start(f32[1,1,4,128]{3,2,1,0:T(4,128)S(1)} %get-tuple-element.117) | copy-start | bytes 6148
  4.4 0.9 copy-start.6
  6.5 0.5 copy-start.15
  7.5 12.3 %copy-start.7 = (bf16[1,128,512]{2,1,0:T(8,128)(2,1)S(1)}, bf16[1,128,512]{2,1,0:T(8,128)(2,1)}, u32[]{:S(2)}) copy-start(bf16[1,128,512]{2,1,0:T(8,128)(2,1)} %param.13) | copy-start | bytes 393220
  7.6 16.5 %collective-permute-start.2 = (f32[4,136,128]{2,1,0:T(8,128)S(1)}, f32[4,136,128]{2,1,0:T(8,128)}, u32[]{:S(2)}, u32[]{:S(2)}) collective-permute-start(f32[4,136,128]{2,1,0:T(8,128)S(1)} %fusion.6), channel_id=1, source_target_pairs={{0,4},{4,8},{8,12},{1,5},{5,9},{9,13},{2,6},{6,10},{10,14},{3,7},{... | collective-permute-start | bytes 835592 | tf_op jit(solution)/shard_map/ppermute | solution.py:18
  13.3 12.4 %collective-permute-start.1 = (f32[4,136,128]{2,1,0:T(8,128)S(1)}, f32[4,136,128]{2,1,0:T(8,128)}, u32[]{:S(2)}, u32[]{:S(2)}) collective-permute-start(f32[4,136,128]{2,1,0:T(8,128)S(1)} %fusion.6), channel_id=1, source_target_pairs={{0,8},{4,12},{1,9},{5,13},{2,10},{6,14},{3,11},{7,15},{16,24},{20,... | collective-permute-start | bytes 835592 | tf_op jit(solution)/shard_map/ppermute | solution.py:18
  17.8 12.3 %collective-permute-start = (f32[4,128,128]{2,1,0:T(8,128)S(1)}, f32[4,128,128]{2,1,0:T(8,128)S(1)}, u32[]{:S(2)}, u32[]{:S(2)}) collective-permute-start(f32[4,128,128]{2,1,0:T(8,128)S(1)} %convolution_add_fusion), channel_id=1, source_target_pairs={{0,12},{1,13},{2,14},{3,15},{16,28},{17,29},{18,30},{19,31}} | collective-permute-start | bytes 786440 | tf_op jit(solution)/shard_map/ppermute | solution.py:18
  20.3 0.6 copy-start.3
  21.5 0.9 copy-start
  22.7 0.7 copy-start.19
  30.2 1.3 %copy-start.20 = (f32[128]{0:T(128)S(1)}, f32[128]{0:T(128)}, u32[]{:S(2)}) copy-start(f32[128]{0:T(128)} %compare_select_fusion.7) | copy-start | bytes 1540
  32.1 0.7 copy-start.8
  33.0 5.0 %copy-start.23 = (f32[1,128]{1,0:T(1,128)S(1)}, f32[1,128]{1,0:T(1,128)}, u32[]{:S(2)}) copy-start(f32[1,128]{1,0:T(1,128)} %param.19) | copy-start | bytes 1540
  38.0 0.5 copy-start.24
  38.6 1.4 %copy-start.14 = (f32[1,1,4,128]{3,2,1,0:T(4,128)S(1)}, f32[1,1,4,128]{3,2,1,0:T(4,128)}, u32[]{:S(2)}) copy-start(f32[1,1,4,128]{3,2,1,0:T(4,128)} %copy-done.13) | copy-start | bytes 6148
  40.0 5.8 %copy-start.4 = (pred[128,128]{1,0:T(8,128)(4,1)S(1)}, pred[128,128]{1,0:T(8,128)(4,1)}, u32[]{:S(2)}) copy-start(pred[128,128]{1,0:T(8,128)(4,1)} %copy-done.3) | copy-start | bytes 49156
  41.7 16.2 %collective-permute-start.5 = (f32[4,136,128]{2,1,0:T(8,128)}, f32[4,136,128]{2,1,0:T(8,128)}, u32[]{:S(2)}, u32[]{:S(2)}) collective-permute-start(f32[4,136,128]{2,1,0:T(8,128)} %fusion.7), channel_id=1, source_target_pairs={{4,0},{8,4},{12,8},{5,1},{9,5},{13,9},{6,2},{10,6},{14,10},{7,3},{... | collective-permute-start | bytes 835592 | tf_op jit(solution)/shard_map/ppermute | solution.py:18
  43.0 32.5 %collective-permute-start.4 = (f32[4,136,128]{2,1,0:T(8,128)}, f32[4,136,128]{2,1,0:T(8,128)}, u32[]{:S(2)}, u32[]{:S(2)}) collective-permute-start(f32[4,136,128]{2,1,0:T(8,128)} %fusion.7), channel_id=1, source_target_pairs={{8,0},{12,4},{9,1},{13,5},{10,2},{14,6},{11,3},{15,7},{24,16},{28,... | collective-permute-start | bytes 835592 | tf_op jit(solution)/shard_map/ppermute | solution.py:18
  44.3 31.9 %collective-permute-start.3 = (f32[4,128,128]{2,1,0:T(8,128)}, f32[4,128,128]{2,1,0:T(8,128)}, u32[]{:S(2)}, u32[]{:S(2)}) collective-permute-start(f32[4,128,128]{2,1,0:T(8,128)} %fusion.64), channel_id=1, source_target_pairs={{12,0},{13,1},{14,2},{15,3},{28,16},{29,17},{30,18},{31,19}} | collective-permute-start | bytes 786440 | tf_op jit(solution)/shard_map/ppermute | solution.py:18
  50.2 1.0 copy-start.1
  78.1 0.7 copy-start.10
  78.3 0.7 copy-start.16
  78.3 0.7 copy-start.21
  80.7 0.9 copy-start.2
  82.2 1.5 %copy-start.12 = (f32[512]{0:T(512)S(1)}, f32[512]{0:T(512)}, u32[]{:S(2)}) copy-start(f32[512]{0:T(512)} %param.17) | copy-start | bytes 6148
  83.0 0.7 copy-start.18
  86.7 0.7 copy-start.17

commit v2 on v1

v2 whole, which is shorter than its diff:
```python
import jax
import jax.numpy as jnp
from jax import lax
from jax.sharding import PartitionSpec as P

DK = 128
DV = 128


epsilon = 1.0
gate_scale = 16.0
highest = lax.Precision.HIGHEST


def from_behind(value, axis, by):
    length = lax.axis_size(axis)
    pairs = [(i, i + by) for i in range(length) if 0 <= i + by < length]
    return lax.ppermute(value, axis, pairs)


def pack_state(state, factor):
    rows = jnp.zeros((state.shape[0], 8, state.shape[2]), state.dtype)
    rows = rows.at[:, 0, :].set(factor)
    return jnp.concatenate([state, rows], axis=1)


def gather_scan(state, factor, span_count, direction):
    if span_count == 1:
        return jnp.zeros_like(state)
    channels = state.shape[1]
    packed = pack_state(state, factor)
    received = []
    for shift in range(1, span_count):
        payload = packed if shift < span_count - 1 else state
        received.append(from_behind(payload, "ctx", direction * shift))
    total = received[-1][:, :channels]
    for shift in range(span_count - 2, 0, -1):
        part = received[shift - 1]
        total = total * part[:, channels, :][..., None] + part[:, :channels]
    return total


def log_decay(logit_in, bias_in):
    return jax.nn.log_sigmoid(logit_in + bias_in) / gate_scale


def segment_ids(start_flags):
    return jnp.cumsum(start_flags, axis=0, dtype=jnp.int32)


def block_inner(query_in, key_in, value_in, logit_in, bias_in, start_flags, kind_id):
    block_len = query_in.shape[0]
    channels = query_in.shape[2]
    log_cum = jnp.cumsum(log_decay(logit_in, bias_in), axis=0)
    segment = segment_ids(start_flags)
    alive_mask = (segment == 0).astype(jnp.float32)
    offsets = jnp.arange(block_len, dtype=jnp.int32)
    distance = offsets[:, None] - offsets[None, :]
    window = block_len // jnp.left_shift(jnp.ones_like(kind_id), kind_id)
    live_pairs = (
        (segment[:, None] == segment[None, :]) & (distance >= 0) & (distance < window)
    )
    query_dec = query_in * jnp.exp(log_cum) * channels ** (-0.5)
    key_dec = key_in * jnp.exp(-log_cum)
    scores = jnp.einsum("ihc,jhc->hij", query_dec, key_dec, precision=highest)
    block_probs = jnp.where(live_pairs[None], scores, 0.0).astype(jnp.bfloat16)
    inner_part = jnp.einsum(
        "hij,jhd->ihd",
        block_probs,
        value_in.astype(jnp.bfloat16),
        preferred_element_type=jnp.float32,
    )
    carried = query_dec * alive_mask[:, None, None]
    return inner_part, carried


def block_summary(key_in, value_in, logit_in, bias_in, start_flags):
    log_cum = jnp.cumsum(log_decay(logit_in, bias_in), axis=0)
    log_last = log_cum[-1]
    segment = segment_ids(start_flags)
    alive_last = (segment[-1] == 0).astype(jnp.float32)
    tail_mask = (segment == segment[-1]).astype(jnp.float32)
    key_tail = key_in * jnp.exp(log_last[None] - log_cum) * tail_mask[:, None, None]
    block_state = jnp.einsum("jhc,jhd->hcd", key_tail, value_in, precision=highest)
    block_decay = jnp.exp(log_last) * alive_last
    return block_state, block_decay


def on_device(
    queries,
    per_head_keys,
    value_rows,
    gate_logits,
    gate_bias,
    value_weight,
    targets,
    mask_ids,
    segment_starts,
):
    token_count = queries.shape[1]
    head_count = gate_bias.shape[0] // DK
    assert mask_ids.shape[1] == 1

    def to_heads(array):
        return array[0].reshape(token_count, head_count, -1).astype(jnp.float32)

    start_flags = segment_starts[0]
    kind_id = mask_ids[0, 0]
    query_f = to_heads(queries)
    key_f = to_heads(per_head_keys)
    value_f = to_heads(value_rows)
    logit_f = to_heads(gate_logits)
    bias_h = gate_bias.reshape(head_count, DK)

    def inner_terms(query_in, key_in, value_in, logit_in, bias_in):
        return block_inner(query_in, key_in, value_in, logit_in, bias_in, start_flags, kind_id)

    def summary_terms(key_in, value_in, logit_in, bias_in):
        return block_summary(key_in, value_in, logit_in, bias_in, start_flags)

    (attended_local, carried), pull_inner = jax.vjp(
        inner_terms, query_f, key_f, value_f, logit_f, bias_h
    )
    (state_local, decay_local), pull_summary = jax.vjp(
        summary_terms, key_f, value_f, logit_f, bias_h
    )

    span_count = lax.axis_size("ctx")
    state_in = gather_scan(state_local, decay_local, span_count, 1)
    attended = attended_local + jnp.einsum("thc,hcd->thd", carried, state_in, precision=highest)

    def value_head(attended_in, weight_in):
        normed = attended_in * lax.rsqrt(
            jnp.mean(attended_in * attended_in, axis=-1, keepdims=True) + epsilon
        )
        return jnp.einsum("thd,hd->t", normed, weight_in, precision=highest)

    partial_value, pull_value = jax.vjp(value_head, attended, value_weight.reshape(head_count, DV))
    value_pred = lax.psum(partial_value, "head")
    residual = value_pred - targets[0]
    grad_attended, grad_weight = pull_value(residual)
    grad_carried = jnp.einsum("thd,hcd->thc", grad_attended, state_in, precision=highest)
    grad_direct = jnp.einsum("thc,thd->hcd", carried, grad_attended, precision=highest)
    inner_grads = pull_inner((grad_attended, grad_carried))

    grad_state = gather_scan(grad_direct, decay_local, span_count, -1)
    grad_decay = jnp.sum(state_in * grad_state, axis=-1)
    summary_grads = pull_summary((grad_state, grad_decay))

    grad_query = inner_grads[0]
    grad_key = inner_grads[1] + summary_grads[0]
    grad_value = inner_grads[2] + summary_grads[1]
    grad_logit = inner_grads[3] + summary_grads[2]
    grad_bias = inner_grads[4] + summary_grads[3]
    token_total = token_count * lax.axis_size("ctx") * lax.axis_size("rep")
    bias_total, weight_total = lax.psum(
        (grad_bias.reshape(-1), grad_weight.reshape(-1)), ("ctx", "rep")
    )

    def to_rows(array):
        return array.reshape(1, token_count, -1).astype(jnp.bfloat16)

    return (
        value_pred[None],
        to_rows(grad_query),
        to_rows(grad_key),
        to_rows(grad_value),
        to_rows(grad_logit),
        bias_total / token_total,
        weight_total / token_total,
    )


def solution(mesh):
    in_specs = (
        P(("groups", "rep"), "ctx", "head"),
        P(("groups", "rep"), "ctx", "head"),
        P(("groups", "rep"), "ctx", "head"),
        P(("groups", "rep"), "ctx", "head"),
        P("head"),
        P("head"),
        P(("groups", "rep"), "ctx"),
        P(("groups", "rep"), "ctx"),
        P(("groups", "rep"), "ctx"),
    )
    out_specs = (
        P(("groups", "rep"), "ctx"),
        P(("groups", "rep"), "ctx", "head"),
        P(("groups", "rep"), "ctx", "head"),
        P(("groups", "rep"), "ctx", "head"),
        P(("groups", "rep"), "ctx", "head"),
        P(("groups", "head")),
        P(("groups", "head")),
    )
    return jax.shard_map(
        on_device, mesh=mesh, in_specs=in_specs, out_specs=out_specs, check_vma=False
    )
```

time: 102 us -> 98.5 us (0.966)
  waiting for transfers between devices: 27.1 us -> 38.6 us
  local copies, waits for them, and re-layouts: 15.7 us -> 9.45 us
  other arithmetic: 11.7 us -> 7.19 us
  matrix products: 10.4 us -> 6.49 us
    ppermute x6, waiting for transfers between devices: 27.1 us -> 38.6 us  [from_behind(): return lax.ppermute(value, axis, pairs)]
    slice x4, local copies, waits for them, and re-layouts: 2.88 us -> 0.73 us  [gather_scan(): total = total * part[:, channels, :][..., None] + part[:, :channels]]
    convert_element_type x8 -> x4, local copies, waits for them, and re-layouts: 3.05 us -> 0.99 us  [the longest x1 0.71 us: to_rows(): return array.reshape(1, token_count, -1).astype(jnp.bfloat16)]
    dot_general x11 -> x9, matrix products: 6.06 us -> 4.1 us  [the longest x3 1.65 us: block_inner(): scores = jnp.einsum('ihc,jhc->hij', query_dec, key_dec, precision=highest)]
    concatenate x2, other arithmetic: 1.71 us -> 0.04 us  [pack_state(): return jnp.concatenate([state, rows], axis=1)]
    reduce_sum x2, other arithmetic: 2.49 us -> 0.89 us  [the longest x1 0.58 us: log_decay(): return jax.nn.log_sigmoid(logit_in + bias_in) / gate_scale]
    unnamed x53 -> x21, local copies, waits for them, and re-layouts: 7.74 us -> 6.35 us
    convert_element_type x4 -> x2, other arithmetic: 2.11 us -> 0.8 us  [the longest x1 0.65 us: block_inner(): alive_mask = (segment == 0).astype(jnp.float32)]
  transfers between devices with their start and end apart: 6 -> 6, of which waited for: 4 -> 4; matrix products, arithmetic and copies ran while one was open for 11% -> 3% of each run, Pallas kernels for 0% -> 0%
where the time goes in v2:
time: 98.5 us; the launch traced here: 98.1 us
  waiting for transfers between devices  38.6 us (39%)
  blocking collectives  18.5 us (19%)
  starting transfers between devices  15.4 us (16%)
  local copies, waits for them, and re-layouts  9.45 us (10%)
  other arithmetic  7.19 us (7%)
  matrix products  6.49 us (7%)
  between operations  2.34 us (2%)
    ppermute x6, waiting for transfers between devices, from_behind(): return lax.ppermute(value, axis, pairs)  38.6 us
    ppermute x6, starting transfers between devices, from_behind(): return lax.ppermute(value, axis, pairs)  15.4 us
    psum x1, blocking collectives, on_device(): lax.psum((grad_bias.reshape(-1), grad_weight.reshape(-1)), ('ctx', 'rep'))  13.6 us
    unnamed x21, local copies, waits for them, and re-layouts  6.35 us
    psum x1, blocking collectives, on_device(): value_pred = lax.psum(partial_value, 'head')  4.94 us
  transfers between devices with their start and end apart: 6, of which 4 were waited for; matrix products, arithmetic and copies ran while one was open for 3% of the time, Pallas kernels for 0%

profile of v2, /device:TPU:0, one launch (start us, length us, event | category | flops | bytes accessed | tf_op | source)
XLA Modules:
  0.0 98.1 jit_solution(8179220389299033713)
XLA Ops:
  0.6 0.6 copy-done.6
  1.4 0.2 broadcast_in_dim.35
  1.6 0.5 slice.73
  2.9 0.6 compare_convert_fusion.1
  3.6 0.9 copy-done
  4.5 0.6 copy-done.5
  5.1 0.3 fusion.18
  5.6 0.8 copy-done.1
  6.5 0.3 slice_reduce_fusion
  6.8 0.4 fusion.45
  7.2 7.0 %collective-permute-start = (f32[4,128,128]{2,1,0:T(8,128)S(1)}, f32[4,128,128]{2,1,0:T(8,128)S(1)}, u32[]{:S(2)}, u32[]{:S(2)}) collective-permute-start(f32[4,128,128]{2,1,0:T(8,128)S(1)} %fusion.45), channel_id=1, source_target_pairs={{0,12},{1,13},{2,14},{3,15},{16,28},{17,29},{18,30},{19,31}} | collective-permute-start | bytes 786440 | tf_op jit(solution)/shard_map/ppermute | solution.py:18
  14.2 1.4 %collective-permute-start.2 = (f32[4,136,128]{2,1,0:T(8,128)S(1)}, f32[4,136,128]{2,1,0:T(8,128)S(1)}, u32[]{:S(2)}, u32[]{:S(2)}) collective-permute-start(f32[4,136,128]{2,1,0:T(8,128)S(1)} %fusion.9), channel_id=1, source_target_pairs={{0,4},{4,8},{8,12},{1,5},{5,9},{9,13},{2,6},{6,10},{10,14},{3,7},{... | collective-permute-start | bytes 835592 | tf_op jit(solution)/shard_map/ppermute | solution.py:18
  15.6 3.2 %collective-permute-start.1 = (f32[4,136,128]{2,1,0:T(8,128)S(1)}, f32[4,136,128]{2,1,0:T(8,128)}, u32[]{:S(2)}, u32[]{:S(2)}) collective-permute-start(f32[4,136,128]{2,1,0:T(8,128)S(1)} %fusion.9), channel_id=1, source_target_pairs={{0,8},{4,12},{1,9},{5,13},{2,10},{6,14},{3,11},{7,15},{16,24},{20,... | collective-permute-start | bytes 835592 | tf_op jit(solution)/shard_map/ppermute | solution.py:18
  19.7 0.6 fusion.4
  20.3 0.2 fusion.41
  20.6 6.2 %collective-permute-done.2 = f32[4,136,128]{2,1,0:T(8,128)S(1)} collective-permute-done((f32[4,136,128]{2,1,0:T(8,128)S(1)}, f32[4,136,128]{2,1,0:T(8,128)S(1)}, u32[]{:S(2)}, u32[]{:S(2)}) %collective-permute-start.2) | collective-permute-done | bytes 278560 | tf_op jit(solution)/shard_map/ppermute | solution.py:18
  26.8 4.9 %collective-permute-done.1 = f32[4,136,128]{2,1,0:T(8,128)} collective-permute-done((f32[4,136,128]{2,1,0:T(8,128)S(1)}, f32[4,136,128]{2,1,0:T(8,128)}, u32[]{:S(2)}, u32[]{:S(2)}) %collective-permute-start.1) | collective-permute-done | bytes 278560 | tf_op jit(solution)/shard_map/ppermute | solution.py:18
  31.7 0.7 slice.74
  32.4 1.1 %slice_add_fusion.2 = f32[4,128,128]{2,1,0:T(8,128)S(1)} fusion(f32[4,136,128]{2,1,0:T(8,128)S(1)} %collective-permute-done.2, f32[4,136,128]{2,1,0:T(8,128)} %collective-permute-done.1, f32[4,128,128]{2,1,0:T(8,128)S(1)} %collective-permute-done, f32[4,128]{1,0:T(4,128)S(1)} %bitcast.120, f32[4,128]{1,0:T(4,128)S(1)} %bitcast.122), kind=kLoop, calls=%fused_computation.37 | loop fusion | flops 262144 | bytes 1052672 | tf_op jit(solution)/shard_map/add | solution.py:39
  33.6 0.6 multiply_reduce_fusion.1
  34.2 0.6 copy-done.4
  34.9 0.2 convolution_bitcast_fusion.2
  35.1 4.9 %psum.21 = f32[128]{0:T(128)S(1)} all-reduce(f32[128]{0:T(128)S(1)} %convolution_bitcast_fusion.2), channel_id=1, replica_groups=mesh['groups'=2,'ctx'=4,'head'=2,'rep'=2] {'head'}, use_global_device_ids=true, to_apply=%region_3.5 | all-reduce | flops 128 | bytes 1024 | tf_op jit(solution)/shard_map/psum | solution.py:139
  40.1 0.5 copy-done.8
  40.8 0.3 fusion.6
  41.0 0.3 fusion.8
  41.4 0.4 convolution_bitcast_fusion
  41.8 0.7 convolution_bitcast_fusion.1
  42.4 0.7 fusion.19
  43.1 1.3 %collective-permute-start.3 = (f32[4,128,128]{2,1,0:T(8,128)S(1)}, f32[4,128,128]{2,1,0:T(8,128)S(1)}, u32[]{:S(2)}, u32[]{:S(2)}) collective-permute-start(f32[4,128,128]{2,1,0:T(8,128)S(1)} %fusion.19), channel_id=1, source_target_pairs={{12,0},{13,1},{14,2},{15,3},{28,16},{29,17},{30,18},{31,19}} | collective-permute-start | bytes 786440 | tf_op jit(solution)/shard_map/ppermute | solution.py:18
  44.5 1.3 %collective-permute-start.5 = (f32[4,136,128]{2,1,0:T(8,128)S(1)}, f32[4,136,128]{2,1,0:T(8,128)S(1)}, u32[]{:S(2)}, u32[]{:S(2)}) collective-permute-start(f32[4,136,128]{2,1,0:T(8,128)S(1)} %fusion.10), channel_id=1, source_target_pairs={{4,0},{8,4},{12,8},{5,1},{9,5},{13,9},{6,2},{10,6},{14,10},{7,3},{... | collective-permute-start | bytes 835592 | tf_op jit(solution)/shard_map/ppermute | solution.py:18
  45.8 1.3 %collective-permute-start.4 = (f32[4,136,128]{2,1,0:T(8,128)S(1)}, f32[4,136,128]{2,1,0:T(8,128)S(1)}, u32[]{:S(2)}, u32[]{:S(2)}) collective-permute-start(f32[4,136,128]{2,1,0:T(8,128)S(1)} %fusion.10), channel_id=1, source_target_pairs={{8,0},{12,4},{9,1},{13,5},{10,2},{14,6},{11,3},{15,7},{24,16},{28,... | collective-permute-start | bytes 835592 | tf_op jit(solution)/shard_map/ppermute | solution.py:18
  47.1 0.3 fusion.55
  47.4 0.5 fusion.3
  47.9 14.4 %collective-permute-done.5 = f32[4,136,128]{2,1,0:T(8,128)S(1)} collective-permute-done((f32[4,136,128]{2,1,0:T(8,128)S(1)}, f32[4,136,128]{2,1,0:T(8,128)S(1)}, u32[]{:S(2)}, u32[]{:S(2)}) %collective-permute-start.5) | collective-permute-done | bytes 278560 | tf_op jit(solution)/shard_map/ppermute | solution.py:18
  62.3 13.1 %collective-permute-done.4 = f32[4,136,128]{2,1,0:T(8,128)S(1)} collective-permute-done((f32[4,136,128]{2,1,0:T(8,128)S(1)}, f32[4,136,128]{2,1,0:T(8,128)S(1)}, u32[]{:S(2)}, u32[]{:S(2)}) %collective-permute-start.4) | collective-permute-done | bytes 278560 | tf_op jit(solution)/shard_map/ppermute | solution.py:18
  75.4 0.3 multiply_reduce_fusion
  75.8 0.7 fusion.5
  76.5 0.8 copy.116
  77.2 0.6 fusion.62
  77.8 0.8 copy.115
  78.6 0.8 copy.114
  80.1 1.1 %fusion.64 = f32[128,4,128]{2,1,0:T(4,128)S(1)} fusion(f32[128,4,128]{2,1,0:T(4,128)S(1)} %copy.113), kind=kOutput, calls=%fused_computation.121 | output fusion | flops 8323072 | bytes 524288 | tf_op jit(solution)/shard_map/transpose(jvp(jit(cumsum)))/reduce_window_sum | solution.py:78
  81.4 1.1 %fusion.63 = f32[128,4,128]{2,1,0:T(4,128)S(1)} fusion(f32[128,4,128]{2,1,0:T(4,128)S(1)} %copy.110), kind=kOutput, calls=%fused_computation.120 | output fusion | flops 8323072 | bytes 524288 | tf_op jit(solution)/shard_map/transpose(jvp(jit(cumsum)))/reduce_window_sum | solution.py:54
  82.4 0.6 fusion.51
  83.2 0.7 convert_element_type.135
  83.9 13.6 %all-reduce.2 = (f32[512]{0:T(512)S(1)}, f32[512]{0:T(512)S(1)}) all-reduce(f32[512]{0:T(512)S(1)} %add_bitcast_fusion, f32[512]{0:T(512)S(1)} %bitcast.118), channel_id=1, replica_groups=mesh['groups'=2,'ctx'=4,'head'=2,'rep'=2] {'ctx','rep'}, use_global_device_ids=true, to_apply=%region_11.13 | all-reduce | flops 1024 | bytes 8192 | tf_op jit(solution)/shard_map/psum | solution.py:156
  97.5 0.6 broadcast_multiply_fusion.1
  (44 shorter events, 2.1 us)
Async XLA Ops:
  0.6 0.7 copy-start.6
  1.3 2.2 %copy-start.3 = (bf16[1,128,512]{2,1,0:T(8,128)(2,1)S(1)}, bf16[1,128,512]{2,1,0:T(8,128)(2,1)}, u32[]{:S(2)}) copy-start(bf16[1,128,512]{2,1,0:T(8,128)(2,1)} %param.16) | copy-start | bytes 393220
  3.5 0.9 copy-start
  4.4 0.7 copy-start.5
  5.5 0.9 copy-start.1
  7.2 25.3 %collective-permute-start = (f32[4,128,128]{2,1,0:T(8,128)S(1)}, f32[4,128,128]{2,1,0:T(8,128)S(1)}, u32[]{:S(2)}, u32[]{:S(2)}) collective-permute-start(f32[4,128,128]{2,1,0:T(8,128)S(1)} %fusion.45), channel_id=1, source_target_pairs={{0,12},{1,13},{2,14},{3,15},{16,28},{17,29},{18,30},{19,31}} | collective-permute-start | bytes 786440 | tf_op jit(solution)/shard_map/ppermute | solution.py:18
  14.1 5.4 %copy-start.2 = (bf16[1,128,512]{2,1,0:T(8,128)(2,1)S(1)}, bf16[1,128,512]{2,1,0:T(8,128)(2,1)}, u32[]{:S(2)}) copy-start(bf16[1,128,512]{2,1,0:T(8,128)(2,1)} %param.14) | copy-start | bytes 393220
  14.2 12.6 %collective-permute-start.2 = (f32[4,136,128]{2,1,0:T(8,128)S(1)}, f32[4,136,128]{2,1,0:T(8,128)S(1)}, u32[]{:S(2)}, u32[]{:S(2)}) collective-permute-start(f32[4,136,128]{2,1,0:T(8,128)S(1)} %fusion.9), channel_id=1, source_target_pairs={{0,4},{4,8},{8,12},{1,5},{5,9},{9,13},{2,6},{6,10},{10,14},{3,7},{... | collective-permute-start | bytes 835592 | tf_op jit(solution)/shard_map/ppermute | solution.py:18
  15.6 16.1 %collective-permute-start.1 = (f32[4,136,128]{2,1,0:T(8,128)S(1)}, f32[4,136,128]{2,1,0:T(8,128)}, u32[]{:S(2)}, u32[]{:S(2)}) collective-permute-start(f32[4,136,128]{2,1,0:T(8,128)S(1)} %fusion.9), channel_id=1, source_target_pairs={{0,8},{4,12},{1,9},{5,13},{2,10},{6,14},{3,11},{7,15},{16,24},{20,... | collective-permute-start | bytes 835592 | tf_op jit(solution)/shard_map/ppermute | solution.py:18
  34.2 0.7 copy-start.4
  35.1 5.0 %copy-start.7 = (f32[1,128]{1,0:T(1,128)S(1)}, f32[1,128]{1,0:T(1,128)}, u32[]{:S(2)}) copy-start(f32[1,128]{1,0:T(1,128)} %param.20) | copy-start | bytes 1540
  40.1 0.5 copy-start.8
  43.1 32.3 %collective-permute-start.3 = (f32[4,128,128]{2,1,0:T(8,128)S(1)}, f32[4,128,128]{2,1,0:T(8,128)S(1)}, u32[]{:S(2)}, u32[]{:S(2)}) collective-permute-start(f32[4,128,128]{2,1,0:T(8,128)S(1)} %fusion.19), channel_id=1, source_target_pairs={{12,0},{13,1},{14,2},{15,3},{28,16},{29,17},{30,18},{31,19}} | collective-permute-start | bytes 786440 | tf_op jit(solution)/shard_map/ppermute | solution.py:18
  44.5 17.8 %collective-permute-start.5 = (f32[4,136,128]{2,1,0:T(8,128)S(1)}, f32[4,136,128]{2,1,0:T(8,128)S(1)}, u32[]{:S(2)}, u32[]{:S(2)}) collective-permute-start(f32[4,136,128]{2,1,0:T(8,128)S(1)} %fusion.10), channel_id=1, source_target_pairs={{4,0},{8,4},{12,8},{5,1},{9,5},{13,9},{6,2},{10,6},{14,10},{7,3},{... | collective-permute-start | bytes 835592 | tf_op jit(solution)/shard_map/ppermute | solution.py:18
  45.8 29.6 %collective-permute-start.4 = (f32[4,136,128]{2,1,0:T(8,128)S(1)}, f32[4,136,128]{2,1,0:T(8,128)S(1)}, u32[]{:S(2)}, u32[]{:S(2)}) collective-permute-start(f32[4,136,128]{2,1,0:T(8,128)S(1)} %fusion.10), channel_id=1, source_target_pairs={{8,0},{12,4},{9,1},{13,5},{10,2},{14,6},{11,3},{15,7},{24,16},{28,... | collective-permute-start | bytes 835592 | tf_op jit(solution)/shard_map/ppermute | solution.py:18

commit v3 on v2

--- a/solution.py
+++ b/solution.py
@@ -25,19 +25,30 @@
 
 
 def gather_scan(state, factor, span_count, direction):
-    if span_count == 1:
+    channels = state.shape[1]
+    near_a, near_b = None, None
+    run_a, run_b = state, factor
+    shift = 1
+    while shift < span_count:
+        last = 2 * shift >= span_count
+        if last:
+            far = from_behind(run_a, "ctx", direction * shift)
+            far_a, far_b = far, None
+        else:
+            far = from_behind(pack_state(run_a, factor=run_b), "ctx", direction * shift)
+            far_a, far_b = far[:, :channels], far[:, channels, :]
+        if near_a is None:
+            near_a, near_b = far_a, far_b
+        else:
+            near_a = far_a * near_b[..., None] + near_a
+            near_b = None if last else far_b * near_b
+        if not last:
+            run_a = far_a * run_b[..., None] + run_a
+            run_b = far_b * run_b
+        shift *= 2
+    if near_a is None:
         return jnp.zeros_like(state)
-    channels = state.shape[1]
-    packed = pack_state(state, factor)
-    received = []
-    for shift in range(1, span_count):
-        payload = packed if shift < span_count - 1 else state
-        received.append(from_behind(payload, "ctx", direction * shift))
-    total = received[-1][:, :channels]
-    for shift in range(span_count - 2, 0, -1):
-        part = received[shift - 1]
-        total = total * part[:, channels, :][..., None] + part[:, :channels]
-    return total
+    return near_a
 
 
 def log_decay(logit_in, bias_in):

time: 98.5 us -> 89.7 us (0.911)
  waiting for transfers between devices: 38.6 us -> 33.8 us
  starting transfers between devices: 15.4 us -> 13.1 us
    ppermute x6 -> x4, waiting for transfers between devices: 38.6 us -> 33.8 us  [from_behind(): return lax.ppermute(value, axis, pairs)]
    ppermute x6 -> x4, starting transfers between devices: 15.4 us -> 13.1 us  [from_behind(): return lax.ppermute(value, axis, pairs)]
  transfers between devices with their start and end apart: 6 -> 4, of which waited for: 4 -> 4; matrix products, arithmetic and copies ran while one was open for 3% -> 3% of each run, Pallas kernels for 0% -> 0%
where the time goes in v3:
time: 89.7 us; the launch traced here: 89.3 us
  waiting for transfers between devices  33.8 us (38%)
  blocking collectives  18.5 us (21%)
  starting transfers between devices  13.1 us (15%)
  local copies, waits for them, and re-layouts  8.73 us (10%)
  matrix products  6.48 us (7%)
  other arithmetic  6.4 us (7%)
  between operations  2.36 us (3%)
    ppermute x4, waiting for transfers between devices, from_behind(): return lax.ppermute(value, axis, pairs)  33.8 us
    psum x1, blocking collectives, on_device(): lax.psum((grad_bias.reshape(-1), grad_weight.reshape(-1)), ('ctx', 'rep'))  13.6 us
    ppermute x4, starting transfers between devices, from_behind(): return lax.ppermute(value, axis, pairs)  13.1 us
    unnamed x21, local copies, waits for them, and re-layouts  6.35 us
    psum x1, blocking collectives, on_device(): value_pred = lax.psum(partial_value, 'head')  4.94 us
  transfers between devices with their start and end apart: 4, of which 4 were waited for; matrix products, arithmetic and copies ran while one was open for 3% of the time, Pallas kernels for 0%

profile of v3, /device:TPU:0, one launch (start us, length us, event | category | flops | bytes accessed | tf_op | source)
XLA Modules:
  0.0 89.3 jit_solution(10864826514311277621)
XLA Ops:
  0.6 0.6 copy-done.6
  1.4 0.2 broadcast_in_dim.37
  1.6 0.5 slice.57
  2.9 0.6 compare_convert_fusion.1
  3.6 0.9 copy-done
  4.5 0.6 copy-done.5
  5.1 0.3 fusion.16
  5.6 0.8 copy-done.1
  6.5 0.3 multiply_reduce_fusion.2
  6.8 0.3 fusion.43
  7.2 5.1 %collective-permute-start = (f32[4,136,128]{2,1,0:T(8,128)S(1)}, f32[4,136,128]{2,1,0:T(8,128)S(1)}, u32[]{:S(2)}, u32[]{:S(2)}) collective-permute-start(f32[4,136,128]{2,1,0:T(8,128)S(1)} %fusion.9), channel_id=1, source_target_pairs={{0,4},{4,8},{8,12},{1,5},{5,9},{9,13},{2,6},{6,10},{10,14},{3,7},{... | collective-permute-start | bytes 835592 | tf_op jit(solution)/shard_map/ppermute | solution.py:18
  13.2 0.6 fusion.4
  13.9 4.3 %collective-permute-done = f32[4,136,128]{2,1,0:T(8,128)S(1)} collective-permute-done((f32[4,136,128]{2,1,0:T(8,128)S(1)}, f32[4,136,128]{2,1,0:T(8,128)S(1)}, u32[]{:S(2)}, u32[]{:S(2)}) %collective-permute-start) | collective-permute-done | bytes 278560 | tf_op jit(solution)/shard_map/ppermute | solution.py:18
  18.3 5.4 %collective-permute-start.1 = (f32[4,128,128]{2,1,0:T(8,128)S(1)}, f32[4,128,128]{2,1,0:T(8,128)S(1)}, u32[]{:S(2)}, u32[]{:S(2)}) collective-permute-start(f32[4,128,128]{2,1,0:T(8,128)S(1)} %multiply_add_fusion.5), channel_id=1, source_target_pairs={{0,8},{4,12},{1,9},{5,13},{2,10},{6,14},{3,11},{7,15},{16,24},{20,... | collective-permute-start | bytes 786440 | tf_op jit(solution)/shard_map/ppermute | solution.py:18
  23.7 0.2 fusion.39
  24.0 4.4 %collective-permute-done.1 = f32[4,128,128]{2,1,0:T(8,128)S(1)} collective-permute-done((f32[4,128,128]{2,1,0:T(8,128)S(1)}, f32[4,128,128]{2,1,0:T(8,128)S(1)}, u32[]{:S(2)}, u32[]{:S(2)}) %collective-permute-start.1) | collective-permute-done | bytes 262176 | tf_op jit(solution)/shard_map/ppermute | solution.py:18
  28.6 0.6 multiply_reduce_fusion.1
  29.2 0.6 copy-done.4
  29.9 0.2 convolution_bitcast_fusion.2
  30.1 4.9 %psum.21 = f32[128]{0:T(128)S(1)} all-reduce(f32[128]{0:T(128)S(1)} %convolution_bitcast_fusion.2), channel_id=1, replica_groups=mesh['groups'=2,'ctx'=4,'head'=2,'rep'=2] {'head'}, use_global_device_ids=true, to_apply=%region_3.5 | all-reduce | flops 128 | bytes 1024 | tf_op jit(solution)/shard_map/psum | solution.py:150
  35.1 0.5 copy-done.8
  35.8 0.3 fusion.6
  36.0 0.3 fusion.8
  36.4 0.7 fusion.17
  37.1 1.3 %collective-permute-start.2 = (f32[4,136,128]{2,1,0:T(8,128)S(1)}, f32[4,136,128]{2,1,0:T(8,128)S(1)}, u32[]{:S(2)}, u32[]{:S(2)}) collective-permute-start(f32[4,136,128]{2,1,0:T(8,128)S(1)} %fusion.10), channel_id=1, source_target_pairs={{4,0},{8,4},{12,8},{5,1},{9,5},{13,9},{6,2},{10,6},{14,10},{7,3},{... | collective-permute-start | bytes 835592 | tf_op jit(solution)/shard_map/ppermute | solution.py:18
  38.4 0.4 convolution_bitcast_fusion
  38.8 0.6 convolution_bitcast_fusion.1
  39.5 12.3 %collective-permute-done.2 = f32[4,136,128]{2,1,0:T(8,128)S(1)} collective-permute-done((f32[4,136,128]{2,1,0:T(8,128)S(1)}, f32[4,136,128]{2,1,0:T(8,128)S(1)}, u32[]{:S(2)}, u32[]{:S(2)}) %collective-permute-start.2) | collective-permute-done | bytes 278560 | tf_op jit(solution)/shard_map/ppermute | solution.py:18
  51.9 1.3 %collective-permute-start.3 = (f32[4,128,128]{2,1,0:T(8,128)S(1)}, f32[4,128,128]{2,1,0:T(8,128)S(1)}, u32[]{:S(2)}, u32[]{:S(2)}) collective-permute-start(f32[4,128,128]{2,1,0:T(8,128)S(1)} %multiply_add_fusion.3), channel_id=1, source_target_pairs={{8,0},{12,4},{9,1},{13,5},{10,2},{14,6},{11,3},{15,7},{24,16},{28,... | collective-permute-start | bytes 786440 | tf_op jit(solution)/shard_map/ppermute | solution.py:18
  53.2 0.3 fusion.53
  53.5 0.5 fusion.3
  54.0 12.7 %collective-permute-done.3 = f32[4,128,128]{2,1,0:T(8,128)S(1)} collective-permute-done((f32[4,128,128]{2,1,0:T(8,128)S(1)}, f32[4,128,128]{2,1,0:T(8,128)S(1)}, u32[]{:S(2)}, u32[]{:S(2)}) %collective-permute-start.3) | collective-permute-done | bytes 262176 | tf_op jit(solution)/shard_map/ppermute | solution.py:18
  66.7 0.2 multiply_reduce_fusion
  67.0 0.7 fusion.5
  67.7 0.8 copy.144
  68.5 0.6 fusion.60
  69.1 0.8 copy.143
  69.8 0.8 copy.142
  70.8 0.1 copy.139
  70.9 0.1 multiply_add_fusion
  71.4 1.1 %fusion.62 = f32[128,4,128]{2,1,0:T(4,128)S(1)} fusion(f32[128,4,128]{2,1,0:T(4,128)S(1)} %copy.141), kind=kOutput, calls=%fused_computation.120 | output fusion | flops 8323072 | bytes 524288 | tf_op jit(solution)/shard_map/transpose(jvp(jit(cumsum)))/reduce_window_sum | solution.py:89
  72.5 0.1 copy.138
  72.6 1.1 %fusion.61 = f32[128,4,128]{2,1,0:T(4,128)S(1)} fusion(f32[128,4,128]{2,1,0:T(4,128)S(1)} %copy.138), kind=kOutput, calls=%fused_computation.119 | output fusion | flops 8323072 | bytes 524288 | tf_op jit(solution)/shard_map/transpose(jvp(jit(cumsum)))/reduce_window_sum | solution.py:65
  73.7 0.6 fusion.49
  74.3 0.1 add_convert_fusion
  74.4 0.7 convert_element_type.135
  75.2 13.6 %all-reduce.2 = (f32[512]{0:T(512)S(1)}, f32[512]{0:T(512)S(1)}) all-reduce(f32[512]{0:T(512)S(1)} %add_bitcast_fusion, f32[512]{0:T(512)S(1)} %bitcast.116), channel_id=1, replica_groups=mesh['groups'=2,'ctx'=4,'head'=2,'rep'=2] {'ctx','rep'}, use_global_device_ids=true, to_apply=%region_11.13 | all-reduce | flops 1024 | bytes 8192 | tf_op jit(solution)/shard_map/psum | solution.py:167
  88.7 0.6 broadcast_multiply_fusion.1
  (41 shorter events, 1.9 us)
Async XLA Ops:
  0.6 0.7 copy-start.6
  1.3 2.2 %copy-start.3 = (bf16[1,128,512]{2,1,0:T(8,128)(2,1)S(1)}, bf16[1,128,512]{2,1,0:T(8,128)(2,1)}, u32[]{:S(2)}) copy-start(bf16[1,128,512]{2,1,0:T(8,128)(2,1)} %param.16) | copy-start | bytes 393220
  3.5 0.9 %copy-start = (bf16[1,128,512]{2,1,0:T(8,128)(2,1)S(1)}, bf16[1,128,512]{2,1,0:T(8,128)(2,1)}, u32[]{:S(2)}) copy-start(bf16[1,128,512]{2,1,0:T(8,128)(2,1)} %param.17) | copy-start | bytes 393220
  4.4 0.7 copy-start.5
  5.5 0.9 %copy-start.1 = (bf16[1,128,512]{2,1,0:T(8,128)(2,1)S(1)}, bf16[1,128,512]{2,1,0:T(8,128)(2,1)}, u32[]{:S(2)}) copy-start(bf16[1,128,512]{2,1,0:T(8,128)(2,1)} %param.15) | copy-start | bytes 393220
  7.2 5.9 %copy-start.2 = (bf16[1,128,512]{2,1,0:T(8,128)(2,1)S(1)}, bf16[1,128,512]{2,1,0:T(8,128)(2,1)}, u32[]{:S(2)}) copy-start(bf16[1,128,512]{2,1,0:T(8,128)(2,1)} %param.14) | copy-start | bytes 393220
  7.2 11.0 %collective-permute-start = (f32[4,136,128]{2,1,0:T(8,128)S(1)}, f32[4,136,128]{2,1,0:T(8,128)S(1)}, u32[]{:S(2)}, u32[]{:S(2)}) collective-permute-start(f32[4,136,128]{2,1,0:T(8,128)S(1)} %fusion.9), channel_id=1, source_target_pairs={{0,4},{4,8},{8,12},{1,5},{5,9},{9,13},{2,6},{6,10},{10,14},{3,7},{... | collective-permute-start | bytes 835592 | tf_op jit(solution)/shard_map/ppermute | solution.py:18
  18.3 10.1 %collective-permute-start.1 = (f32[4,128,128]{2,1,0:T(8,128)S(1)}, f32[4,128,128]{2,1,0:T(8,128)S(1)}, u32[]{:S(2)}, u32[]{:S(2)}) collective-permute-start(f32[4,128,128]{2,1,0:T(8,128)S(1)} %multiply_add_fusion.5), channel_id=1, source_target_pairs={{0,8},{4,12},{1,9},{5,13},{2,10},{6,14},{3,11},{7,15},{16,24},{20,... | collective-permute-start | bytes 786440 | tf_op jit(solution)/shard_map/ppermute | solution.py:18
  29.2 0.7 copy-start.4
  30.1 5.0 %copy-start.7 = (f32[1,128]{1,0:T(1,128)S(1)}, f32[1,128]{1,0:T(1,128)}, u32[]{:S(2)}) copy-start(f32[1,128]{1,0:T(1,128)} %param.20) | copy-start | bytes 1540
  35.1 0.5 copy-start.8
  37.1 14.6 %collective-permute-start.2 = (f32[4,136,128]{2,1,0:T(8,128)S(1)}, f32[4,136,128]{2,1,0:T(8,128)S(1)}, u32[]{:S(2)}, u32[]{:S(2)}) collective-permute-start(f32[4,136,128]{2,1,0:T(8,128)S(1)} %fusion.10), channel_id=1, source_target_pairs={{4,0},{8,4},{12,8},{5,1},{9,5},{13,9},{6,2},{10,6},{14,10},{7,3},{... | collective-permute-start | bytes 835592 | tf_op jit(solution)/shard_map/ppermute | solution.py:18
  51.9 14.8 %collective-permute-start.3 = (f32[4,128,128]{2,1,0:T(8,128)S(1)}, f32[4,128,128]{2,1,0:T(8,128)S(1)}, u32[]{:S(2)}, u32[]{:S(2)}) collective-permute-start(f32[4,128,128]{2,1,0:T(8,128)S(1)} %multiply_add_fusion.3), channel_id=1, source_target_pairs={{8,0},{12,4},{9,1},{13,5},{10,2},{14,6},{11,3},{15,7},{24,16},{28,... | collective-permute-start | bytes 786440 | tf_op jit(solution)/shard_map/ppermute | solution.py:18

commit v4 on v3

--- a/solution.py
+++ b/solution.py
@@ -16,6 +16,18 @@
     length = lax.axis_size(axis)
     pairs = [(i, i + by) for i in range(length) if 0 <= i + by < length]
     return lax.ppermute(value, axis, pairs)
+
+
+def butterfly_sum(value, axis):
+    length = lax.axis_size(axis)
+    if length & (length - 1):
+        return lax.psum(value, axis)
+    bit = 1
+    while bit < length:
+        pairs = [(i, i ^ bit) for i in range(length)]
+        value = value + lax.ppermute(value, axis, pairs)
+        bit *= 2
+    return value
 
 
 def pack_state(state, factor):
@@ -147,7 +159,7 @@
         return jnp.einsum("thd,hd->t", normed, weight_in, precision=highest)
 
     partial_value, pull_value = jax.vjp(value_head, attended, value_weight.reshape(head_count, DV))
-    value_pred = lax.psum(partial_value, "head")
+    value_pred = butterfly_sum(partial_value, "head")
     residual = value_pred - targets[0]
     grad_attended, grad_weight = pull_value(residual)
     grad_carried = jnp.einsum("thd,hcd->thc", grad_attended, state_in, precision=highest)
@@ -164,9 +176,11 @@
     grad_logit = inner_grads[3] + summary_grads[2]
     grad_bias = inner_grads[4] + summary_grads[3]
     token_total = token_count * lax.axis_size("ctx") * lax.axis_size("rep")
-    bias_total, weight_total = lax.psum(
-        (grad_bias.reshape(-1), grad_weight.reshape(-1)), ("ctx", "rep")
-    )
+    both_total = butterfly_sum(
+        butterfly_sum(jnp.concatenate([grad_bias.reshape(-1), grad_weight.reshape(-1)]), "rep"),
+        "ctx",
+    )
+    bias_total, weight_total = jnp.split(both_total, 2)
 
     def to_rows(array):
         return array.reshape(1, token_count, -1).astype(jnp.bfloat16)

time: 89.7 us -> 79.6 us (0.89)
  blocking collectives: 18.5 us -> 0 us
  waiting for transfers between devices: 33.8 us -> 40.6 us
  starting transfers between devices: 13.1 us -> 14.7 us
    psum x2 -> x0, blocking collectives: 18.5 us -> none  [the longest x1 13.6 us: on_device(): lax.psum((grad_bias.reshape(-1), grad_weight.reshape(-1)), ('ctx', 'rep'))]
    ppermute x0 -> x4, waiting for transfers between devices: none -> 7.17 us  [butterfly_sum(): value = value + lax.ppermute(value, axis, pairs)]
    ppermute x0 -> x4, starting transfers between devices: none -> 1.63 us  [butterfly_sum(): value = value + lax.ppermute(value, axis, pairs)]
    unnamed x21 -> x19, local copies, waits for them, and re-layouts: 6.35 us -> 5.84 us
  transfers between devices with their start and end apart: 4 -> 8, of which waited for: 4 -> 8; matrix products, arithmetic and copies ran while one was open for 3% -> 9% of each run, Pallas kernels for 0% -> 0%
where the time goes in v4:
time: 79.6 us; the launch traced here: 79.3 us
  waiting for transfers between devices  40.6 us (51%)
  starting transfers between devices  14.7 us (18%)
  local copies, waits for them, and re-layouts  8.22 us (10%)
  other arithmetic  6.93 us (9%)
  matrix products  6.49 us (8%)
  between operations  2.38 us (3%)
    ppermute x4, waiting for transfers between devices, from_behind(): return lax.ppermute(value, axis, pairs)  33.4 us
    ppermute x4, starting transfers between devices, from_behind(): return lax.ppermute(value, axis, pairs)  13.1 us
    ppermute x4, waiting for transfers between devices, butterfly_sum(): value = value + lax.ppermute(value, axis, pairs)  7.17 us
    unnamed x19, local copies, waits for them, and re-layouts  5.84 us
    dot_general x3, matrix products, block_inner(): scores = jnp.einsum('ihc,jhc->hij', query_dec, key_dec, precision=highest)  1.64 us
    dot_general x3, matrix products, block_summary(): jnp.einsum('jhc,jhd->hcd', key_tail, value_in, precision=highest)  1.64 us
    ppermute x4, starting transfers between devices, butterfly_sum(): value = value + lax.ppermute(value, axis, pairs)  1.63 us
  transfers between devices with their start and end apart: 8, of which 8 were waited for; matrix products, arithmetic and copies ran while one was open for 9% of the time, Pallas kernels for 0%

profile of v4, /device:TPU:0, one launch (start us, length us, event | category | flops | bytes accessed | tf_op | source)
XLA Modules:
  0.0 79.3 jit_solution(16996890119751912196)
XLA Ops:
  0.6 0.6 copy-done.6
  1.4 0.2 broadcast_in_dim.37
  1.6 0.5 slice.57
  2.9 0.6 compare_convert_fusion.1
  3.6 0.9 %copy-done = bf16[1,128,512]{2,1,0:T(8,128)(2,1)S(1)} copy-done((bf16[1,128,512]{2,1,0:T(8,128)(2,1)S(1)}, bf16[1,128,512]{2,1,0:T(8,128)(2,1)}, u32[]{:S(2)}) %copy-start) | copy-done | bytes 131096
  4.5 0.6 copy-done.5
  5.1 0.3 fusion.16
  5.6 0.8 copy-done.1
  6.5 0.3 multiply_reduce_fusion.2
  6.8 0.3 fusion.43
  7.2 5.1 %collective-permute-start = (f32[4,136,128]{2,1,0:T(8,128)S(1)}, f32[4,136,128]{2,1,0:T(8,128)S(1)}, u32[]{:S(2)}, u32[]{:S(2)}) collective-permute-start(f32[4,136,128]{2,1,0:T(8,128)S(1)} %fusion.9), channel_id=1, source_target_pairs={{0,4},{4,8},{8,12},{1,5},{5,9},{9,13},{2,6},{6,10},{10,14},{3,7},{... | collective-permute-start | bytes 835592 | tf_op jit(solution)/shard_map/ppermute | solution.py:18
  13.2 0.6 fusion.4
  13.9 4.3 %collective-permute-done = f32[4,136,128]{2,1,0:T(8,128)S(1)} collective-permute-done((f32[4,136,128]{2,1,0:T(8,128)S(1)}, f32[4,136,128]{2,1,0:T(8,128)S(1)}, u32[]{:S(2)}, u32[]{:S(2)}) %collective-permute-start) | collective-permute-done | bytes 278560 | tf_op jit(solution)/shard_map/ppermute | solution.py:18
  18.3 5.4 %collective-permute-start.1 = (f32[4,128,128]{2,1,0:T(8,128)S(1)}, f32[4,128,128]{2,1,0:T(8,128)S(1)}, u32[]{:S(2)}, u32[]{:S(2)}) collective-permute-start(f32[4,128,128]{2,1,0:T(8,128)S(1)} %multiply_add_fusion.5), channel_id=1, source_target_pairs={{0,8},{4,12},{1,9},{5,13},{2,10},{6,14},{3,11},{7,15},{16,24},{20,... | collective-permute-start | bytes 786440 | tf_op jit(solution)/shard_map/ppermute | solution.py:18
  23.7 0.2 fusion.39
  24.0 4.4 %collective-permute-done.1 = f32[4,128,128]{2,1,0:T(8,128)S(1)} collective-permute-done((f32[4,128,128]{2,1,0:T(8,128)S(1)}, f32[4,128,128]{2,1,0:T(8,128)S(1)}, u32[]{:S(2)}, u32[]{:S(2)}) %collective-permute-start.1) | collective-permute-done | bytes 262176 | tf_op jit(solution)/shard_map/ppermute | solution.py:18
  28.6 0.6 multiply_reduce_fusion.1
  29.3 0.6 copy-done.4
  29.9 0.2 convolution_bitcast_fusion.2
  30.1 1.6 %collective-permute-start.2 = (f32[128]{0:T(128)S(1)}, f32[128]{0:T(128)S(1)}, u32[]{:S(2)}, u32[]{:S(2)}) collective-permute-start(f32[128]{0:T(128)S(1)} %convolution_bitcast_fusion.2), channel_id=1, source_target_pairs={{0,2},{2,0},{1,3},{3,1},{4,6},{6,4},{5,7},{7,5},{8,10},{10,8},{9,1... | collective-permute-start | bytes 1544 | tf_op jit(solution)/shard_map/ppermute | solution.py:28
  31.7 2.0 %collective-permute-done.2 = f32[128]{0:T(128)S(1)} collective-permute-done((f32[128]{0:T(128)S(1)}, f32[128]{0:T(128)S(1)}, u32[]{:S(2)}, u32[]{:S(2)}) %collective-permute-start.2) | collective-permute-done | bytes 544 | tf_op jit(solution)/shard_map/ppermute | solution.py:28
  33.7 0.5 bitcast_subtract_fusion
  34.4 0.7 fusion.17
  35.2 1.3 %collective-permute-start.3 = (f32[4,136,128]{2,1,0:T(8,128)S(1)}, f32[4,136,128]{2,1,0:T(8,128)S(1)}, u32[]{:S(2)}, u32[]{:S(2)}) collective-permute-start(f32[4,136,128]{2,1,0:T(8,128)S(1)} %fusion.10), channel_id=1, source_target_pairs={{4,0},{8,4},{12,8},{5,1},{9,5},{13,9},{6,2},{10,6},{14,10},{7,3},{... | collective-permute-start | bytes 835592 | tf_op jit(solution)/shard_map/ppermute | solution.py:18
  36.5 0.3 fusion.8
  36.8 0.4 convolution_bitcast_fusion
  37.2 0.6 convolution_bitcast_fusion.1
  37.9 12.0 %collective-permute-done.3 = f32[4,136,128]{2,1,0:T(8,128)S(1)} collective-permute-done((f32[4,136,128]{2,1,0:T(8,128)S(1)}, f32[4,136,128]{2,1,0:T(8,128)S(1)}, u32[]{:S(2)}, u32[]{:S(2)}) %collective-permute-start.3) | collective-permute-done | bytes 278560 | tf_op jit(solution)/shard_map/ppermute | solution.py:18
  50.0 1.3 %collective-permute-start.4 = (f32[4,128,128]{2,1,0:T(8,128)S(1)}, f32[4,128,128]{2,1,0:T(8,128)S(1)}, u32[]{:S(2)}, u32[]{:S(2)}) collective-permute-start(f32[4,128,128]{2,1,0:T(8,128)S(1)} %multiply_add_fusion.3), channel_id=1, source_target_pairs={{8,0},{12,4},{9,1},{13,5},{10,2},{14,6},{11,3},{15,7},{24,16},{28,... | collective-permute-start | bytes 786440 | tf_op jit(solution)/shard_map/ppermute | solution.py:18
  51.3 0.3 fusion.53
  51.6 0.5 fusion.3
  52.1 12.7 %collective-permute-done.4 = f32[4,128,128]{2,1,0:T(8,128)S(1)} collective-permute-done((f32[4,128,128]{2,1,0:T(8,128)S(1)}, f32[4,128,128]{2,1,0:T(8,128)S(1)}, u32[]{:S(2)}, u32[]{:S(2)}) %collective-permute-start.4) | collective-permute-done | bytes 262176 | tf_op jit(solution)/shard_map/ppermute | solution.py:18
  64.8 0.2 multiply_reduce_fusion
  65.1 0.6 fusion.61
  65.8 0.1 copy.139
  66.4 1.1 %fusion.63 = f32[128,4,128]{2,1,0:T(4,128)S(1)} fusion(f32[128,4,128]{2,1,0:T(4,128)S(1)} %copy.141), kind=kOutput, calls=%fused_computation.123 | output fusion | flops 8323072 | bytes 524288 | tf_op jit(solution)/shard_map/transpose(jvp(jit(cumsum)))/reduce_window_sum | solution.py:101
  67.7 1.1 %fusion.62 = f32[128,4,128]{2,1,0:T(4,128)S(1)} fusion(f32[128,4,128]{2,1,0:T(4,128)S(1)} %copy.138), kind=kOutput, calls=%fused_computation.122 | output fusion | flops 8323072 | bytes 524288 | tf_op jit(solution)/shard_map/transpose(jvp(jit(cumsum)))/reduce_window_sum | solution.py:77
  68.8 0.6 fusion.49
  69.4 0.3 fusion.6
  69.7 0.9 %collective-permute-done.5 = f32[1024]{0:T(1024)S(1)} collective-permute-done((f32[1024]{0:T(1024)S(1)}, f32[1024]{0:T(1024)S(1)}, u32[]{:S(2)}, u32[]{:S(2)}) %collective-permute-start.5) | collective-permute-done | bytes 4128 | tf_op jit(solution)/shard_map/ppermute | solution.py:28
  70.6 0.7 fusion.5
  71.3 2.9 %collective-permute-done.6 = f32[1024]{0:T(1024)S(1)} collective-permute-done((f32[1024]{0:T(1024)S(1)}, f32[1024]{0:T(1024)S(1)}, u32[]{:S(2)}, u32[]{:S(2)}) %collective-permute-start.6) | collective-permute-done | bytes 4128 | tf_op jit(solution)/shard_map/ppermute | solution.py:28
  74.4 0.8 copy.144
  75.1 0.8 copy.143
  75.9 0.8 copy.142
  76.7 0.7 convert_element_type.135
  77.4 1.3 %collective-permute-done.7 = f32[1024]{0:T(1024)S(1)} collective-permute-done((f32[1024]{0:T(1024)S(1)}, f32[1024]{0:T(1024)S(1)}, u32[]{:S(2)}, u32[]{:S(2)}) %collective-permute-start.7) | collective-permute-done | bytes 4128 | tf_op jit(solution)/shard_map/ppermute | solution.py:28
  78.7 0.6 slice_multiply_fusion
  (49 shorter events, 2.5 us)
Async XLA Ops:
  0.6 0.7 copy-start.6
  1.3 2.2 %copy-start.3 = (bf16[1,128,512]{2,1,0:T(8,128)(2,1)S(1)}, bf16[1,128,512]{2,1,0:T(8,128)(2,1)}, u32[]{:S(2)}) copy-start(bf16[1,128,512]{2,1,0:T(8,128)(2,1)} %param.16) | copy-start | bytes 393220
  3.5 0.9 %copy-start = (bf16[1,128,512]{2,1,0:T(8,128)(2,1)S(1)}, bf16[1,128,512]{2,1,0:T(8,128)(2,1)}, u32[]{:S(2)}) copy-start(bf16[1,128,512]{2,1,0:T(8,128)(2,1)} %param.17) | copy-start | bytes 393220
  4.4 0.7 copy-start.5
  5.5 0.9 %copy-start.1 = (bf16[1,128,512]{2,1,0:T(8,128)(2,1)S(1)}, bf16[1,128,512]{2,1,0:T(8,128)(2,1)}, u32[]{:S(2)}) copy-start(bf16[1,128,512]{2,1,0:T(8,128)(2,1)} %param.15) | copy-start | bytes 393220
  7.2 5.9 %copy-start.2 = (bf16[1,128,512]{2,1,0:T(8,128)(2,1)S(1)}, bf16[1,128,512]{2,1,0:T(8,128)(2,1)}, u32[]{:S(2)}) copy-start(bf16[1,128,512]{2,1,0:T(8,128)(2,1)} %param.14) | copy-start | bytes 393220
  7.2 11.0 %collective-permute-start = (f32[4,136,128]{2,1,0:T(8,128)S(1)}, f32[4,136,128]{2,1,0:T(8,128)S(1)}, u32[]{:S(2)}, u32[]{:S(2)}) collective-permute-start(f32[4,136,128]{2,1,0:T(8,128)S(1)} %fusion.9), channel_id=1, source_target_pairs={{0,4},{4,8},{8,12},{1,5},{5,9},{9,13},{2,6},{6,10},{10,14},{3,7},{... | collective-permute-start | bytes 835592 | tf_op jit(solution)/shard_map/ppermute | solution.py:18
  18.3 10.1 %collective-permute-start.1 = (f32[4,128,128]{2,1,0:T(8,128)S(1)}, f32[4,128,128]{2,1,0:T(8,128)S(1)}, u32[]{:S(2)}, u32[]{:S(2)}) collective-permute-start(f32[4,128,128]{2,1,0:T(8,128)S(1)} %multiply_add_fusion.5), channel_id=1, source_target_pairs={{0,8},{4,12},{1,9},{5,13},{2,10},{6,14},{3,11},{7,15},{16,24},{20,... | collective-permute-start | bytes 786440 | tf_op jit(solution)/shard_map/ppermute | solution.py:18
  29.2 0.7 copy-start.4
  29.9 3.8 %copy-start.7 = (f32[1,128]{1,0:T(1,128)S(1)}, f32[1,128]{1,0:T(1,128)}, u32[]{:S(2)}) copy-start(f32[1,128]{1,0:T(1,128)} %param.20) | copy-start | bytes 1540
  30.1 3.6 %collective-permute-start.2 = (f32[128]{0:T(128)S(1)}, f32[128]{0:T(128)S(1)}, u32[]{:S(2)}, u32[]{:S(2)}) collective-permute-start(f32[128]{0:T(128)S(1)} %convolution_bitcast_fusion.2), channel_id=1, source_target_pairs={{0,2},{2,0},{1,3},{3,1},{4,6},{6,4},{5,7},{7,5},{8,10},{10,8},{9,1... | collective-permute-start | bytes 1544 | tf_op jit(solution)/shard_map/ppermute | solution.py:28
  35.2 14.6 %collective-permute-start.3 = (f32[4,136,128]{2,1,0:T(8,128)S(1)}, f32[4,136,128]{2,1,0:T(8,128)S(1)}, u32[]{:S(2)}, u32[]{:S(2)}) collective-permute-start(f32[4,136,128]{2,1,0:T(8,128)S(1)} %fusion.10), channel_id=1, source_target_pairs={{4,0},{8,4},{12,8},{5,1},{9,5},{13,9},{6,2},{10,6},{14,10},{7,3},{... | collective-permute-start | bytes 835592 | tf_op jit(solution)/shard_map/ppermute | solution.py:18
  50.0 14.8 %collective-permute-start.4 = (f32[4,128,128]{2,1,0:T(8,128)S(1)}, f32[4,128,128]{2,1,0:T(8,128)S(1)}, u32[]{:S(2)}, u32[]{:S(2)}) collective-permute-start(f32[4,128,128]{2,1,0:T(8,128)S(1)} %multiply_add_fusion.3), channel_id=1, source_target_pairs={{8,0},{12,4},{9,1},{13,5},{10,2},{14,6},{11,3},{15,7},{24,16},{28,... | collective-permute-start | bytes 786440 | tf_op jit(solution)/shard_map/ppermute | solution.py:18
  69.4 1.2 %collective-permute-start.5 = (f32[1024]{0:T(1024)S(1)}, f32[1024]{0:T(1024)S(1)}, u32[]{:S(2)}, u32[]{:S(2)}) collective-permute-start(f32[1024]{0:T(1024)S(1)} %pad_maximum_fusion), channel_id=1, source_target_pairs={{0,1},{1,0},{2,3},{3,2},{4,5},{5,4},{6,7},{7,6},{8,9},{9,8},{10,11... | collective-permute-start | bytes 12296 | tf_op jit(solution)/shard_map/ppermute | solution.py:28
  70.6 3.6 %collective-permute-start.6 = (f32[1024]{0:T(1024)S(1)}, f32[1024]{0:T(1024)S(1)}, u32[]{:S(2)}, u32[]{:S(2)}) collective-permute-start(f32[1024]{0:T(1024)S(1)} %fusion.59), channel_id=1, source_target_pairs={{0,4},{4,0},{8,12},{12,8},{1,5},{5,1},{9,13},{13,9},{2,6},{6,2},{1... | collective-permute-start | bytes 12296 | tf_op jit(solution)/shard_map/ppermute | solution.py:28
  74.2 4.5 %collective-permute-start.7 = (f32[1024]{0:T(1024)S(1)}, f32[1024]{0:T(1024)S(1)}, u32[]{:S(2)}, u32[]{:S(2)}) collective-permute-start(f32[1024]{0:T(1024)S(1)} %add.110), channel_id=1, source_target_pairs={{0,8},{4,12},{8,0},{12,4},{1,9},{5,13},{9,1},{13,5},{2,10},{6,14},... | collective-permute-start | bytes 12296 | tf_op jit(solution)/shard_map/ppermute | solution.py:28

commit v5 on v4

--- a/solution.py
+++ b/solution.py
@@ -28,6 +28,22 @@
         value = value + lax.ppermute(value, axis, pairs)
         bit *= 2
     return value
+
+
+def direct_sum(value, axis):
+    length = lax.axis_size(axis)
+    me = lax.axis_index(axis)
+    terms = [value]
+    for shift in range(1, length):
+        pairs = [(i, (i + shift) % length) for i in range(length)]
+        terms.append(lax.ppermute(value, axis, pairs))
+    stacked = jnp.stack(terms)
+    order = (me - jnp.arange(length, dtype=jnp.int32)) % length
+    ordered = jnp.take(stacked, order, axis=0)
+    total = ordered[0]
+    for member in range(1, length):
+        total = total + ordered[member]
+    return total
 
 
 def pack_state(state, factor):
@@ -176,7 +192,7 @@
     grad_logit = inner_grads[3] + summary_grads[2]
     grad_bias = inner_grads[4] + summary_grads[3]
     token_total = token_count * lax.axis_size("ctx") * lax.axis_size("rep")
-    both_total = butterfly_sum(
+    both_total = direct_sum(
         butterfly_sum(jnp.concatenate([grad_bias.reshape(-1), grad_weight.reshape(-1)]), "rep"),
         "ctx",
     )

time: 79.6 us -> 78.8 us (0.990)
  waiting for transfers between devices: 40.6 us -> 37 us
  starting transfers between devices: 14.7 us -> 16.7 us
    ppermute x4 -> x2, waiting for transfers between devices: 7.17 us -> 2.49 us  [butterfly_sum(): value = value + lax.ppermute(value, axis, pairs)]
    ppermute x0 -> x3, starting transfers between devices: none -> 2.02 us  [direct_sum(): terms.append(lax.ppermute(value, axis, pairs))]
    ppermute x0 -> x3, waiting for transfers between devices: none -> 0.81 us  [direct_sum(): terms.append(lax.ppermute(value, axis, pairs))]
    ppermute x4 -> x2, starting transfers between devices: 1.63 us -> 1.63 us  [butterfly_sum(): value = value + lax.ppermute(value, axis, pairs)]
  transfers between devices with their start and end apart: 8 -> 9, of which waited for: 8 -> 7; matrix products, arithmetic and copies ran while one was open for 9% -> 9% of each run, Pallas kernels for 0% -> 0%
where the time goes in v5:
time: 78.8 us; the launch traced here: 78.5 us
  waiting for transfers between devices  37 us (47%)
  starting transfers between devices  16.7 us (21%)
  local copies, waits for them, and re-layouts  8.79 us (11%)
  other arithmetic  7.06 us (9%)
  matrix products  6.49 us (8%)
  between operations  2.43 us (3%)
    ppermute x4, waiting for transfers between devices, from_behind(): return lax.ppermute(value, axis, pairs)  33.7 us
    ppermute x4, starting transfers between devices, from_behind(): return lax.ppermute(value, axis, pairs)  13.1 us
    unnamed x19, local copies, waits for them, and re-layouts  5.84 us
    ppermute x2, waiting for transfers between devices, butterfly_sum(): value = value + lax.ppermute(value, axis, pairs)  2.49 us
    ppermute x3, starting transfers between devices, direct_sum(): terms.append(lax.ppermute(value, axis, pairs))  2.02 us
    dot_general x3, matrix products, block_inner(): scores = jnp.einsum('ihc,jhc->hij', query_dec, key_dec, precision=highest)  1.63 us
    dot_general x3, matrix products, block_summary(): jnp.einsum('jhc,jhd->hcd', key_tail, value_in, precision=highest)  1.63 us
    ppermute x2, starting transfers between devices, butterfly_sum(): value = value + lax.ppermute(value, axis, pairs)  1.63 us
  transfers between devices with their start and end apart: 9, of which 7 were waited for; matrix products, arithmetic and copies ran while one was open for 9% of the time, Pallas kernels for 0%

profile of v5, /device:TPU:0, one launch (start us, length us, event | category | flops | bytes accessed | tf_op | source)
XLA Modules:
  0.0 78.5 jit_solution(16440109318752015440)
XLA Ops:
  0.6 0.6 copy-done.6
  1.4 0.2 broadcast_in_dim.47
  1.6 0.5 slice.77
  2.9 0.6 compare_convert_fusion.1
  3.6 0.9 %copy-done = bf16[1,128,512]{2,1,0:T(8,128)(2,1)S(1)} copy-done((bf16[1,128,512]{2,1,0:T(8,128)(2,1)S(1)}, bf16[1,128,512]{2,1,0:T(8,128)(2,1)}, u32[]{:S(2)}) %copy-start) | copy-done | bytes 131096
  4.5 0.6 copy-done.5
  5.1 0.3 fusion.16
  5.6 0.8 copy-done.1
  6.5 0.3 multiply_reduce_fusion.2
  6.8 0.3 fusion.43
  7.2 5.1 %collective-permute-start = (f32[4,136,128]{2,1,0:T(8,128)S(1)}, f32[4,136,128]{2,1,0:T(8,128)S(1)}, u32[]{:S(2)}, u32[]{:S(2)}) collective-permute-start(f32[4,136,128]{2,1,0:T(8,128)S(1)} %fusion.9), channel_id=1, source_target_pairs={{0,4},{4,8},{8,12},{1,5},{5,9},{9,13},{2,6},{6,10},{10,14},{3,7},{... | collective-permute-start | bytes 835592 | tf_op jit(solution)/shard_map/ppermute | solution.py:18
  13.3 0.6 fusion.4
  13.9 4.3 %collective-permute-done = f32[4,136,128]{2,1,0:T(8,128)S(1)} collective-permute-done((f32[4,136,128]{2,1,0:T(8,128)S(1)}, f32[4,136,128]{2,1,0:T(8,128)S(1)}, u32[]{:S(2)}, u32[]{:S(2)}) %collective-permute-start) | collective-permute-done | bytes 278560 | tf_op jit(solution)/shard_map/ppermute | solution.py:18
  18.3 5.4 %collective-permute-start.1 = (f32[4,128,128]{2,1,0:T(8,128)S(1)}, f32[4,128,128]{2,1,0:T(8,128)S(1)}, u32[]{:S(2)}, u32[]{:S(2)}) collective-permute-start(f32[4,128,128]{2,1,0:T(8,128)S(1)} %multiply_add_fusion.5), channel_id=1, source_target_pairs={{0,8},{4,12},{1,9},{5,13},{2,10},{6,14},{3,11},{7,15},{16,24},{20,... | collective-permute-start | bytes 786440 | tf_op jit(solution)/shard_map/ppermute | solution.py:18
  23.7 0.2 fusion.39
  24.0 4.4 %collective-permute-done.1 = f32[4,128,128]{2,1,0:T(8,128)S(1)} collective-permute-done((f32[4,128,128]{2,1,0:T(8,128)S(1)}, f32[4,128,128]{2,1,0:T(8,128)S(1)}, u32[]{:S(2)}, u32[]{:S(2)}) %collective-permute-start.1) | collective-permute-done | bytes 262176 | tf_op jit(solution)/shard_map/ppermute | solution.py:18
  28.6 0.6 multiply_reduce_fusion.1
  29.2 0.6 copy-done.4
  29.9 0.2 convolution_bitcast_fusion.2
  30.1 1.6 %collective-permute-start.2 = (f32[128]{0:T(128)S(1)}, f32[128]{0:T(128)S(1)}, u32[]{:S(2)}, u32[]{:S(2)}) collective-permute-start(f32[128]{0:T(128)S(1)} %convolution_bitcast_fusion.2), channel_id=1, source_target_pairs={{0,2},{2,0},{1,3},{3,1},{4,6},{6,4},{5,7},{7,5},{8,10},{10,8},{9,1... | collective-permute-start | bytes 1544 | tf_op jit(solution)/shard_map/ppermute | solution.py:28
  31.7 2.0 %collective-permute-done.2 = f32[128]{0:T(128)S(1)} collective-permute-done((f32[128]{0:T(128)S(1)}, f32[128]{0:T(128)S(1)}, u32[]{:S(2)}, u32[]{:S(2)}) %collective-permute-start.2) | collective-permute-done | bytes 544 | tf_op jit(solution)/shard_map/ppermute | solution.py:28
  33.8 0.5 bitcast_subtract_fusion
  34.4 0.3 fusion.6
  34.7 0.3 fusion.8
  35.0 0.7 fusion.17
  35.8 1.3 %collective-permute-start.3 = (f32[4,136,128]{2,1,0:T(8,128)S(1)}, f32[4,136,128]{2,1,0:T(8,128)S(1)}, u32[]{:S(2)}, u32[]{:S(2)}) collective-permute-start(f32[4,136,128]{2,1,0:T(8,128)S(1)} %fusion.10), channel_id=1, source_target_pairs={{4,0},{8,4},{12,8},{5,1},{9,5},{13,9},{6,2},{10,6},{14,10},{7,3},{... | collective-permute-start | bytes 835592 | tf_op jit(solution)/shard_map/ppermute | solution.py:18
  37.1 0.4 convolution_bitcast_fusion
  37.5 0.6 convolution_bitcast_fusion.1
  38.1 12.3 %collective-permute-done.3 = f32[4,136,128]{2,1,0:T(8,128)S(1)} collective-permute-done((f32[4,136,128]{2,1,0:T(8,128)S(1)}, f32[4,136,128]{2,1,0:T(8,128)S(1)}, u32[]{:S(2)}, u32[]{:S(2)}) %collective-permute-start.3) | collective-permute-done | bytes 278560 | tf_op jit(solution)/shard_map/ppermute | solution.py:18
  50.6 1.3 %collective-permute-start.4 = (f32[4,128,128]{2,1,0:T(8,128)S(1)}, f32[4,128,128]{2,1,0:T(8,128)S(1)}, u32[]{:S(2)}, u32[]{:S(2)}) collective-permute-start(f32[4,128,128]{2,1,0:T(8,128)S(1)} %multiply_add_fusion.3), channel_id=1, source_target_pairs={{8,0},{12,4},{9,1},{13,5},{10,2},{14,6},{11,3},{15,7},{24,16},{28,... | collective-permute-start | bytes 786440 | tf_op jit(solution)/shard_map/ppermute | solution.py:18
  51.9 0.3 fusion.56
  52.2 0.5 fusion.3
  52.7 12.7 %collective-permute-done.4 = f32[4,128,128]{2,1,0:T(8,128)S(1)} collective-permute-done((f32[4,128,128]{2,1,0:T(8,128)S(1)}, f32[4,128,128]{2,1,0:T(8,128)S(1)}, u32[]{:S(2)}, u32[]{:S(2)}) %collective-permute-start.4) | collective-permute-done | bytes 262176 | tf_op jit(solution)/shard_map/ppermute | solution.py:18
  65.4 0.2 multiply_reduce_fusion
  65.7 0.6 fusion.64
  67.0 1.1 %fusion.66 = f32[128,4,128]{2,1,0:T(4,128)S(1)} fusion(f32[128,4,128]{2,1,0:T(4,128)S(1)} %copy.141), kind=kOutput, calls=%fused_computation.142 | output fusion | flops 8323072 | bytes 524288 | tf_op jit(solution)/shard_map/transpose(jvp(jit(cumsum)))/reduce_window_sum | solution.py:117
  68.3 1.1 %fusion.65 = f32[128,4,128]{2,1,0:T(4,128)S(1)} fusion(f32[128,4,128]{2,1,0:T(4,128)S(1)} %copy.138), kind=kOutput, calls=%fused_computation.141 | output fusion | flops 8323072 | bytes 524288 | tf_op jit(solution)/shard_map/transpose(jvp(jit(cumsum)))/reduce_window_sum | solution.py:93
  69.4 0.6 fusion.49
  70.0 0.7 fusion.5
  70.7 0.5 collective-permute-done.5
  71.3 1.9 %collective-permute-start.6 = (f32[1024]{0:T(1024)S(1)}, f32[1024]{0:T(1024)S(1)}, u32[]{:S(2)}, u32[]{:S(2)}) collective-permute-start(f32[1024]{0:T(1024)S(1)} %fusion.62), channel_id=1, source_target_pairs={{0,4},{4,8},{8,12},{12,0},{1,5},{5,9},{9,13},{13,1},{2,6},{6,10},{... | collective-permute-start | bytes 12296 | tf_op jit(solution)/shard_map/ppermute | solution.py:39
  73.4 0.8 copy.144
  74.2 0.8 copy.143
  74.9 0.8 copy.142
  75.7 0.7 convert_element_type.135
  76.4 0.8 %collective-permute-done.6 = f32[1024]{0:T(1024)S(1)} collective-permute-done((f32[1024]{0:T(1024)S(1)}, f32[1024]{0:T(1024)S(1)}, u32[]{:S(2)}, u32[]{:S(2)}) %collective-permute-start.6) | collective-permute-done | bytes 4128 | tf_op jit(solution)/shard_map/ppermute | solution.py:39
  77.2 0.6 gather_fusion
  77.9 0.6 slice_multiply_fusion
  (56 shorter events, 2.8 us)
Async XLA Ops:
  0.6 0.7 copy-start.6
  1.3 2.2 %copy-start.3 = (bf16[1,128,512]{2,1,0:T(8,128)(2,1)S(1)}, bf16[1,128,512]{2,1,0:T(8,128)(2,1)}, u32[]{:S(2)}) copy-start(bf16[1,128,512]{2,1,0:T(8,128)(2,1)} %param.16) | copy-start | bytes 393220
  3.5 0.9 %copy-start = (bf16[1,128,512]{2,1,0:T(8,128)(2,1)S(1)}, bf16[1,128,512]{2,1,0:T(8,128)(2,1)}, u32[]{:S(2)}) copy-start(bf16[1,128,512]{2,1,0:T(8,128)(2,1)} %param.17) | copy-start | bytes 393220
  4.4 0.7 copy-start.5
  5.5 0.9 %copy-start.1 = (bf16[1,128,512]{2,1,0:T(8,128)(2,1)S(1)}, bf16[1,128,512]{2,1,0:T(8,128)(2,1)}, u32[]{:S(2)}) copy-start(bf16[1,128,512]{2,1,0:T(8,128)(2,1)} %param.15) | copy-start | bytes 393220
  7.2 5.9 %copy-start.2 = (bf16[1,128,512]{2,1,0:T(8,128)(2,1)S(1)}, bf16[1,128,512]{2,1,0:T(8,128)(2,1)}, u32[]{:S(2)}) copy-start(bf16[1,128,512]{2,1,0:T(8,128)(2,1)} %param.14) | copy-start | bytes 393220
  7.2 11.0 %collective-permute-start = (f32[4,136,128]{2,1,0:T(8,128)S(1)}, f32[4,136,128]{2,1,0:T(8,128)S(1)}, u32[]{:S(2)}, u32[]{:S(2)}) collective-permute-start(f32[4,136,128]{2,1,0:T(8,128)S(1)} %fusion.9), channel_id=1, source_target_pairs={{0,4},{4,8},{8,12},{1,5},{5,9},{9,13},{2,6},{6,10},{10,14},{3,7},{... | collective-permute-start | bytes 835592 | tf_op jit(solution)/shard_map/ppermute | solution.py:18
  18.3 10.1 %collective-permute-start.1 = (f32[4,128,128]{2,1,0:T(8,128)S(1)}, f32[4,128,128]{2,1,0:T(8,128)S(1)}, u32[]{:S(2)}, u32[]{:S(2)}) collective-permute-start(f32[4,128,128]{2,1,0:T(8,128)S(1)} %multiply_add_fusion.5), channel_id=1, source_target_pairs={{0,8},{4,12},{1,9},{5,13},{2,10},{6,14},{3,11},{7,15},{16,24},{20,... | collective-permute-start | bytes 786440 | tf_op jit(solution)/shard_map/ppermute | solution.py:18
  29.2 0.7 copy-start.4
  30.1 3.6 %copy-start.7 = (f32[1,128]{1,0:T(1,128)S(1)}, f32[1,128]{1,0:T(1,128)}, u32[]{:S(2)}) copy-start(f32[1,128]{1,0:T(1,128)} %param.20) | copy-start | bytes 1540
  30.1 3.6 %collective-permute-start.2 = (f32[128]{0:T(128)S(1)}, f32[128]{0:T(128)S(1)}, u32[]{:S(2)}, u32[]{:S(2)}) collective-permute-start(f32[128]{0:T(128)S(1)} %convolution_bitcast_fusion.2), channel_id=1, source_target_pairs={{0,2},{2,0},{1,3},{3,1},{4,6},{6,4},{5,7},{7,5},{8,10},{10,8},{9,1... | collective-permute-start | bytes 1544 | tf_op jit(solution)/shard_map/ppermute | solution.py:28
  35.8 14.6 %collective-permute-start.3 = (f32[4,136,128]{2,1,0:T(8,128)S(1)}, f32[4,136,128]{2,1,0:T(8,128)S(1)}, u32[]{:S(2)}, u32[]{:S(2)}) collective-permute-start(f32[4,136,128]{2,1,0:T(8,128)S(1)} %fusion.10), channel_id=1, source_target_pairs={{4,0},{8,4},{12,8},{5,1},{9,5},{13,9},{6,2},{10,6},{14,10},{7,3},{... | collective-permute-start | bytes 835592 | tf_op jit(solution)/shard_map/ppermute | solution.py:18
  50.6 14.8 %collective-permute-start.4 = (f32[4,128,128]{2,1,0:T(8,128)S(1)}, f32[4,128,128]{2,1,0:T(8,128)S(1)}, u32[]{:S(2)}, u32[]{:S(2)}) collective-permute-start(f32[4,128,128]{2,1,0:T(8,128)S(1)} %multiply_add_fusion.3), channel_id=1, source_target_pairs={{8,0},{12,4},{9,1},{13,5},{10,2},{14,6},{11,3},{15,7},{24,16},{28,... | collective-permute-start | bytes 786440 | tf_op jit(solution)/shard_map/ppermute | solution.py:18
  70.0 1.2 %collective-permute-start.5 = (f32[1024]{0:T(1024)S(1)}, f32[1024]{0:T(1024)S(1)}, u32[]{:S(2)}, u32[]{:S(2)}) collective-permute-start(f32[1024]{0:T(1024)S(1)} %pad_maximum_fusion.1), channel_id=1, source_target_pairs={{0,1},{1,0},{2,3},{3,2},{4,5},{5,4},{6,7},{7,6},{8,9},{9,8},{10,11... | collective-permute-start | bytes 12296 | tf_op jit(solution)/shard_map/ppermute | solution.py:28
  71.2 5.2 %collective-permute-start.8 = (f32[1024]{0:T(1024)S(1)}, f32[1024]{0:T(1024)S(1)}, u32[]{:S(2)}, u32[]{:S(2)}) collective-permute-start(f32[1024]{0:T(1024)S(1)} %fusion.62), channel_id=1, source_target_pairs={{0,12},{4,0},{8,4},{12,8},{1,13},{5,1},{9,5},{13,9},{2,14},{6,2},{... | collective-permute-start | bytes 12296 | tf_op jit(solution)/shard_map/ppermute | solution.py:39
  71.2 5.2 %collective-permute-start.7 = (f32[1024]{0:T(1024)S(1)}, f32[1024]{0:T(1024)S(1)}, u32[]{:S(2)}, u32[]{:S(2)}) collective-permute-start(f32[1024]{0:T(1024)S(1)} %fusion.62), channel_id=1, source_target_pairs={{0,8},{4,12},{8,0},{12,4},{1,9},{5,13},{9,1},{13,5},{2,10},{6,14},... | collective-permute-start | bytes 12296 | tf_op jit(solution)/shard_map/ppermute | solution.py:39
  71.3 5.9 %collective-permute-start.6 = (f32[1024]{0:T(1024)S(1)}, f32[1024]{0:T(1024)S(1)}, u32[]{:S(2)}, u32[]{:S(2)}) collective-permute-start(f32[1024]{0:T(1024)S(1)} %fusion.62), channel_id=1, source_target_pairs={{0,4},{4,8},{8,12},{12,0},{1,5},{5,9},{9,13},{13,1},{2,6},{6,10},{... | collective-permute-start | bytes 12296 | tf_op jit(solution)/shard_map/ppermute | solution.py:39

commit v6 on v5

--- a/solution.py
+++ b/solution.py
@@ -125,6 +125,19 @@
     return block_state, block_decay
 
 
+def bias_transfer(key_in, value_in, logit_in, bias_in, start_flags, state_in, block_decay):
+    slope = jax.nn.sigmoid(-(logit_in + bias_in)) / gate_scale
+    log_cum = jnp.cumsum(log_decay(logit_in, bias_in), axis=0)
+    log_last = log_cum[-1]
+    segment = segment_ids(start_flags)
+    tail_mask = (segment == segment[-1]).astype(jnp.float32)
+    key_tail = key_in * jnp.exp(log_last[None] - log_cum) * tail_mask[:, None, None]
+    from_end = jnp.cumsum(slope[::-1], axis=0)[::-1]
+    later = jnp.concatenate([from_end[1:], jnp.zeros_like(from_end[:1])], axis=0)
+    through = jnp.einsum("thc,thd->hcd", key_tail * later, value_in, precision=highest)
+    return through + (block_decay * from_end[0])[..., None] * state_in
+
+
 def on_device(
     queries,
     per_head_keys,
@@ -180,7 +193,10 @@
     grad_attended, grad_weight = pull_value(residual)
     grad_carried = jnp.einsum("thd,hcd->thc", grad_attended, state_in, precision=highest)
     grad_direct = jnp.einsum("thc,thd->hcd", carried, grad_attended, precision=highest)
-    inner_grads = pull_inner((grad_attended, grad_carried))
+    inner_grads = lax.optimization_barrier(pull_inner((grad_attended, grad_carried)))
+    transfer = bias_transfer(key_f, value_f, logit_f, bias_h, start_flags, state_in, decay_local)
+    transfer_in = gather_scan(transfer, decay_local, span_count, 1)
+    bias_far = jnp.sum(grad_direct * transfer_in, axis=-1)
 
     grad_state = gather_scan(grad_direct, decay_local, span_count, -1)
     grad_decay = jnp.sum(state_in * grad_state, axis=-1)
@@ -190,7 +206,7 @@
     grad_key = inner_grads[1] + summary_grads[0]
     grad_value = inner_grads[2] + summary_grads[1]
     grad_logit = inner_grads[3] + summary_grads[2]
-    grad_bias = inner_grads[4] + summary_grads[3]
+    grad_bias = inner_grads[4] + bias_far
     token_total = token_count * lax.axis_size("ctx") * lax.axis_size("rep")
     both_total = direct_sum(
         butterfly_sum(jnp.concatenate([grad_bias.reshape(-1), grad_weight.reshape(-1)]), "rep"),

time: 78.8 us -> 100 us (1.27)
  starting transfers between devices: 16.7 us -> 39.3 us
  waiting for transfers between devices: 37 us -> 28.5 us
  local copies, waits for them, and re-layouts: 8.79 us -> 13 us
  other arithmetic: 7.06 us -> 9.43 us
    ppermute x4 -> x6, starting transfers between devices: 13.1 us -> 27.4 us  [from_behind(): return lax.ppermute(value, axis, pairs)]
    ppermute x4 -> x6, waiting for transfers between devices: 33.7 us -> 23.7 us  [from_behind(): return lax.ppermute(value, axis, pairs)]
    ppermute x3, starting transfers between devices: 2.02 us -> 10.3 us  [direct_sum(): terms.append(lax.ppermute(value, axis, pairs))]
    unnamed x19 -> x59, local copies, waits for them, and re-layouts: 5.84 us -> 9.61 us
    ppermute x3, waiting for transfers between devices: 0.81 us -> 2.51 us  [direct_sum(): terms.append(lax.ppermute(value, axis, pairs))]
  transfers between devices with their start and end apart: 9 -> 11, of which waited for: 7 -> 9; matrix products, arithmetic and copies ran while one was open for 9% -> 6% of each run, Pallas kernels for 0% -> 0%
where the time goes in v6:
time: 100 us; the launch traced here: 99.6 us
  starting transfers between devices  39.3 us (39%)
  waiting for transfers between devices  28.5 us (28%)
  local copies, waits for them, and re-layouts  13 us (13%)
  other arithmetic  9.43 us (9%)
  matrix products  6.79 us (7%)
  between operations  2.63 us (3%)
    ppermute x6, starting transfers between devices, from_behind(): return lax.ppermute(value, axis, pairs)  27.4 us
    ppermute x6, waiting for transfers between devices, from_behind(): return lax.ppermute(value, axis, pairs)  23.7 us
    ppermute x3, starting transfers between devices, direct_sum(): terms.append(lax.ppermute(value, axis, pairs))  10.3 us
    unnamed x59, local copies, waits for them, and re-layouts  9.61 us
    ppermute x3, waiting for transfers between devices, direct_sum(): terms.append(lax.ppermute(value, axis, pairs))  2.51 us
    ppermute x2, waiting for transfers between devices, butterfly_sum(): value = value + lax.ppermute(value, axis, pairs)  2.26 us
  transfers between devices with their start and end apart: 11, of which 9 were waited for; matrix products, arithmetic and copies ran while one was open for 6% of the time, Pallas kernels for 0%

profile of v6, /device:TPU:0, one launch (start us, length us, event | category | flops | bytes accessed | tf_op | source)
XLA Modules:
  0.0 99.6 jit_solution(5581322944368216121)
XLA Ops:
  0.6 0.6 copy-done.24
  1.6 0.5 slice.114
  2.9 1.2 %compare_convert_fusion.1 = (f32[128]{0:T(128)}, f32[128]{0:T(128)S(1)}) fusion(s32[128]{0:T(128)S(1)} %reduce.4, s32[]{:T(128)} %bitcast.7), kind=kLoop, calls=%fused_computation.150 | loop fusion | flops 512 | bytes 1540 | tf_op jit(solution)/shard_map/jvp()/convert_element_type | solution.py:95
  4.1 0.9 copy-done.1
  5.0 0.6 copy-done.15
  6.1 0.8 copy-done.2
  7.9 4.9 %collective-permute-start = (f32[4,136,128]{2,1,0:T(8,128)S(1)}, f32[4,136,128]{2,1,0:T(8,128)S(1)}, u32[]{:S(2)}, u32[]{:S(2)}) collective-permute-start(f32[4,136,128]{2,1,0:T(8,128)S(1)} %fusion.12), channel_id=1, source_target_pairs={{0,4},{4,8},{8,12},{1,5},{5,9},{9,13},{2,6},{6,10},{10,14},{3,7},{... | collective-permute-start | bytes 835592 | tf_op jit(solution)/shard_map/ppermute | solution.py:18
  13.9 0.7 copy-done.3
  14.8 0.6 fusion.5
  15.5 3.3 %collective-permute-done = f32[4,136,128]{2,1,0:T(8,128)S(1)} collective-permute-done((f32[4,136,128]{2,1,0:T(8,128)S(1)}, f32[4,136,128]{2,1,0:T(8,128)S(1)}, u32[]{:S(2)}, u32[]{:S(2)}) %collective-permute-start) | collective-permute-done | bytes 278560 | tf_op jit(solution)/shard_map/ppermute | solution.py:18
  18.9 5.4 %collective-permute-start.1 = (f32[4,128,128]{2,1,0:T(8,128)S(1)}, f32[4,128,128]{2,1,0:T(8,128)S(1)}, u32[]{:S(2)}, u32[]{:S(2)}) collective-permute-start(f32[4,128,128]{2,1,0:T(8,128)S(1)} %multiply_add_fusion.7), channel_id=1, source_target_pairs={{0,8},{4,12},{1,9},{5,13},{2,10},{6,14},{3,11},{7,15},{16,24},{20,... | collective-permute-start | bytes 786440 | tf_op jit(solution)/shard_map/ppermute | solution.py:18
  24.3 0.6 fusion.78
  25.7 3.3 %collective-permute-done.1 = f32[4,128,128]{2,1,0:T(8,128)S(1)} collective-permute-done((f32[4,128,128]{2,1,0:T(8,128)S(1)}, f32[4,128,128]{2,1,0:T(8,128)S(1)}, u32[]{:S(2)}, u32[]{:S(2)}) %collective-permute-start.1) | collective-permute-done | bytes 262176 | tf_op jit(solution)/shard_map/ppermute | solution.py:18
  29.1 0.6 multiply_reduce_fusion.2
  29.8 0.6 copy-done.5
  30.7 1.6 %collective-permute-start.2 = (f32[128]{0:T(128)S(1)}, f32[128]{0:T(128)S(1)}, u32[]{:S(2)}, u32[]{:S(2)}) collective-permute-start(f32[128]{0:T(128)S(1)} %convolution_bitcast_fusion.3), channel_id=1, source_target_pairs={{0,2},{2,0},{1,3},{3,1},{4,6},{6,4},{5,7},{7,5},{8,10},{10,8},{9,1... | collective-permute-start | bytes 1544 | tf_op jit(solution)/shard_map/ppermute | solution.py:28
  32.6 1.7 %collective-permute-done.2 = f32[128]{0:T(128)S(1)} collective-permute-done((f32[128]{0:T(128)S(1)}, f32[128]{0:T(128)S(1)}, u32[]{:S(2)}, u32[]{:S(2)}) %collective-permute-start.2) | collective-permute-done | bytes 544 | tf_op jit(solution)/shard_map/ppermute | solution.py:28
  34.3 0.5 bitcast_subtract_fusion
  35.0 0.6 copy-done.17
  36.3 0.6 convolution_bitcast_fusion.2
  37.0 0.7 fusion.33
  37.7 0.6 copy-done.23
  38.3 0.5 exponential_multiply_fusion
  38.9 0.8 multiply_add_fusion.5
  39.9 1.1 %fusion.91 = f32[128,4,128]{2,1,0:T(4,128)S(1)} fusion(f32[128,4,128]{2,1,0:T(4,128)S(1)} %copy.162), kind=kOutput, calls=%fused_computation.169 | output fusion | flops 8323072 | bytes 524288 | tf_op jit(solution)/shard_map/transpose(jvp(jit(cumsum)))/reduce_window_sum | solution.py:93
  41.0 9.0 %collective-permute-start.5 = (f32[4,136,128]{2,1,0:T(8,128)S(1)}, f32[4,136,128]{2,1,0:T(8,128)S(1)}, u32[]{:S(2)}, u32[]{:S(2)}) collective-permute-start(f32[4,136,128]{2,1,0:T(8,128)S(1)} %get-tuple-element.103), channel_id=1, source_target_pairs={{0,4},{4,8},{8,12},{1,5},{5,9},{9,13},{2,6},{6,10},{10,14},{3,7},{... | collective-permute-start | bytes 835592 | tf_op jit(solution)/shard_map/ppermute | solution.py:18
  50.0 0.5 fusion.71
  50.6 1.3 %collective-permute-start.3 = (f32[4,136,128]{2,1,0:T(8,128)S(1)}, f32[4,136,128]{2,1,0:T(8,128)S(1)}, u32[]{:S(2)}, u32[]{:S(2)}) collective-permute-start(f32[4,136,128]{2,1,0:T(8,128)S(1)} %get-tuple-element.104), channel_id=1, source_target_pairs={{4,0},{8,4},{12,8},{5,1},{9,5},{13,9},{6,2},{10,6},{14,10},{7,3},{... | collective-permute-start | bytes 835592 | tf_op jit(solution)/shard_map/ppermute | solution.py:18
  52.2 2.7 %collective-permute-done.5 = f32[4,136,128]{2,1,0:T(8,128)S(1)} collective-permute-done((f32[4,136,128]{2,1,0:T(8,128)S(1)}, f32[4,136,128]{2,1,0:T(8,128)S(1)}, u32[]{:S(2)}, u32[]{:S(2)}) %collective-permute-start.5) | collective-permute-done | bytes 278560 | tf_op jit(solution)/shard_map/ppermute | solution.py:18
  55.0 5.3 %collective-permute-start.6 = (f32[4,128,128]{2,1,0:T(8,128)S(1)}, f32[4,128,128]{2,1,0:T(8,128)S(1)}, u32[]{:S(2)}, u32[]{:S(2)}) collective-permute-start(f32[4,128,128]{2,1,0:T(8,128)S(1)} %multiply_add_fusion), channel_id=1, source_target_pairs={{0,8},{4,12},{1,9},{5,13},{2,10},{6,14},{3,11},{7,15},{16,24},{20,... | collective-permute-start | bytes 786440 | tf_op jit(solution)/shard_map/ppermute | solution.py:18
  60.8 3.4 %collective-permute-done.6 = f32[4,128,128]{2,1,0:T(8,128)S(1)} collective-permute-done((f32[4,128,128]{2,1,0:T(8,128)S(1)}, f32[4,128,128]{2,1,0:T(8,128)S(1)}, u32[]{:S(2)}, u32[]{:S(2)}) %collective-permute-start.6) | collective-permute-done | bytes 262176 | tf_op jit(solution)/shard_map/ppermute | solution.py:18
  64.6 0.6 copy-done.26
  65.2 0.6 collective-permute-done.7
  65.8 9.7 %collective-permute-start.10 = (f32[1024]{0:T(1024)S(1)}, f32[1024]{0:T(1024)S(1)}, u32[]{:S(2)}, u32[]{:S(2)}) collective-permute-start(f32[1024]{0:T(1024)S(1)} %fusion.88), channel_id=1, source_target_pairs={{0,12},{4,0},{8,4},{12,8},{1,13},{5,1},{9,5},{13,9},{2,14},{6,2},{... | collective-permute-start | bytes 12296 | tf_op jit(solution)/shard_map/ppermute | solution.py:39
  75.5 0.6 collective-permute-start.8
  76.1 0.8 copy.173
  76.9 1.5 %collective-permute-start.4 = (f32[4,128,128]{2,1,0:T(8,128)S(1)}, f32[4,128,128]{2,1,0:T(8,128)S(1)}, u32[]{:S(2)}, u32[]{:S(2)}) collective-permute-start(f32[4,128,128]{2,1,0:T(8,128)S(1)} %get-tuple-element.100), channel_id=1, source_target_pairs={{8,0},{12,4},{9,1},{13,5},{10,2},{14,6},{11,3},{15,7},{24,16},{28,... | collective-permute-start | bytes 786440 | tf_op jit(solution)/shard_map/ppermute | solution.py:18
  78.4 1.6 %collective-permute-done.9 = f32[1024]{0:T(1024)S(1)} collective-permute-done((f32[1024]{0:T(1024)S(1)}, f32[1024]{0:T(1024)S(1)}, u32[]{:S(2)}, u32[]{:S(2)}) %collective-permute-start.9) | collective-permute-done | bytes 4128 | tf_op jit(solution)/shard_map/ppermute | solution.py:39
  80.0 0.9 collective-permute-done.8
  80.9 0.6 gather_fusion
  81.6 0.6 slice_multiply_fusion
  82.1 11.0 %collective-permute-done.4 = f32[4,128,128]{2,1,0:T(8,128)S(1)} collective-permute-done((f32[4,128,128]{2,1,0:T(8,128)S(1)}, f32[4,128,128]{2,1,0:T(8,128)S(1)}, u32[]{:S(2)}, u32[]{:S(2)}) %collective-permute-start.4) | collective-permute-done | bytes 262176 | tf_op jit(solution)/shard_map/ppermute | solution.py:18
  94.0 0.7 fusion.6
  94.9 0.5 fusion.89
  95.4 0.8 copy.175
  96.2 0.8 copy.174
  97.7 1.2 %add_convert_fusion = bf16[128,4,128]{2,1,0:T(4,128)(2,1)S(1)} fusion(f32[128,4,128]{2,1,0:T(4,128)S(1)} %fusion.72, f32[128,4,128]{2,1,0:T(4,128)S(1)} %get-tuple-element.93, f32[128,4,128]{2,1,0:T(4,128)S(1)} %copy.169), kind=kOutput, calls=%fused_computation.57 | output fusion | flops 8716288 | bytes 917504 | tf_op jit(solution)/shard_map/transpose(jvp(jit(cumsum)))/reduce_window_sum | solution.py:117
  98.9 0.7 convert_element_type.135
  (111 shorter events, 8.4 us)
Async XLA Ops:
  0.6 0.7 copy-start.24
  1.3 2.7 %copy-start.4 = (bf16[1,128,512]{2,1,0:T(8,128)(2,1)S(1)}, bf16[1,128,512]{2,1,0:T(8,128)(2,1)}, u32[]{:S(2)}) copy-start(bf16[1,128,512]{2,1,0:T(8,128)(2,1)} %param.18) | copy-start | bytes 393220
  4.0 28.2 %copy-start.21 = (f32[128]{0:T(128)}, f32[128]{0:T(128)S(1)}, u32[]{:S(2)}) copy-start(f32[128]{0:T(128)S(1)} %get-tuple-element.110) | copy-start | bytes 1540
  4.0 0.9 copy-start.1
  4.9 0.7 copy-start.15
  6.0 0.9 copy-start.2
  7.3 0.6 copy-start.13
  7.3 6.6 %copy-start.7 = (f32[4,128]{1,0:T(4,128)}, f32[4,128]{1,0:T(4,128)S(1)}, u32[]{:S(2)}) copy-start(f32[4,128]{1,0:T(4,128)S(1)} %get-tuple-element.85) | copy-start | bytes 6148
  7.9 10.8 %collective-permute-start = (f32[4,136,128]{2,1,0:T(8,128)S(1)}, f32[4,136,128]{2,1,0:T(8,128)S(1)}, u32[]{:S(2)}, u32[]{:S(2)}) collective-permute-start(f32[4,136,128]{2,1,0:T(8,128)S(1)} %fusion.12), channel_id=1, source_target_pairs={{0,4},{4,8},{8,12},{1,5},{5,9},{9,13},{2,6},{6,10},{10,14},{3,7},{... | collective-permute-start | bytes 835592 | tf_op jit(solution)/shard_map/ppermute | solution.py:18
  13.8 0.9 copy-start.3
  14.7 4.1 %copy-start.9 = (f32[4,128]{1,0:T(4,128)}, f32[4,128]{1,0:T(4,128)S(1)}, u32[]{:S(2)}) copy-start(f32[4,128]{1,0:T(4,128)S(1)} %get-tuple-element.87) | copy-start | bytes 6148
  18.9 10.1 %collective-permute-start.1 = (f32[4,128,128]{2,1,0:T(8,128)S(1)}, f32[4,128,128]{2,1,0:T(8,128)S(1)}, u32[]{:S(2)}, u32[]{:S(2)}) collective-permute-start(f32[4,128,128]{2,1,0:T(8,128)S(1)} %multiply_add_fusion.7), channel_id=1, source_target_pairs={{0,8},{4,12},{1,9},{5,13},{2,10},{6,14},{3,11},{7,15},{16,24},{20,... | collective-permute-start | bytes 786440 | tf_op jit(solution)/shard_map/ppermute | solution.py:18
  29.8 0.7 copy-start.5
  30.7 3.6 %collective-permute-start.2 = (f32[128]{0:T(128)S(1)}, f32[128]{0:T(128)S(1)}, u32[]{:S(2)}, u32[]{:S(2)}) collective-permute-start(f32[128]{0:T(128)S(1)} %convolution_bitcast_fusion.3), channel_id=1, source_target_pairs={{0,2},{2,0},{1,3},{3,1},{4,6},{6,4},{5,7},{7,5},{8,10},{10,8},{9,1... | collective-permute-start | bytes 1544 | tf_op jit(solution)/shard_map/ppermute | solution.py:28
  32.3 2.0 %copy-start.25 = (f32[1,128]{1,0:T(1,128)S(1)}, f32[1,128]{1,0:T(1,128)}, u32[]{:S(2)}) copy-start(f32[1,128]{1,0:T(1,128)} %param.22) | copy-start | bytes 1540
  34.8 2.9 %copy-start.11 = (f32[128]{0:T(128)}, f32[128]{0:T(128)S(1)}, u32[]{:S(2)}) copy-start(f32[128]{0:T(128)S(1)} %get-tuple-element.107) | copy-start | bytes 1540
  35.0 0.6 copy-start.17
  35.0 0.6 copy-start.19
  37.7 0.7 copy-start.23
  39.8 1.1 %copy-start.14 = (f32[4,128]{1,0:T(4,128)S(1)}, f32[4,128]{1,0:T(4,128)}, u32[]{:S(2)}) copy-start(f32[4,128]{1,0:T(4,128)} %copy-done.13) | copy-start | bytes 6148
  41.0 9.0 %copy-start.16 = (f32[512]{0:T(512)S(1)}, f32[512]{0:T(512)}, u32[]{:S(2)}) copy-start(f32[512]{0:T(512)} %param.20) | copy-start | bytes 6148
  41.0 13.9 %collective-permute-start.5 = (f32[4,136,128]{2,1,0:T(8,128)S(1)}, f32[4,136,128]{2,1,0:T(8,128)S(1)}, u32[]{:S(2)}, u32[]{:S(2)}) collective-permute-start(f32[4,136,128]{2,1,0:T(8,128)S(1)} %get-tuple-element.103), channel_id=1, source_target_pairs={{0,4},{4,8},{8,12},{1,5},{5,9},{9,13},{2,6},{6,10},{10,14},{3,7},{... | collective-permute-start | bytes 835592 | tf_op jit(solution)/shard_map/ppermute | solution.py:18
  50.0 1.9 %copy-start.6 = (f32[512]{0:T(512)S(1)}, f32[512]{0:T(512)}, u32[]{:S(2)}) copy-start(f32[512]{0:T(512)} %param.21) | copy-start | bytes 6148
  50.0 1.9 %copy-start.18 = (f32[4,128]{1,0:T(4,128)S(1)}, f32[4,128]{1,0:T(4,128)}, u32[]{:S(2)}) copy-start(f32[4,128]{1,0:T(4,128)} %copy-done.17) | copy-start | bytes 6148
  50.0 1.9 %copy-start.20 = (f32[4,128]{1,0:T(4,128)S(1)}, f32[4,128]{1,0:T(4,128)}, u32[]{:S(2)}) copy-start(f32[4,128]{1,0:T(4,128)} %copy-done.19) | copy-start | bytes 6148
  50.5 1.4 %copy-start.12 = (f32[128]{0:T(128)S(1)}, f32[128]{0:T(128)}, u32[]{:S(2)}) copy-start(f32[128]{0:T(128)} %copy-done.11) | copy-start | bytes 1540
  50.6 4.3 %copy-start.10 = (f32[4,128]{1,0:T(4,128)S(1)}, f32[4,128]{1,0:T(4,128)}, u32[]{:S(2)}) copy-start(f32[4,128]{1,0:T(4,128)} %copy-done.9) | copy-start | bytes 6148
  50.6 10.2 %collective-permute-start.3 = (f32[4,136,128]{2,1,0:T(8,128)S(1)}, f32[4,136,128]{2,1,0:T(8,128)S(1)}, u32[]{:S(2)}, u32[]{:S(2)}) collective-permute-start(f32[4,136,128]{2,1,0:T(8,128)S(1)} %get-tuple-element.104), channel_id=1, source_target_pairs={{4,0},{8,4},{12,8},{5,1},{9,5},{13,9},{6,2},{10,6},{14,10},{7,3},{... | collective-permute-start | bytes 835592 | tf_op jit(solution)/shard_map/ppermute | solution.py:18
  55.0 9.2 %collective-permute-start.6 = (f32[4,128,128]{2,1,0:T(8,128)S(1)}, f32[4,128,128]{2,1,0:T(8,128)S(1)}, u32[]{:S(2)}, u32[]{:S(2)}) collective-permute-start(f32[4,128,128]{2,1,0:T(8,128)S(1)} %multiply_add_fusion), channel_id=1, source_target_pairs={{0,8},{4,12},{1,9},{5,13},{2,10},{6,14},{3,11},{7,15},{16,24},{20,... | collective-permute-start | bytes 786440 | tf_op jit(solution)/shard_map/ppermute | solution.py:18
  64.5 0.7 copy-start.26
  64.5 1.2 %collective-permute-start.7 = (f32[1024]{0:T(1024)S(1)}, f32[1024]{0:T(1024)S(1)}, u32[]{:S(2)}, u32[]{:S(2)}) collective-permute-start(f32[1024]{0:T(1024)S(1)} %pad_maximum_fusion.1), channel_id=1, source_target_pairs={{0,1},{1,0},{2,3},{3,2},{4,5},{5,4},{6,7},{7,6},{8,9},{9,8},{10,11... | collective-permute-start | bytes 12296 | tf_op jit(solution)/shard_map/ppermute | solution.py:28
  65.8 12.6 %collective-permute-start.10 = (f32[1024]{0:T(1024)S(1)}, f32[1024]{0:T(1024)S(1)}, u32[]{:S(2)}, u32[]{:S(2)}) collective-permute-start(f32[1024]{0:T(1024)S(1)} %fusion.88), channel_id=1, source_target_pairs={{0,12},{4,0},{8,4},{12,8},{1,13},{5,1},{9,5},{13,9},{2,14},{6,2},{... | collective-permute-start | bytes 12296 | tf_op jit(solution)/shard_map/ppermute | solution.py:39
  75.5 4.5 %collective-permute-start.9 = (f32[1024]{0:T(1024)S(1)}, f32[1024]{0:T(1024)S(1)}, u32[]{:S(2)}, u32[]{:S(2)}) collective-permute-start(f32[1024]{0:T(1024)S(1)} %fusion.88), channel_id=1, source_target_pairs={{0,8},{4,12},{8,0},{12,4},{1,9},{5,13},{9,1},{13,5},{2,10},{6,14},... | collective-permute-start | bytes 12296 | tf_op jit(solution)/shard_map/ppermute | solution.py:39
  75.5 5.4 %collective-permute-start.8 = (f32[1024]{0:T(1024)S(1)}, f32[1024]{0:T(1024)S(1)}, u32[]{:S(2)}, u32[]{:S(2)}) collective-permute-start(f32[1024]{0:T(1024)S(1)} %fusion.88), channel_id=1, source_target_pairs={{0,4},{4,8},{8,12},{12,0},{1,5},{5,9},{9,13},{13,1},{2,6},{6,10},{... | collective-permute-start | bytes 12296 | tf_op jit(solution)/shard_map/ppermute | solution.py:39
  76.9 16.2 %collective-permute-start.4 = (f32[4,128,128]{2,1,0:T(8,128)S(1)}, f32[4,128,128]{2,1,0:T(8,128)S(1)}, u32[]{:S(2)}, u32[]{:S(2)}) collective-permute-start(f32[4,128,128]{2,1,0:T(8,128)S(1)} %get-tuple-element.100), channel_id=1, source_target_pairs={{8,0},{12,4},{9,1},{13,5},{10,2},{14,6},{11,3},{15,7},{24,16},{28,... | collective-permute-start | bytes 786440 | tf_op jit(solution)/shard_map/ppermute | solution.py:18
  93.1 0.7 copy-start.8
  93.3 0.6 copy-start.22
  94.0 0.9 copy-start

commit v7 on v5

--- a/solution.py
+++ b/solution.py
@@ -9,7 +9,7 @@
 
 epsilon = 1.0
 gate_scale = 16.0
-highest = lax.Precision.HIGHEST
+highest = lax.Precision.HIGH
 
 
 def from_behind(value, axis, by):
@@ -37,12 +37,16 @@
     for shift in range(1, length):
         pairs = [(i, (i + shift) % length) for i in range(length)]
         terms.append(lax.ppermute(value, axis, pairs))
-    stacked = jnp.stack(terms)
-    order = (me - jnp.arange(length, dtype=jnp.int32)) % length
-    ordered = jnp.take(stacked, order, axis=0)
-    total = ordered[0]
+    def from_member(member):
+        source_shift = (me - member) % length
+        picked = jnp.zeros_like(value)
+        for shift, term in enumerate(terms):
+            picked = jnp.where(source_shift == shift, term, picked)
+        return picked
+
+    total = from_member(0)
     for member in range(1, length):
-        total = total + ordered[member]
+        total = total + from_member(member)
     return total
 
 

time: 78.8 us -> 78.4 us (level)
  starting transfers between devices: 16.7 us -> 18.5 us
  matrix products: 6.49 us -> 4.8 us
    ppermute x3, starting transfers between devices: 2.02 us -> 3.81 us  [direct_sum(): terms.append(lax.ppermute(value, axis, pairs))]
    ppermute x3, waiting for transfers between devices: 0.81 us -> 0.01 us  [direct_sum(): terms.append(lax.ppermute(value, axis, pairs))]
  transfers between devices with their start and end apart: 9 -> 9, of which waited for: 7 -> 6; matrix products, arithmetic and copies ran while one was open for 9% -> 7% of each run, Pallas kernels for 0% -> 0%
where the time goes in v7:
time: 78.4 us; the launch traced here: 78.1 us
  waiting for transfers between devices  37.2 us (47%)
  starting transfers between devices  18.5 us (24%)
  local copies, waits for them, and re-layouts  8.22 us (10%)
  other arithmetic  6.94 us (9%)
  matrix products  4.8 us (6%)
  between operations  2.47 us (3%)
    ppermute x4, waiting for transfers between devices, from_behind(): return lax.ppermute(value, axis, pairs)  34.5 us
    ppermute x4, starting transfers between devices, from_behind(): return lax.ppermute(value, axis, pairs)  13.1 us
    unnamed x19, local copies, waits for them, and re-layouts  5.84 us
    ppermute x3, starting transfers between devices, direct_sum(): terms.append(lax.ppermute(value, axis, pairs))  3.81 us
    ppermute x2, waiting for transfers between devices, butterfly_sum(): value = value + lax.ppermute(value, axis, pairs)  2.71 us
    ppermute x2, starting transfers between devices, butterfly_sum(): value = value + lax.ppermute(value, axis, pairs)  1.61 us
  transfers between devices with their start and end apart: 9, of which 6 were waited for; matrix products, arithmetic and copies ran while one was open for 7% of the time, Pallas kernels for 0%

profile of v7, /device:TPU:0, one launch (start us, length us, event | category | flops | bytes accessed | tf_op | source)
XLA Modules:
  0.0 78.1 jit_solution(2591309142424971607)
XLA Ops:
  0.6 0.6 copy-done.6
  1.4 0.2 broadcast_in_dim.37
  1.6 0.5 slice.57
  2.9 0.6 compare_convert_fusion.1
  3.6 0.9 %copy-done = bf16[1,128,512]{2,1,0:T(8,128)(2,1)S(1)} copy-done((bf16[1,128,512]{2,1,0:T(8,128)(2,1)S(1)}, bf16[1,128,512]{2,1,0:T(8,128)(2,1)}, u32[]{:S(2)}) %copy-start) | copy-done | bytes 131096
  4.5 0.6 copy-done.5
  5.1 0.3 fusion.16
  5.6 0.8 copy-done.1
  6.5 0.3 multiply_reduce_fusion.2
  6.8 0.3 fusion.43
  7.2 5.1 %collective-permute-start = (f32[4,136,128]{2,1,0:T(8,128)S(1)}, f32[4,136,128]{2,1,0:T(8,128)S(1)}, u32[]{:S(2)}, u32[]{:S(2)}) collective-permute-start(f32[4,136,128]{2,1,0:T(8,128)S(1)} %fusion.9), channel_id=1, source_target_pairs={{0,4},{4,8},{8,12},{1,5},{5,9},{9,13},{2,6},{6,10},{10,14},{3,7},{... | collective-permute-start | bytes 835592 | tf_op jit(solution)/shard_map/ppermute | solution.py:18
  13.2 0.4 fusion.4
  13.6 4.5 %collective-permute-done = f32[4,136,128]{2,1,0:T(8,128)S(1)} collective-permute-done((f32[4,136,128]{2,1,0:T(8,128)S(1)}, f32[4,136,128]{2,1,0:T(8,128)S(1)}, u32[]{:S(2)}, u32[]{:S(2)}) %collective-permute-start) | collective-permute-done | bytes 278560 | tf_op jit(solution)/shard_map/ppermute | solution.py:18
  18.3 5.4 %collective-permute-start.1 = (f32[4,128,128]{2,1,0:T(8,128)S(1)}, f32[4,128,128]{2,1,0:T(8,128)S(1)}, u32[]{:S(2)}, u32[]{:S(2)}) collective-permute-start(f32[4,128,128]{2,1,0:T(8,128)S(1)} %multiply_add_fusion.5), channel_id=1, source_target_pairs={{0,8},{4,12},{1,9},{5,13},{2,10},{6,14},{3,11},{7,15},{16,24},{20,... | collective-permute-start | bytes 786440 | tf_op jit(solution)/shard_map/ppermute | solution.py:18
  23.8 0.2 fusion.39
  24.0 4.4 %collective-permute-done.1 = f32[4,128,128]{2,1,0:T(8,128)S(1)} collective-permute-done((f32[4,128,128]{2,1,0:T(8,128)S(1)}, f32[4,128,128]{2,1,0:T(8,128)S(1)}, u32[]{:S(2)}, u32[]{:S(2)}) %collective-permute-start.1) | collective-permute-done | bytes 262176 | tf_op jit(solution)/shard_map/ppermute | solution.py:18
  28.5 0.4 multiply_reduce_fusion.1
  29.0 0.6 copy-done.4
  29.6 0.2 convolution_bitcast_fusion.2
  29.8 1.5 %collective-permute-start.2 = (f32[128]{0:T(128)S(1)}, f32[128]{0:T(128)S(1)}, u32[]{:S(2)}, u32[]{:S(2)}) collective-permute-start(f32[128]{0:T(128)S(1)} %convolution_bitcast_fusion.2), channel_id=1, source_target_pairs={{0,2},{2,0},{1,3},{3,1},{4,6},{6,4},{5,7},{7,5},{8,10},{10,8},{9,1... | collective-permute-start | bytes 1544 | tf_op jit(solution)/shard_map/ppermute | solution.py:28
  31.3 2.1 %collective-permute-done.2 = f32[128]{0:T(128)S(1)} collective-permute-done((f32[128]{0:T(128)S(1)}, f32[128]{0:T(128)S(1)}, u32[]{:S(2)}, u32[]{:S(2)}) %collective-permute-start.2) | collective-permute-done | bytes 544 | tf_op jit(solution)/shard_map/ppermute | solution.py:28
  33.4 0.5 bitcast_subtract_fusion
  34.1 0.3 fusion.6
  34.3 0.3 fusion.8
  34.7 0.5 fusion.17
  35.2 1.3 %collective-permute-start.3 = (f32[4,136,128]{2,1,0:T(8,128)S(1)}, f32[4,136,128]{2,1,0:T(8,128)S(1)}, u32[]{:S(2)}, u32[]{:S(2)}) collective-permute-start(f32[4,136,128]{2,1,0:T(8,128)S(1)} %fusion.10), channel_id=1, source_target_pairs={{4,0},{8,4},{12,8},{5,1},{9,5},{13,9},{6,2},{10,6},{14,10},{7,3},{... | collective-permute-start | bytes 835592 | tf_op jit(solution)/shard_map/ppermute | solution.py:18
  36.5 0.3 convolution_bitcast_fusion
  36.8 0.4 convolution_bitcast_fusion.1
  37.2 12.7 %collective-permute-done.3 = f32[4,136,128]{2,1,0:T(8,128)S(1)} collective-permute-done((f32[4,136,128]{2,1,0:T(8,128)S(1)}, f32[4,136,128]{2,1,0:T(8,128)S(1)}, u32[]{:S(2)}, u32[]{:S(2)}) %collective-permute-start.3) | collective-permute-done | bytes 278560 | tf_op jit(solution)/shard_map/ppermute | solution.py:18
  50.0 1.3 %collective-permute-start.4 = (f32[4,128,128]{2,1,0:T(8,128)S(1)}, f32[4,128,128]{2,1,0:T(8,128)S(1)}, u32[]{:S(2)}, u32[]{:S(2)}) collective-permute-start(f32[4,128,128]{2,1,0:T(8,128)S(1)} %multiply_add_fusion.3), channel_id=1, source_target_pairs={{8,0},{12,4},{9,1},{13,5},{10,2},{14,6},{11,3},{15,7},{24,16},{28,... | collective-permute-start | bytes 786440 | tf_op jit(solution)/shard_map/ppermute | solution.py:18
  51.3 0.2 fusion.53
  51.5 0.4 fusion.3
  51.9 12.9 %collective-permute-done.4 = f32[4,128,128]{2,1,0:T(8,128)S(1)} collective-permute-done((f32[4,128,128]{2,1,0:T(8,128)S(1)}, f32[4,128,128]{2,1,0:T(8,128)S(1)}, u32[]{:S(2)}, u32[]{:S(2)}) %collective-permute-start.4) | collective-permute-done | bytes 262176 | tf_op jit(solution)/shard_map/ppermute | solution.py:18
  64.8 0.2 multiply_reduce_fusion
  65.1 0.5 fusion.61
  65.6 0.2 copy.140
  65.7 0.1 copy.139
  66.3 1.1 %fusion.63 = f32[128,4,128]{2,1,0:T(4,128)S(1)} fusion(f32[128,4,128]{2,1,0:T(4,128)S(1)} %copy.141), kind=kOutput, calls=%fused_computation.124 | output fusion | flops 8323072 | bytes 524288 | tf_op jit(solution)/shard_map/transpose(jvp(jit(cumsum)))/reduce_window_sum | solution.py:121
  67.6 1.1 %fusion.62 = f32[128,4,128]{2,1,0:T(4,128)S(1)} fusion(f32[128,4,128]{2,1,0:T(4,128)S(1)} %copy.138), kind=kOutput, calls=%fused_computation.123 | output fusion | flops 8323072 | bytes 524288 | tf_op jit(solution)/shard_map/transpose(jvp(jit(cumsum)))/reduce_window_sum | solution.py:97
  68.7 0.6 fusion.49
  69.3 0.5 fusion.5
  69.8 0.7 collective-permute-done.5
  70.6 3.7 %collective-permute-start.6 = (f32[1024]{0:T(1024)S(1)}, f32[1024]{0:T(1024)S(1)}, u32[]{:S(2)}, u32[]{:S(2)}) collective-permute-start(f32[1024]{0:T(1024)S(1)} %fusion.59), channel_id=1, source_target_pairs={{0,12},{4,0},{8,4},{12,8},{1,13},{5,1},{9,5},{13,9},{2,14},{6,2},{... | collective-permute-start | bytes 12296 | tf_op jit(solution)/shard_map/ppermute | solution.py:39
  74.5 0.8 copy.144
  75.3 0.8 copy.143
  76.0 0.8 copy.142
  76.8 0.7 convert_element_type.135
  77.5 0.6 slice_multiply_fusion
  (50 shorter events, 2.4 us)
Async XLA Ops:
  0.6 0.7 copy-start.6
  1.3 2.2 %copy-start.3 = (bf16[1,128,512]{2,1,0:T(8,128)(2,1)S(1)}, bf16[1,128,512]{2,1,0:T(8,128)(2,1)}, u32[]{:S(2)}) copy-start(bf16[1,128,512]{2,1,0:T(8,128)(2,1)} %param.16) | copy-start | bytes 393220
  3.5 0.9 %copy-start = (bf16[1,128,512]{2,1,0:T(8,128)(2,1)S(1)}, bf16[1,128,512]{2,1,0:T(8,128)(2,1)}, u32[]{:S(2)}) copy-start(bf16[1,128,512]{2,1,0:T(8,128)(2,1)} %param.17) | copy-start | bytes 393220
  4.4 0.7 copy-start.5
  5.5 0.9 %copy-start.1 = (bf16[1,128,512]{2,1,0:T(8,128)(2,1)S(1)}, bf16[1,128,512]{2,1,0:T(8,128)(2,1)}, u32[]{:S(2)}) copy-start(bf16[1,128,512]{2,1,0:T(8,128)(2,1)} %param.15) | copy-start | bytes 393220
  7.1 5.9 %copy-start.2 = (bf16[1,128,512]{2,1,0:T(8,128)(2,1)S(1)}, bf16[1,128,512]{2,1,0:T(8,128)(2,1)}, u32[]{:S(2)}) copy-start(bf16[1,128,512]{2,1,0:T(8,128)(2,1)} %param.14) | copy-start | bytes 393220
  7.2 11.0 %collective-permute-start = (f32[4,136,128]{2,1,0:T(8,128)S(1)}, f32[4,136,128]{2,1,0:T(8,128)S(1)}, u32[]{:S(2)}, u32[]{:S(2)}) collective-permute-start(f32[4,136,128]{2,1,0:T(8,128)S(1)} %fusion.9), channel_id=1, source_target_pairs={{0,4},{4,8},{8,12},{1,5},{5,9},{9,13},{2,6},{6,10},{10,14},{3,7},{... | collective-permute-start | bytes 835592 | tf_op jit(solution)/shard_map/ppermute | solution.py:18
  18.3 10.1 %collective-permute-start.1 = (f32[4,128,128]{2,1,0:T(8,128)S(1)}, f32[4,128,128]{2,1,0:T(8,128)S(1)}, u32[]{:S(2)}, u32[]{:S(2)}) collective-permute-start(f32[4,128,128]{2,1,0:T(8,128)S(1)} %multiply_add_fusion.5), channel_id=1, source_target_pairs={{0,8},{4,12},{1,9},{5,13},{2,10},{6,14},{3,11},{7,15},{16,24},{20,... | collective-permute-start | bytes 786440 | tf_op jit(solution)/shard_map/ppermute | solution.py:18
  28.9 0.7 copy-start.4
  29.8 3.6 %collective-permute-start.2 = (f32[128]{0:T(128)S(1)}, f32[128]{0:T(128)S(1)}, u32[]{:S(2)}, u32[]{:S(2)}) collective-permute-start(f32[128]{0:T(128)S(1)} %convolution_bitcast_fusion.2), channel_id=1, source_target_pairs={{0,2},{2,0},{1,3},{3,1},{4,6},{6,4},{5,7},{7,5},{8,10},{10,8},{9,1... | collective-permute-start | bytes 1544 | tf_op jit(solution)/shard_map/ppermute | solution.py:28
  31.3 2.1 %copy-start.7 = (f32[1,128]{1,0:T(1,128)S(1)}, f32[1,128]{1,0:T(1,128)}, u32[]{:S(2)}) copy-start(f32[1,128]{1,0:T(1,128)} %param.20) | copy-start | bytes 1540
  35.2 14.6 %collective-permute-start.3 = (f32[4,136,128]{2,1,0:T(8,128)S(1)}, f32[4,136,128]{2,1,0:T(8,128)S(1)}, u32[]{:S(2)}, u32[]{:S(2)}) collective-permute-start(f32[4,136,128]{2,1,0:T(8,128)S(1)} %fusion.10), channel_id=1, source_target_pairs={{4,0},{8,4},{12,8},{5,1},{9,5},{13,9},{6,2},{10,6},{14,10},{7,3},{... | collective-permute-start | bytes 835592 | tf_op jit(solution)/shard_map/ppermute | solution.py:18
  50.0 14.8 %collective-permute-start.4 = (f32[4,128,128]{2,1,0:T(8,128)S(1)}, f32[4,128,128]{2,1,0:T(8,128)S(1)}, u32[]{:S(2)}, u32[]{:S(2)}) collective-permute-start(f32[4,128,128]{2,1,0:T(8,128)S(1)} %multiply_add_fusion.3), channel_id=1, source_target_pairs={{8,0},{12,4},{9,1},{13,5},{10,2},{14,6},{11,3},{15,7},{24,16},{28,... | collective-permute-start | bytes 786440 | tf_op jit(solution)/shard_map/ppermute | solution.py:18
  69.3 1.2 %collective-permute-start.5 = (f32[1024]{0:T(1024)S(1)}, f32[1024]{0:T(1024)S(1)}, u32[]{:S(2)}, u32[]{:S(2)}) collective-permute-start(f32[1024]{0:T(1024)S(1)} %pad_maximum_fusion), channel_id=1, source_target_pairs={{0,1},{1,0},{2,3},{3,2},{4,5},{5,4},{6,7},{7,6},{8,9},{9,8},{10,11... | collective-permute-start | bytes 12296 | tf_op jit(solution)/shard_map/ppermute | solution.py:28
  70.5 7.0 %collective-permute-start.8 = (f32[1024]{0:T(1024)S(1)}, f32[1024]{0:T(1024)S(1)}, u32[]{:S(2)}, u32[]{:S(2)}) collective-permute-start(f32[1024]{0:T(1024)S(1)} %fusion.59), channel_id=1, source_target_pairs={{0,4},{4,8},{8,12},{12,0},{1,5},{5,9},{9,13},{13,1},{2,6},{6,10},{... | collective-permute-start | bytes 12296 | tf_op jit(solution)/shard_map/ppermute | solution.py:39
  70.5 7.0 %collective-permute-start.7 = (f32[1024]{0:T(1024)S(1)}, f32[1024]{0:T(1024)S(1)}, u32[]{:S(2)}, u32[]{:S(2)}) collective-permute-start(f32[1024]{0:T(1024)S(1)} %fusion.59), channel_id=1, source_target_pairs={{0,8},{4,12},{8,0},{12,4},{1,9},{5,13},{9,1},{13,5},{2,10},{6,14},... | collective-permute-start | bytes 12296 | tf_op jit(solution)/shard_map/ppermute | solution.py:39
  70.6 6.9 %collective-permute-start.6 = (f32[1024]{0:T(1024)S(1)}, f32[1024]{0:T(1024)S(1)}, u32[]{:S(2)}, u32[]{:S(2)}) collective-permute-start(f32[1024]{0:T(1024)S(1)} %fusion.59), channel_id=1, source_target_pairs={{0,12},{4,0},{8,4},{12,8},{1,13},{5,1},{9,5},{13,9},{2,14},{6,2},{... | collective-permute-start | bytes 12296 | tf_op jit(solution)/shard_map/ppermute | solution.py:39

commit v8 on v7

--- a/solution.py
+++ b/solution.py
@@ -121,8 +121,9 @@
     log_cum = jnp.cumsum(log_decay(logit_in, bias_in), axis=0)
     log_last = log_cum[-1]
     segment = segment_ids(start_flags)
-    alive_last = (segment[-1] == 0).astype(jnp.float32)
-    tail_mask = (segment == segment[-1]).astype(jnp.float32)
+    last_segment = jnp.sum(start_flags)
+    alive_last = (last_segment == 0).astype(jnp.float32)
+    tail_mask = (segment == last_segment).astype(jnp.float32)
     key_tail = key_in * jnp.exp(log_last[None] - log_cum) * tail_mask[:, None, None]
     block_state = jnp.einsum("jhc,jhd->hcd", key_tail, value_in, precision=highest)
     block_decay = jnp.exp(log_last) * alive_last
@@ -179,9 +180,11 @@
         return jnp.einsum("thd,hd->t", normed, weight_in, precision=highest)
 
     partial_value, pull_value = jax.vjp(value_head, attended, value_weight.reshape(head_count, DV))
+    unit_attended = pull_value(jnp.ones_like(partial_value))[0]
     value_pred = butterfly_sum(partial_value, "head")
     residual = value_pred - targets[0]
-    grad_attended, grad_weight = pull_value(residual)
+    grad_attended = unit_attended * residual[:, None, None]
+    grad_weight = pull_value(residual)[1]
     grad_carried = jnp.einsum("thd,hcd->thc", grad_attended, state_in, precision=highest)
     grad_direct = jnp.einsum("thc,thd->hcd", carried, grad_attended, precision=highest)
     inner_grads = pull_inner((grad_attended, grad_carried))

time: 78.4 us -> 79 us (level)
  other arithmetic: 6.94 us -> 8.08 us
    reduce_sum x1, other arithmetic: 0.15 us -> 1.3 us  [block_summary(): last_segment = jnp.sum(start_flags)]
where the time goes in v8:
time: 79 us; the launch traced here: 78.6 us
  waiting for transfers between devices  37.2 us (47%)
  starting transfers between devices  18.5 us (23%)
  other arithmetic  8.08 us (10%)
  local copies, waits for them, and re-layouts  7.61 us (10%)
  matrix products  4.81 us (6%)
  between operations  2.46 us (3%)
    ppermute x4, waiting for transfers between devices, from_behind(): return lax.ppermute(value, axis, pairs)  34.5 us
    ppermute x4, starting transfers between devices, from_behind(): return lax.ppermute(value, axis, pairs)  13.1 us
    unnamed x19, local copies, waits for them, and re-layouts  5.74 us
    ppermute x3, starting transfers between devices, direct_sum(): terms.append(lax.ppermute(value, axis, pairs))  3.81 us
    ppermute x2, waiting for transfers between devices, butterfly_sum(): value = value + lax.ppermute(value, axis, pairs)  2.7 us
    ppermute x2, starting transfers between devices, butterfly_sum(): value = value + lax.ppermute(value, axis, pairs)  1.63 us
  transfers between devices with their start and end apart: 9, of which 6 were waited for; matrix products, arithmetic and copies ran while one was open for 7% of the time, Pallas kernels for 0%

profile of v8, /device:TPU:0, one launch (start us, length us, event | category | flops | bytes accessed | tf_op | source)
XLA Modules:
  0.0 78.6 jit_solution(2740662043843609091)
XLA Ops:
  0.6 1.3 %reduce_sum.64 = s32[]{:T(128)} reduce(s32[1,128]{1,0:T(1,128)} %param.22, s32[]{:T(128)} %constant.122.clone.1), dimensions={0,1}, to_apply=%region_2.4 | reduce | flops 127 | bytes 520 | tf_op jit(solution)/shard_map/jvp()/reduce_sum | solution.py:124
  2.6 0.6 copy-done.6
  3.4 0.2 reduce-window.7
  3.6 0.7 compare_convert_fusion.1
  4.4 0.9 %copy-done = bf16[1,128,512]{2,1,0:T(8,128)(2,1)S(1)} copy-done((bf16[1,128,512]{2,1,0:T(8,128)(2,1)S(1)}, bf16[1,128,512]{2,1,0:T(8,128)(2,1)}, u32[]{:S(2)}) %copy-start) | copy-done | bytes 131096
  5.3 0.6 copy-done.5
  5.9 0.3 fusion.16
  6.4 0.8 copy-done.1
  7.3 0.3 multiply_reduce_fusion.3
  7.6 0.3 fusion.45
  7.9 5.1 %collective-permute-start = (f32[4,136,128]{2,1,0:T(8,128)S(1)}, f32[4,136,128]{2,1,0:T(8,128)S(1)}, u32[]{:S(2)}, u32[]{:S(2)}) collective-permute-start(f32[4,136,128]{2,1,0:T(8,128)S(1)} %fusion.9), channel_id=1, source_target_pairs={{0,4},{4,8},{8,12},{1,5},{5,9},{9,13},{2,6},{6,10},{10,14},{3,7},{... | collective-permute-start | bytes 835592 | tf_op jit(solution)/shard_map/ppermute | solution.py:18
  14.0 0.4 fusion.4
  14.4 4.5 %collective-permute-done = f32[4,136,128]{2,1,0:T(8,128)S(1)} collective-permute-done((f32[4,136,128]{2,1,0:T(8,128)S(1)}, f32[4,136,128]{2,1,0:T(8,128)S(1)}, u32[]{:S(2)}, u32[]{:S(2)}) %collective-permute-start) | collective-permute-done | bytes 278560 | tf_op jit(solution)/shard_map/ppermute | solution.py:18
  19.0 5.4 %collective-permute-start.1 = (f32[4,128,128]{2,1,0:T(8,128)S(1)}, f32[4,128,128]{2,1,0:T(8,128)S(1)}, u32[]{:S(2)}, u32[]{:S(2)}) collective-permute-start(f32[4,128,128]{2,1,0:T(8,128)S(1)} %multiply_add_fusion.5), channel_id=1, source_target_pairs={{0,8},{4,12},{1,9},{5,13},{2,10},{6,14},{3,11},{7,15},{16,24},{20,... | collective-permute-start | bytes 786440 | tf_op jit(solution)/shard_map/ppermute | solution.py:18
  24.6 0.2 fusion.41
  24.8 4.3 %collective-permute-done.1 = f32[4,128,128]{2,1,0:T(8,128)S(1)} collective-permute-done((f32[4,128,128]{2,1,0:T(8,128)S(1)}, f32[4,128,128]{2,1,0:T(8,128)S(1)}, u32[]{:S(2)}, u32[]{:S(2)}) %collective-permute-start.1) | collective-permute-done | bytes 262176 | tf_op jit(solution)/shard_map/ppermute | solution.py:18
  29.3 0.5 copy-done.4
  29.8 0.4 multiply_reduce_fusion.1
  30.3 0.2 convolution_bitcast_fusion.2
  30.5 1.6 %collective-permute-start.2 = (f32[128]{0:T(128)S(1)}, f32[128]{0:T(128)S(1)}, u32[]{:S(2)}, u32[]{:S(2)}) collective-permute-start(f32[128]{0:T(128)S(1)} %convolution_bitcast_fusion.2), channel_id=1, source_target_pairs={{0,2},{2,0},{1,3},{3,1},{4,6},{6,4},{5,7},{7,5},{8,10},{10,8},{9,1... | collective-permute-start | bytes 1544 | tf_op jit(solution)/shard_map/ppermute | solution.py:28
  32.0 2.0 %collective-permute-done.2 = f32[128]{0:T(128)S(1)} collective-permute-done((f32[128]{0:T(128)S(1)}, f32[128]{0:T(128)S(1)}, u32[]{:S(2)}, u32[]{:S(2)}) %collective-permute-start.2) | collective-permute-done | bytes 544 | tf_op jit(solution)/shard_map/ppermute | solution.py:28
  34.1 0.5 bitcast_subtract_fusion
  34.6 0.3 fusion.6
  34.9 0.3 fusion.8
  35.2 0.5 fusion.17
  35.7 1.3 %collective-permute-start.3 = (f32[4,136,128]{2,1,0:T(8,128)S(1)}, f32[4,136,128]{2,1,0:T(8,128)S(1)}, u32[]{:S(2)}, u32[]{:S(2)}) collective-permute-start(f32[4,136,128]{2,1,0:T(8,128)S(1)} %fusion.10), channel_id=1, source_target_pairs={{4,0},{8,4},{12,8},{5,1},{9,5},{13,9},{6,2},{10,6},{14,10},{7,3},{... | collective-permute-start | bytes 835592 | tf_op jit(solution)/shard_map/ppermute | solution.py:18
  37.0 0.3 convolution_bitcast_fusion
  37.3 0.4 convolution_bitcast_fusion.1
  37.7 12.7 %collective-permute-done.3 = f32[4,136,128]{2,1,0:T(8,128)S(1)} collective-permute-done((f32[4,136,128]{2,1,0:T(8,128)S(1)}, f32[4,136,128]{2,1,0:T(8,128)S(1)}, u32[]{:S(2)}, u32[]{:S(2)}) %collective-permute-start.3) | collective-permute-done | bytes 278560 | tf_op jit(solution)/shard_map/ppermute | solution.py:18
  50.5 1.3 %collective-permute-start.4 = (f32[4,128,128]{2,1,0:T(8,128)S(1)}, f32[4,128,128]{2,1,0:T(8,128)S(1)}, u32[]{:S(2)}, u32[]{:S(2)}) collective-permute-start(f32[4,128,128]{2,1,0:T(8,128)S(1)} %multiply_add_fusion.3), channel_id=1, source_target_pairs={{8,0},{12,4},{9,1},{13,5},{10,2},{14,6},{11,3},{15,7},{24,16},{28,... | collective-permute-start | bytes 786440 | tf_op jit(solution)/shard_map/ppermute | solution.py:18
  51.8 0.2 fusion.57
  52.0 0.4 fusion.3
  52.4 12.9 %collective-permute-done.4 = f32[4,128,128]{2,1,0:T(8,128)S(1)} collective-permute-done((f32[4,128,128]{2,1,0:T(8,128)S(1)}, f32[4,128,128]{2,1,0:T(8,128)S(1)}, u32[]{:S(2)}, u32[]{:S(2)}) %collective-permute-start.4) | collective-permute-done | bytes 262176 | tf_op jit(solution)/shard_map/ppermute | solution.py:18
  65.3 0.2 multiply_reduce_fusion
  65.6 0.5 fusion.65
  66.1 0.2 copy.140
  66.2 0.1 copy.139
  66.8 1.1 %fusion.67 = f32[128,4,128]{2,1,0:T(4,128)S(1)} fusion(f32[128,4,128]{2,1,0:T(4,128)S(1)} %copy.141), kind=kOutput, calls=%fused_computation.122 | output fusion | flops 8323072 | bytes 524288 | tf_op jit(solution)/shard_map/transpose(jvp(jit(cumsum)))/reduce_window_sum | solution.py:121
  68.1 1.1 %fusion.66 = f32[128,4,128]{2,1,0:T(4,128)S(1)} fusion(f32[128,4,128]{2,1,0:T(4,128)S(1)} %copy.138), kind=kOutput, calls=%fused_computation.121 | output fusion | flops 8323072 | bytes 524288 | tf_op jit(solution)/shard_map/transpose(jvp(jit(cumsum)))/reduce_window_sum | solution.py:97
  69.2 0.6 fusion.51
  69.9 0.5 fusion.5
  70.3 0.7 collective-permute-done.5
  71.1 3.7 %collective-permute-start.6 = (f32[1024]{0:T(1024)S(1)}, f32[1024]{0:T(1024)S(1)}, u32[]{:S(2)}, u32[]{:S(2)}) collective-permute-start(f32[1024]{0:T(1024)S(1)} %fusion.63), channel_id=1, source_target_pairs={{0,12},{4,0},{8,4},{12,8},{1,13},{5,1},{9,5},{13,9},{2,14},{6,2},{... | collective-permute-start | bytes 12296 | tf_op jit(solution)/shard_map/ppermute | solution.py:39
  75.0 0.8 copy.144
  75.8 0.8 copy.143
  76.5 0.8 copy.142
  77.3 0.7 convert_element_type.135
  78.1 0.6 slice_multiply_fusion
  (48 shorter events, 2.2 us)
Async XLA Ops:
  2.6 0.7 copy-start.6
  3.2 1.1 %copy-start.3 = (bf16[1,128,512]{2,1,0:T(8,128)(2,1)S(1)}, bf16[1,128,512]{2,1,0:T(8,128)(2,1)}, u32[]{:S(2)}) copy-start(bf16[1,128,512]{2,1,0:T(8,128)(2,1)} %param.16) | copy-start | bytes 393220
  4.3 0.9 %copy-start = (bf16[1,128,512]{2,1,0:T(8,128)(2,1)S(1)}, bf16[1,128,512]{2,1,0:T(8,128)(2,1)}, u32[]{:S(2)}) copy-start(bf16[1,128,512]{2,1,0:T(8,128)(2,1)} %param.17) | copy-start | bytes 393220
  5.2 0.7 copy-start.5
  6.2 0.9 %copy-start.1 = (bf16[1,128,512]{2,1,0:T(8,128)(2,1)S(1)}, bf16[1,128,512]{2,1,0:T(8,128)(2,1)}, u32[]{:S(2)}) copy-start(bf16[1,128,512]{2,1,0:T(8,128)(2,1)} %param.15) | copy-start | bytes 393220
  7.9 5.9 %copy-start.2 = (bf16[1,128,512]{2,1,0:T(8,128)(2,1)S(1)}, bf16[1,128,512]{2,1,0:T(8,128)(2,1)}, u32[]{:S(2)}) copy-start(bf16[1,128,512]{2,1,0:T(8,128)(2,1)} %param.14) | copy-start | bytes 393220
  7.9 11.0 %collective-permute-start = (f32[4,136,128]{2,1,0:T(8,128)S(1)}, f32[4,136,128]{2,1,0:T(8,128)S(1)}, u32[]{:S(2)}, u32[]{:S(2)}) collective-permute-start(f32[4,136,128]{2,1,0:T(8,128)S(1)} %fusion.9), channel_id=1, source_target_pairs={{0,4},{4,8},{8,12},{1,5},{5,9},{9,13},{2,6},{6,10},{10,14},{3,7},{... | collective-permute-start | bytes 835592 | tf_op jit(solution)/shard_map/ppermute | solution.py:18
  19.0 10.1 %collective-permute-start.1 = (f32[4,128,128]{2,1,0:T(8,128)S(1)}, f32[4,128,128]{2,1,0:T(8,128)S(1)}, u32[]{:S(2)}, u32[]{:S(2)}) collective-permute-start(f32[4,128,128]{2,1,0:T(8,128)S(1)} %multiply_add_fusion.5), channel_id=1, source_target_pairs={{0,8},{4,12},{1,9},{5,13},{2,10},{6,14},{3,11},{7,15},{16,24},{20,... | collective-permute-start | bytes 786440 | tf_op jit(solution)/shard_map/ppermute | solution.py:18
  29.2 0.7 copy-start.4
  30.5 3.6 %copy-start.7 = (f32[1,128]{1,0:T(1,128)S(1)}, f32[1,128]{1,0:T(1,128)}, u32[]{:S(2)}) copy-start(f32[1,128]{1,0:T(1,128)} %param.20) | copy-start | bytes 1540
  30.5 3.6 %collective-permute-start.2 = (f32[128]{0:T(128)S(1)}, f32[128]{0:T(128)S(1)}, u32[]{:S(2)}, u32[]{:S(2)}) collective-permute-start(f32[128]{0:T(128)S(1)} %convolution_bitcast_fusion.2), channel_id=1, source_target_pairs={{0,2},{2,0},{1,3},{3,1},{4,6},{6,4},{5,7},{7,5},{8,10},{10,8},{9,1... | collective-permute-start | bytes 1544 | tf_op jit(solution)/shard_map/ppermute | solution.py:28
  35.7 14.6 %collective-permute-start.3 = (f32[4,136,128]{2,1,0:T(8,128)S(1)}, f32[4,136,128]{2,1,0:T(8,128)S(1)}, u32[]{:S(2)}, u32[]{:S(2)}) collective-permute-start(f32[4,136,128]{2,1,0:T(8,128)S(1)} %fusion.10), channel_id=1, source_target_pairs={{4,0},{8,4},{12,8},{5,1},{9,5},{13,9},{6,2},{10,6},{14,10},{7,3},{... | collective-permute-start | bytes 835592 | tf_op jit(solution)/shard_map/ppermute | solution.py:18
  50.5 14.8 %collective-permute-start.4 = (f32[4,128,128]{2,1,0:T(8,128)S(1)}, f32[4,128,128]{2,1,0:T(8,128)S(1)}, u32[]{:S(2)}, u32[]{:S(2)}) collective-permute-start(f32[4,128,128]{2,1,0:T(8,128)S(1)} %multiply_add_fusion.3), channel_id=1, source_target_pairs={{8,0},{12,4},{9,1},{13,5},{10,2},{14,6},{11,3},{15,7},{24,16},{28,... | collective-permute-start | bytes 786440 | tf_op jit(solution)/shard_map/ppermute | solution.py:18
  69.8 1.2 %collective-permute-start.5 = (f32[1024]{0:T(1024)S(1)}, f32[1024]{0:T(1024)S(1)}, u32[]{:S(2)}, u32[]{:S(2)}) collective-permute-start(f32[1024]{0:T(1024)S(1)} %pad_maximum_fusion), channel_id=1, source_target_pairs={{0,1},{1,0},{2,3},{3,2},{4,5},{5,4},{6,7},{7,6},{8,9},{9,8},{10,11... | collective-permute-start | bytes 12296 | tf_op jit(solution)/shard_map/ppermute | solution.py:28
  71.0 7.0 %collective-permute-start.8 = (f32[1024]{0:T(1024)S(1)}, f32[1024]{0:T(1024)S(1)}, u32[]{:S(2)}, u32[]{:S(2)}) collective-permute-start(f32[1024]{0:T(1024)S(1)} %fusion.63), channel_id=1, source_target_pairs={{0,4},{4,8},{8,12},{12,0},{1,5},{5,9},{9,13},{13,1},{2,6},{6,10},{... | collective-permute-start | bytes 12296 | tf_op jit(solution)/shard_map/ppermute | solution.py:39
  71.0 7.0 %collective-permute-start.7 = (f32[1024]{0:T(1024)S(1)}, f32[1024]{0:T(1024)S(1)}, u32[]{:S(2)}, u32[]{:S(2)}) collective-permute-start(f32[1024]{0:T(1024)S(1)} %fusion.63), channel_id=1, source_target_pairs={{0,8},{4,12},{8,0},{12,4},{1,9},{5,13},{9,1},{13,5},{2,10},{6,14},... | collective-permute-start | bytes 12296 | tf_op jit(solution)/shard_map/ppermute | solution.py:39
  71.1 6.9 %collective-permute-start.6 = (f32[1024]{0:T(1024)S(1)}, f32[1024]{0:T(1024)S(1)}, u32[]{:S(2)}, u32[]{:S(2)}) collective-permute-start(f32[1024]{0:T(1024)S(1)} %fusion.63), channel_id=1, source_target_pairs={{0,12},{4,0},{8,4},{12,8},{1,13},{5,1},{9,5},{13,9},{2,14},{6,2},{... | collective-permute-start | bytes 12296 | tf_op jit(solution)/shard_map/ppermute | solution.py:39

commit v9 on v7

--- a/solution.py
+++ b/solution.py
@@ -129,6 +129,19 @@
     return block_state, block_decay
 
 
+def bias_transfer(key_in, value_in, logit_in, bias_in, start_flags, state_in, block_decay):
+    slope = jax.nn.sigmoid(-(logit_in + bias_in)) / gate_scale
+    log_cum = jnp.cumsum(log_decay(logit_in, bias_in), axis=0)
+    log_last = log_cum[-1]
+    segment = segment_ids(start_flags)
+    tail_mask = (segment == segment[-1]).astype(jnp.float32)
+    key_tail = key_in * jnp.exp(log_last[None] - log_cum) * tail_mask[:, None, None]
+    from_end = jnp.cumsum(slope[::-1], axis=0)[::-1]
+    later = jnp.concatenate([from_end[1:], jnp.zeros_like(from_end[:1])], axis=0)
+    through = jnp.einsum("thc,thd->hcd", key_tail * later, value_in, precision=highest)
+    return through + (block_decay * from_end[0])[..., None] * state_in
+
+
 def on_device(
     queries,
     per_head_keys,
@@ -185,6 +198,7 @@
     grad_carried = jnp.einsum("thd,hcd->thc", grad_attended, state_in, precision=highest)
     grad_direct = jnp.einsum("thc,thd->hcd", carried, grad_attended, precision=highest)
     inner_grads = pull_inner((grad_attended, grad_carried))
+    transfer = bias_transfer(key_f, value_f, logit_f, bias_h, start_flags, state_in, decay_local)
 
     grad_state = gather_scan(grad_direct, decay_local, span_count, -1)
     grad_decay = jnp.sum(state_in * grad_state, axis=-1)
@@ -193,8 +207,8 @@
     grad_query = inner_grads[0]
     grad_key = inner_grads[1] + summary_grads[0]
     grad_value = inner_grads[2] + summary_grads[1]
-    grad_logit = inner_grads[3] + summary_grads[2]
-    grad_bias = inner_grads[4] + summary_grads[3]
+    grad_logit = lax.optimization_barrier(inner_grads[3]) + summary_grads[2]
+    grad_bias = inner_grads[4] + jnp.sum(grad_state * transfer, axis=-1)
     token_total = token_count * lax.axis_size("ctx") * lax.axis_size("rep")
     both_total = direct_sum(
         butterfly_sum(jnp.concatenate([grad_bias.reshape(-1), grad_weight.reshape(-1)]), "rep"),

time: 78.4 us -> 85.1 us (1.085)
  local copies, waits for them, and re-layouts: 8.22 us -> 13.4 us
  waiting for transfers between devices: 37.2 us -> 34.9 us
  other arithmetic: 6.94 us -> 8.85 us
  matrix products: 4.8 us -> 6.44 us
    unnamed x19 -> x53, local copies, waits for them, and re-layouts: 5.84 us -> 9.84 us
    ppermute x4, waiting for transfers between devices: 34.5 us -> 32.7 us  [from_behind(): return lax.ppermute(value, axis, pairs)]
  transfers between devices with their start and end apart: 9 -> 9, of which waited for: 6 -> 6; matrix products, arithmetic and copies ran while one was open for 7% -> 10% of each run, Pallas kernels for 0% -> 0%
where the time goes in v9:
time: 85.1 us; the launch traced here: 84.5 us
  waiting for transfers between devices  34.9 us (41%)
  starting transfers between devices  18.3 us (22%)
  local copies, waits for them, and re-layouts  13.4 us (16%)
  other arithmetic  8.85 us (10%)
  matrix products  6.44 us (8%)
  between operations  2.59 us (3%)
    ppermute x4, waiting for transfers between devices, from_behind(): return lax.ppermute(value, axis, pairs)  32.7 us
    ppermute x4, starting transfers between devices, from_behind(): return lax.ppermute(value, axis, pairs)  12.9 us
    unnamed x53, local copies, waits for them, and re-layouts  9.84 us
    ppermute x3, starting transfers between devices, direct_sum(): terms.append(lax.ppermute(value, axis, pairs))  3.81 us
    ppermute x2, waiting for transfers between devices, butterfly_sum(): value = value + lax.ppermute(value, axis, pairs)  2.24 us
    dot_general x3, matrix products, block_summary(): jnp.einsum('jhc,jhd->hcd', key_tail, value_in, precision=highest)  1.98 us
  transfers between devices with their start and end apart: 9, of which 6 were waited for; matrix products, arithmetic and copies ran while one was open for 10% of the time, Pallas kernels for 0%

profile of v9, /device:TPU:0, one launch (start us, length us, event | category | flops | bytes accessed | tf_op | source)
XLA Modules:
  0.0 84.5 jit_solution(8262078540641883081)
XLA Ops:
  0.6 0.6 copy-done.23
  1.6 0.5 slice.75
  2.9 1.2 %compare_convert_fusion.1 = (f32[128]{0:T(128)}, f32[128]{0:T(128)S(1)}) fusion(s32[128]{0:T(128)S(1)} %reduce.3, s32[]{:T(128)} %bitcast.7), kind=kLoop, calls=%fused_computation.126 | loop fusion | flops 512 | bytes 1540 | tf_op jit(solution)/shard_map/jvp()/convert_element_type | solution.py:99
  4.1 0.9 %copy-done.5 = bf16[1,128,512]{2,1,0:T(8,128)(2,1)S(1)} copy-done((bf16[1,128,512]{2,1,0:T(8,128)(2,1)S(1)}, bf16[1,128,512]{2,1,0:T(8,128)(2,1)}, u32[]{:S(2)}) %copy-start.5) | copy-done | bytes 131096
  5.0 0.6 copy-done.14
  5.6 0.3 fusion.16
  6.1 0.8 copy-done.6
  7.0 0.3 multiply_reduce_fusion.3
  7.9 4.9 %collective-permute-start = (f32[4,136,128]{2,1,0:T(8,128)S(1)}, f32[4,136,128]{2,1,0:T(8,128)S(1)}, u32[]{:S(2)}, u32[]{:S(2)}) collective-permute-start(f32[4,136,128]{2,1,0:T(8,128)S(1)} %fusion.9), channel_id=1, source_target_pairs={{0,4},{4,8},{8,12},{1,5},{5,9},{9,13},{2,6},{6,10},{10,14},{3,7},{... | collective-permute-start | bytes 835592 | tf_op jit(solution)/shard_map/ppermute | solution.py:18
  13.9 0.6 fusion.66
  14.8 0.6 slice_bitcast_fusion.1
  15.4 0.4 fusion.4
  15.8 2.9 %collective-permute-done = f32[4,136,128]{2,1,0:T(8,128)S(1)} collective-permute-done((f32[4,136,128]{2,1,0:T(8,128)S(1)}, f32[4,136,128]{2,1,0:T(8,128)S(1)}, u32[]{:S(2)}, u32[]{:S(2)}) %collective-permute-start) | collective-permute-done | bytes 278560 | tf_op jit(solution)/shard_map/ppermute | solution.py:18
  18.9 5.4 %collective-permute-start.1 = (f32[4,128,128]{2,1,0:T(8,128)S(1)}, f32[4,128,128]{2,1,0:T(8,128)S(1)}, u32[]{:S(2)}, u32[]{:S(2)}) collective-permute-start(f32[4,128,128]{2,1,0:T(8,128)S(1)} %multiply_add_fusion.5), channel_id=1, source_target_pairs={{0,8},{4,12},{1,9},{5,13},{2,10},{6,14},{3,11},{7,15},{16,24},{20,... | collective-permute-start | bytes 786440 | tf_op jit(solution)/shard_map/ppermute | solution.py:18
  24.8 4.2 %collective-permute-done.1 = f32[4,128,128]{2,1,0:T(8,128)S(1)} collective-permute-done((f32[4,128,128]{2,1,0:T(8,128)S(1)}, f32[4,128,128]{2,1,0:T(8,128)S(1)}, u32[]{:S(2)}, u32[]{:S(2)}) %collective-permute-start.1) | collective-permute-done | bytes 262176 | tf_op jit(solution)/shard_map/ppermute | solution.py:18
  29.1 0.4 multiply_reduce_fusion.2
  29.6 0.6 copy-done.9
  30.2 0.7 convolution_bitcast_fusion.2
  31.0 1.5 %collective-permute-start.2 = (f32[128]{0:T(128)}, f32[128]{0:T(128)}, u32[]{:S(2)}, u32[]{:S(2)}) collective-permute-start(f32[128]{0:T(128)} %convolution_bitcast_fusion.2), channel_id=1, source_target_pairs={{0,2},{2,0},{1,3},{3,1},{4,6},{6,4},{5,7},{7,5},{8,10},{10,8},{9,1... | collective-permute-start | bytes 1544 | tf_op jit(solution)/shard_map/ppermute | solution.py:28
  32.7 0.4 slice.72
  33.0 1.5 %collective-permute-done.2 = f32[128]{0:T(128)} collective-permute-done((f32[128]{0:T(128)}, f32[128]{0:T(128)}, u32[]{:S(2)}, u32[]{:S(2)}) %collective-permute-start.2) | collective-permute-done | bytes 544 | tf_op jit(solution)/shard_map/ppermute | solution.py:28
  34.5 1.2 %bitcast_subtract_fusion = (f32[128]{0:T(128)S(1)}, f32[1,128]{1,0:T(1,128)}) fusion(f32[1,128]{1,0:T(1,128)} %param.20, f32[128]{0:T(128)} %convolution_bitcast_fusion.2, f32[128]{0:T(128)} %collective-permute-done.2), kind=kLoop, calls=%fused_computation.131 | loop fusion | flops 256 | bytes 2560 | tf_op jit(solution)/shard_map/sub | solution.py:196
  36.2 0.5 copy-done.4
  36.6 0.3 fusion.8
  37.0 0.5 fusion.30
  37.7 1.3 %collective-permute-start.3 = (f32[4,136,128]{2,1,0:T(8,128)S(1)}, f32[4,136,128]{2,1,0:T(8,128)S(1)}, u32[]{:S(2)}, u32[]{:S(2)}) collective-permute-start(f32[4,136,128]{2,1,0:T(8,128)S(1)} %fusion.10), channel_id=1, source_target_pairs={{4,0},{8,4},{12,8},{5,1},{9,5},{13,9},{6,2},{10,6},{14,10},{7,3},{... | collective-permute-start | bytes 835592 | tf_op jit(solution)/shard_map/ppermute | solution.py:18
  39.2 0.4 convolution_bitcast_fusion.1
  39.6 13.0 %collective-permute-done.3 = f32[4,136,128]{2,1,0:T(8,128)S(1)} collective-permute-done((f32[4,136,128]{2,1,0:T(8,128)S(1)}, f32[4,136,128]{2,1,0:T(8,128)S(1)}, u32[]{:S(2)}, u32[]{:S(2)}) %collective-permute-start.3) | collective-permute-done | bytes 278560 | tf_op jit(solution)/shard_map/ppermute | solution.py:18
  52.7 1.3 %collective-permute-start.4 = (f32[4,128,128]{2,1,0:T(8,128)S(1)}, f32[4,128,128]{2,1,0:T(8,128)S(1)}, u32[]{:S(2)}, u32[]{:S(2)}) collective-permute-start(f32[4,128,128]{2,1,0:T(8,128)S(1)} %multiply_add_fusion.3), channel_id=1, source_target_pairs={{8,0},{12,4},{9,1},{13,5},{10,2},{14,6},{11,3},{15,7},{24,16},{28,... | collective-permute-start | bytes 786440 | tf_op jit(solution)/shard_map/ppermute | solution.py:18
  54.3 0.7 copy-done.22
  54.9 0.4 fusion.3
  55.3 12.6 %collective-permute-done.4 = f32[4,128,128]{2,1,0:T(8,128)S(1)} collective-permute-done((f32[4,128,128]{2,1,0:T(8,128)S(1)}, f32[4,128,128]{2,1,0:T(8,128)S(1)}, u32[]{:S(2)}, u32[]{:S(2)}) %collective-permute-start.4) | collective-permute-done | bytes 262176 | tf_op jit(solution)/shard_map/ppermute | solution.py:18
  68.2 0.4 copy-done.11
  68.8 0.5 fusion.5
  69.3 1.2 %fusion.80 = (f32[4,128]{1,0:T(4,128)S(1)}, f32[128,4,128]{0,2,1:T(8,128)S(1)}, bf16[128,4,128]{0,2,1:T(8,128)(2,1)}, f32[128,4,128]{0,2,1:T(8,128)}, bf16[128,4,128]{0,2,1:T(8,128)(2,1)}) fusion(f32[128,4,128]{0,2,1:T(8,128)S(1)} %copy.135, f32[4,128]{1,0:T(4,128)S(1)} %copy-done.11, f32[128,4,128]{0,2,1:T(8,128)S(1)} %bitcast.111, ...), kind=kOutput, calls=%fused_computation.141 | convolution fusion | flops 51510784 | bytes 2494976 | tf_op jit(solution)/shard_map/transpose(jvp(jhc,jhd->hcd))/dot_general | solution.py:127
  70.8 0.6 copy-done
  71.6 1.1 %fusion.81 = f32[128,4,128]{2,1,0:T(4,128)S(1)} fusion(f32[128,4,128]{2,1,0:T(4,128)S(1)} %copy.154), kind=kOutput, calls=%fused_computation.142 | output fusion | flops 8323072 | bytes 524288 | tf_op jit(solution)/shard_map/transpose(jvp(jit(cumsum)))/reduce_window_sum | solution.py:97
  72.7 0.5 fusion.64
  73.3 0.6 copy-done.20
  73.9 0.4 multiply_reduce_fusion
  74.9 0.7 collective-permute-done.5
  75.7 3.7 %collective-permute-start.6 = (f32[1024]{0:T(1024)S(1)}, f32[1024]{0:T(1024)S(1)}, u32[]{:S(2)}, u32[]{:S(2)}) collective-permute-start(f32[1024]{0:T(1024)S(1)} %fusion.78), channel_id=1, source_target_pairs={{0,12},{4,0},{8,4},{12,8},{1,13},{5,1},{9,5},{13,9},{2,14},{6,2},{... | collective-permute-start | bytes 12296 | tf_op jit(solution)/shard_map/ppermute | solution.py:39
  79.4 1.2 %add_convert_fusion = bf16[128,4,128]{2,1,0:T(4,128)(2,1)S(1)} fusion(f32[128,4,128]{2,1,0:T(4,128)S(1)} %fusion.65, f32[128,4,128]{2,1,0:T(4,128)S(1)} %get-tuple-element.69, f32[128,4,128]{2,1,0:T(4,128)S(1)} %copy.157), kind=kOutput, calls=%fused_computation.51 | output fusion | flops 8716288 | bytes 917504 | tf_op jit(solution)/shard_map/transpose(jvp(jit(cumsum)))/reduce_window_sum | solution.py:121
  80.6 0.8 copy.165
  81.5 0.8 copy.164
  82.4 0.8 copy.163
  83.2 0.7 convert_element_type.136
  83.9 0.6 slice_multiply_fusion
  (92 shorter events, 5.9 us)
Async XLA Ops:
  0.6 0.7 copy-start.23
  1.3 2.7 %copy-start.8 = (bf16[1,128,512]{2,1,0:T(8,128)(2,1)S(1)}, bf16[1,128,512]{2,1,0:T(8,128)(2,1)}, u32[]{:S(2)}) copy-start(bf16[1,128,512]{2,1,0:T(8,128)(2,1)} %param.16) | copy-start | bytes 393220
  4.0 3.3 %copy-start.18 = (f32[128]{0:T(128)}, f32[128]{0:T(128)S(1)}, u32[]{:S(2)}) copy-start(f32[128]{0:T(128)S(1)} %get-tuple-element.88) | copy-start | bytes 1540
  4.0 0.9 %copy-start.5 = (bf16[1,128,512]{2,1,0:T(8,128)(2,1)S(1)}, bf16[1,128,512]{2,1,0:T(8,128)(2,1)}, u32[]{:S(2)}) copy-start(bf16[1,128,512]{2,1,0:T(8,128)(2,1)} %param.17) | copy-start | bytes 393220
  4.9 0.7 copy-start.14
  6.0 0.9 %copy-start.6 = (bf16[1,128,512]{2,1,0:T(8,128)(2,1)S(1)}, bf16[1,128,512]{2,1,0:T(8,128)(2,1)}, u32[]{:S(2)}) copy-start(bf16[1,128,512]{2,1,0:T(8,128)(2,1)} %param.15) | copy-start | bytes 393220
  7.3 0.6 copy-start.12
  7.3 6.6 %copy-start.10 = (f32[4,128]{1,0:T(4,128)}, f32[4,128]{1,0:T(4,128)S(1)}, u32[]{:S(2)}) copy-start(f32[4,128]{1,0:T(4,128)S(1)} %get-tuple-element.67) | copy-start | bytes 6148
  7.9 10.8 %collective-permute-start = (f32[4,136,128]{2,1,0:T(8,128)S(1)}, f32[4,136,128]{2,1,0:T(8,128)S(1)}, u32[]{:S(2)}, u32[]{:S(2)}) collective-permute-start(f32[4,136,128]{2,1,0:T(8,128)S(1)} %fusion.9), channel_id=1, source_target_pairs={{0,4},{4,8},{8,12},{1,5},{5,9},{9,13},{2,6},{6,10},{10,14},{3,7},{... | collective-permute-start | bytes 835592 | tf_op jit(solution)/shard_map/ppermute | solution.py:18
  13.6 1.8 %copy-start.3 = (pred[128,128]{1,0:T(8,128)(4,1)}, pred[128,128]{1,0:T(8,128)(4,1)S(1)}, u32[]{:S(2)}) copy-start(pred[128,128]{1,0:T(8,128)(4,1)S(1)} %fusion.63) | copy-start | bytes 49156
  13.8 0.9 %copy-start.7 = (bf16[1,128,512]{2,1,0:T(8,128)(2,1)S(1)}, bf16[1,128,512]{2,1,0:T(8,128)(2,1)}, u32[]{:S(2)}) copy-start(bf16[1,128,512]{2,1,0:T(8,128)(2,1)} %param.14) | copy-start | bytes 393220
  14.7 4.1 %copy-start.16 = (f32[4,128]{1,0:T(4,128)}, f32[4,128]{1,0:T(4,128)S(1)}, u32[]{:S(2)}) copy-start(f32[4,128]{1,0:T(4,128)S(1)} %get-tuple-element.71) | copy-start | bytes 6148
  18.9 10.1 %collective-permute-start.1 = (f32[4,128,128]{2,1,0:T(8,128)S(1)}, f32[4,128,128]{2,1,0:T(8,128)S(1)}, u32[]{:S(2)}, u32[]{:S(2)}) collective-permute-start(f32[4,128,128]{2,1,0:T(8,128)S(1)} %multiply_add_fusion.5), channel_id=1, source_target_pairs={{0,8},{4,12},{1,9},{5,13},{2,10},{6,14},{3,11},{7,15},{16,24},{20,... | collective-permute-start | bytes 786440 | tf_op jit(solution)/shard_map/ppermute | solution.py:18
  29.6 0.7 copy-start.9
  31.0 3.6 %collective-permute-start.2 = (f32[128]{0:T(128)}, f32[128]{0:T(128)}, u32[]{:S(2)}, u32[]{:S(2)}) collective-permute-start(f32[128]{0:T(128)} %convolution_bitcast_fusion.2), channel_id=1, source_target_pairs={{0,2},{2,0},{1,3},{3,1},{4,6},{6,4},{5,7},{7,5},{8,10},{10,8},{9,1... | collective-permute-start | bytes 1544 | tf_op jit(solution)/shard_map/ppermute | solution.py:28
  35.9 0.7 copy-start.4
  37.0 0.7 copy-start.13
  37.7 14.9 %collective-permute-start.3 = (f32[4,136,128]{2,1,0:T(8,128)S(1)}, f32[4,136,128]{2,1,0:T(8,128)S(1)}, u32[]{:S(2)}, u32[]{:S(2)}) collective-permute-start(f32[4,136,128]{2,1,0:T(8,128)S(1)} %fusion.10), channel_id=1, source_target_pairs={{4,0},{8,4},{12,8},{5,1},{9,5},{13,9},{6,2},{10,6},{14,10},{7,3},{... | collective-permute-start | bytes 835592 | tf_op jit(solution)/shard_map/ppermute | solution.py:18
  39.2 13.4 %copy-start.17 = (f32[4,128]{1,0:T(4,128)S(1)}, f32[4,128]{1,0:T(4,128)}, u32[]{:S(2)}) copy-start(f32[4,128]{1,0:T(4,128)} %copy-done.16) | copy-start | bytes 6148
  52.7 15.2 %collective-permute-start.4 = (f32[4,128,128]{2,1,0:T(8,128)S(1)}, f32[4,128,128]{2,1,0:T(8,128)S(1)}, u32[]{:S(2)}, u32[]{:S(2)}) collective-permute-start(f32[4,128,128]{2,1,0:T(8,128)S(1)} %multiply_add_fusion.3), channel_id=1, source_target_pairs={{8,0},{12,4},{9,1},{13,5},{10,2},{14,6},{11,3},{15,7},{24,16},{28,... | collective-permute-start | bytes 786440 | tf_op jit(solution)/shard_map/ppermute | solution.py:18
  54.3 0.7 copy-start.22
  67.9 0.7 copy-start.11
  68.2 0.6 copy-start.19
  70.5 0.9 %copy-start = (f32[128,4,128]{0,2,1:T(8,128)S(1)}, f32[128,4,128]{0,2,1:T(8,128)}, u32[]{:S(2)}) copy-start(f32[128,4,128]{0,2,1:T(8,128)} %get-tuple-element.79) | copy-start | bytes 786436
  71.6 1.1 %copy-start.15 = (f32[512]{0:T(512)S(1)}, f32[512]{0:T(512)}, u32[]{:S(2)}) copy-start(f32[512]{0:T(512)} %param.18) | copy-start | bytes 6148
  73.2 0.7 copy-start.20
  73.2 0.7 copy-start.21
  74.4 1.2 %collective-permute-start.5 = (f32[1024]{0:T(1024)S(1)}, f32[1024]{0:T(1024)S(1)}, u32[]{:S(2)}, u32[]{:S(2)}) collective-permute-start(f32[1024]{0:T(1024)S(1)} %pad_maximum_fusion), channel_id=1, source_target_pairs={{0,1},{1,0},{2,3},{3,2},{4,5},{5,4},{6,7},{7,6},{8,9},{9,8},{10,11... | collective-permute-start | bytes 12296 | tf_op jit(solution)/shard_map/ppermute | solution.py:28
  75.6 8.3 %collective-permute-start.8 = (f32[1024]{0:T(1024)S(1)}, f32[1024]{0:T(1024)S(1)}, u32[]{:S(2)}, u32[]{:S(2)}) collective-permute-start(f32[1024]{0:T(1024)S(1)} %fusion.78), channel_id=1, source_target_pairs={{0,4},{4,8},{8,12},{12,0},{1,5},{5,9},{9,13},{13,1},{2,6},{6,10},{... | collective-permute-start | bytes 12296 | tf_op jit(solution)/shard_map/ppermute | solution.py:39
  75.6 8.3 %collective-permute-start.7 = (f32[1024]{0:T(1024)S(1)}, f32[1024]{0:T(1024)S(1)}, u32[]{:S(2)}, u32[]{:S(2)}) collective-permute-start(f32[1024]{0:T(1024)S(1)} %fusion.78), channel_id=1, source_target_pairs={{0,8},{4,12},{8,0},{12,4},{1,9},{5,13},{9,1},{13,5},{2,10},{6,14},... | collective-permute-start | bytes 12296 | tf_op jit(solution)/shard_map/ppermute | solution.py:39
  75.7 8.2 %collective-permute-start.6 = (f32[1024]{0:T(1024)S(1)}, f32[1024]{0:T(1024)S(1)}, u32[]{:S(2)}, u32[]{:S(2)}) collective-permute-start(f32[1024]{0:T(1024)S(1)} %fusion.78), channel_id=1, source_target_pairs={{0,12},{4,0},{8,4},{12,8},{1,13},{5,1},{9,5},{13,9},{2,14},{6,2},{... | collective-permute-start | bytes 12296 | tf_op jit(solution)/shard_map/ppermute | solution.py:39
  80.6 0.9 %copy-start.2 = (bf16[128,4,128]{0,2,1:T(8,128)(2,1)S(1)}, bf16[128,4,128]{0,2,1:T(8,128)(2,1)}, u32[]{:S(2)}) copy-start(bf16[128,4,128]{0,2,1:T(8,128)(2,1)} %get-tuple-element.78) | copy-start | bytes 393220
  81.5 0.9 %copy-start.1 = (bf16[128,4,128]{0,2,1:T(8,128)(2,1)S(1)}, bf16[128,4,128]{0,2,1:T(8,128)(2,1)}, u32[]{:S(2)}) copy-start(bf16[128,4,128]{0,2,1:T(8,128)(2,1)} %get-tuple-element.80) | copy-start | bytes 393220

commit v10 on v7

--- a/solution.py
+++ b/solution.py
@@ -149,10 +149,13 @@
 
     start_flags = segment_starts[0]
     kind_id = mask_ids[0, 0]
-    query_f = to_heads(queries)
-    key_f = to_heads(per_head_keys)
-    value_f = to_heads(value_rows)
-    logit_f = to_heads(gate_logits)
+    rows_in = lax.optimization_barrier(
+        jnp.concatenate([queries, per_head_keys, value_rows, gate_logits], axis=0)
+    )
+    query_f = to_heads(rows_in[0:1])
+    key_f = to_heads(rows_in[1:2])
+    value_f = to_heads(rows_in[2:3])
+    logit_f = to_heads(rows_in[3:4])
     bias_h = gate_bias.reshape(head_count, DK)
 
     def inner_terms(query_in, key_in, value_in, logit_in, bias_in):

time: 78.4 us -> 77.9 us (level)
  local copies, waits for them, and re-layouts: 8.22 us -> 6.72 us
  other arithmetic: 6.94 us -> 8.05 us
    unnamed x19 -> x15, local copies, waits for them, and re-layouts: 5.84 us -> 4.2 us
    concatenate x0 -> x1, other arithmetic: none -> 1.04 us  [on_device(): jnp.concatenate([queries, per_head_keys, value_rows, gate_logits], axis=0)]
where the time goes in v10:
time: 77.9 us; the launch traced here: 77.6 us
  waiting for transfers between devices  37.2 us (48%)
  starting transfers between devices  18.4 us (24%)
  other arithmetic  8.05 us (10%)
  local copies, waits for them, and re-layouts  6.72 us (9%)
  matrix products  4.74 us (6%)
  between operations  2.47 us (3%)
    ppermute x4, waiting for transfers between devices, from_behind(): return lax.ppermute(value, axis, pairs)  34.5 us
    ppermute x4, starting transfers between devices, from_behind(): return lax.ppermute(value, axis, pairs)  12.9 us
    unnamed x15, local copies, waits for them, and re-layouts  4.2 us
    ppermute x3, starting transfers between devices, direct_sum(): terms.append(lax.ppermute(value, axis, pairs))  3.81 us
    ppermute x2, waiting for transfers between devices, butterfly_sum(): value = value + lax.ppermute(value, axis, pairs)  2.71 us
    ppermute x2, starting transfers between devices, butterfly_sum(): value = value + lax.ppermute(value, axis, pairs)  1.62 us
  transfers between devices with their start and end apart: 9, of which 6 were waited for; matrix products, arithmetic and copies ran while one was open for 7% of the time, Pallas kernels for 0%

profile of v10, /device:TPU:0, one launch (start us, length us, event | category | flops | bytes accessed | tf_op | source)
XLA Modules:
  0.0 77.6 jit_solution(3806363827890430530)
XLA Ops:
  0.6 0.6 copy-done.4
  1.4 0.2 broadcast_in_dim.37
  1.6 0.5 slice.77
  2.9 0.6 compare_convert_fusion.1
  3.5 1.0 %pad_maximum_fusion = bf16[4,128,512]{2,1,0:T(8,128)(2,1)S(1)} fusion(bf16[1,128,512]{2,1,0:T(8,128)(2,1)S(1)} %copy-done, bf16[1,128,512]{2,1,0:T(8,128)(2,1)S(1)} %copy-done.1, bf16[1,128,512]{2,1,0:T(8,128)(2,1)} %param.15, bf16[1,128,512]{2,1,0:T(8,128)(2,1)} %param.14), kind=kLoop, calls=%fused_computation.22 | loop fusion | flops 786432 | bytes 1048576 | tf_op jit(solution)/shard_map/concatenate | solution.py:153
  5.0 0.6 copy-done.3
  5.6 0.3 fusion.16
  6.1 0.3 multiply_reduce_fusion.1
  6.4 0.3 fusion.46
  6.8 4.9 %collective-permute-start = (f32[4,136,128]{2,1,0:T(8,128)S(1)}, f32[4,136,128]{2,1,0:T(8,128)S(1)}, u32[]{:S(2)}, u32[]{:S(2)}) collective-permute-start(f32[4,136,128]{2,1,0:T(8,128)S(1)} %fusion.9), channel_id=1, source_target_pairs={{0,4},{4,8},{8,12},{1,5},{5,9},{9,13},{2,6},{6,10},{10,14},{3,7},{... | collective-permute-start | bytes 835592 | tf_op jit(solution)/shard_map/ppermute | solution.py:18
  12.7 0.4 fusion.4
  13.1 4.5 %collective-permute-done = f32[4,136,128]{2,1,0:T(8,128)S(1)} collective-permute-done((f32[4,136,128]{2,1,0:T(8,128)S(1)}, f32[4,136,128]{2,1,0:T(8,128)S(1)}, u32[]{:S(2)}, u32[]{:S(2)}) %collective-permute-start) | collective-permute-done | bytes 278560 | tf_op jit(solution)/shard_map/ppermute | solution.py:18
  17.8 5.4 %collective-permute-start.1 = (f32[4,128,128]{2,1,0:T(8,128)S(1)}, f32[4,128,128]{2,1,0:T(8,128)S(1)}, u32[]{:S(2)}, u32[]{:S(2)}) collective-permute-start(f32[4,128,128]{2,1,0:T(8,128)S(1)} %multiply_add_fusion.5), channel_id=1, source_target_pairs={{0,8},{4,12},{1,9},{5,13},{2,10},{6,14},{3,11},{7,15},{16,24},{20,... | collective-permute-start | bytes 786440 | tf_op jit(solution)/shard_map/ppermute | solution.py:18
  23.3 0.2 fusion.66
  23.5 4.4 %collective-permute-done.1 = f32[4,128,128]{2,1,0:T(8,128)S(1)} collective-permute-done((f32[4,128,128]{2,1,0:T(8,128)S(1)}, f32[4,128,128]{2,1,0:T(8,128)S(1)}, u32[]{:S(2)}, u32[]{:S(2)}) %collective-permute-start.1) | collective-permute-done | bytes 262176 | tf_op jit(solution)/shard_map/ppermute | solution.py:18
  28.0 0.4 fusion.15
  28.5 0.6 copy-done.2
  29.1 0.2 convolution_bitcast_fusion.2
  29.3 1.5 %collective-permute-start.2 = (f32[128]{0:T(128)S(1)}, f32[128]{0:T(128)S(1)}, u32[]{:S(2)}, u32[]{:S(2)}) collective-permute-start(f32[128]{0:T(128)S(1)} %convolution_bitcast_fusion.2), channel_id=1, source_target_pairs={{0,2},{2,0},{1,3},{3,1},{4,6},{6,4},{5,7},{7,5},{8,10},{10,8},{9,1... | collective-permute-start | bytes 1544 | tf_op jit(solution)/shard_map/ppermute | solution.py:28
  30.8 2.0 %collective-permute-done.2 = f32[128]{0:T(128)S(1)} collective-permute-done((f32[128]{0:T(128)S(1)}, f32[128]{0:T(128)S(1)}, u32[]{:S(2)}, u32[]{:S(2)}) %collective-permute-start.2) | collective-permute-done | bytes 544 | tf_op jit(solution)/shard_map/ppermute | solution.py:28
  32.9 0.5 bitcast_subtract_fusion
  33.6 0.5 fusion.17
  34.1 0.3 fusion.8
  34.4 0.3 convolution_bitcast_fusion
  34.7 1.3 %collective-permute-start.3 = (f32[4,136,128]{2,1,0:T(8,128)S(1)}, f32[4,136,128]{2,1,0:T(8,128)S(1)}, u32[]{:S(2)}, u32[]{:S(2)}) collective-permute-start(f32[4,136,128]{2,1,0:T(8,128)S(1)} %fusion.10), channel_id=1, source_target_pairs={{4,0},{8,4},{12,8},{5,1},{9,5},{13,9},{6,2},{10,6},{14,10},{7,3},{... | collective-permute-start | bytes 835592 | tf_op jit(solution)/shard_map/ppermute | solution.py:18
  36.0 0.3 fusion.6
  36.2 0.4 convolution_bitcast_fusion.1
  36.6 12.7 %collective-permute-done.3 = f32[4,136,128]{2,1,0:T(8,128)S(1)} collective-permute-done((f32[4,136,128]{2,1,0:T(8,128)S(1)}, f32[4,136,128]{2,1,0:T(8,128)S(1)}, u32[]{:S(2)}, u32[]{:S(2)}) %collective-permute-start.3) | collective-permute-done | bytes 278560 | tf_op jit(solution)/shard_map/ppermute | solution.py:18
  49.5 1.3 %collective-permute-start.4 = (f32[4,128,128]{2,1,0:T(8,128)S(1)}, f32[4,128,128]{2,1,0:T(8,128)S(1)}, u32[]{:S(2)}, u32[]{:S(2)}) collective-permute-start(f32[4,128,128]{2,1,0:T(8,128)S(1)} %multiply_add_fusion.3), channel_id=1, source_target_pairs={{8,0},{12,4},{9,1},{13,5},{10,2},{14,6},{11,3},{15,7},{24,16},{28,... | collective-permute-start | bytes 786440 | tf_op jit(solution)/shard_map/ppermute | solution.py:18
  50.8 0.2 fusion.55
  51.0 0.4 fusion.3
  51.4 12.9 %collective-permute-done.4 = f32[4,128,128]{2,1,0:T(8,128)S(1)} collective-permute-done((f32[4,128,128]{2,1,0:T(8,128)S(1)}, f32[4,128,128]{2,1,0:T(8,128)S(1)}, u32[]{:S(2)}, u32[]{:S(2)}) %collective-permute-start.4) | collective-permute-done | bytes 262176 | tf_op jit(solution)/shard_map/ppermute | solution.py:18
  64.3 0.2 multiply_reduce_fusion
  64.6 0.5 fusion.63
  65.0 0.1 copy.140
  65.2 0.1 copy.139
  65.3 0.1 multiply_add_fusion
  65.8 1.1 %fusion.65 = f32[128,4,128]{2,1,0:T(4,128)S(1)} fusion(f32[128,4,128]{2,1,0:T(4,128)S(1)} %copy.141), kind=kOutput, calls=%fused_computation.130 | output fusion | flops 8323072 | bytes 524288 | tf_op jit(solution)/shard_map/transpose(jvp(jit(cumsum)))/reduce_window_sum | solution.py:121
  67.0 1.1 %fusion.64 = f32[128,4,128]{2,1,0:T(4,128)S(1)} fusion(f32[128,4,128]{2,1,0:T(4,128)S(1)} %copy.138), kind=kOutput, calls=%fused_computation.129 | output fusion | flops 8323072 | bytes 524288 | tf_op jit(solution)/shard_map/transpose(jvp(jit(cumsum)))/reduce_window_sum | solution.py:97
  68.1 0.6 fusion.51
  68.8 0.5 fusion.5
  69.3 0.7 collective-permute-done.5
  70.0 3.7 %collective-permute-start.6 = (f32[1024]{0:T(1024)S(1)}, f32[1024]{0:T(1024)S(1)}, u32[]{:S(2)}, u32[]{:S(2)}) collective-permute-start(f32[1024]{0:T(1024)S(1)} %fusion.61), channel_id=1, source_target_pairs={{0,12},{4,0},{8,4},{12,8},{1,13},{5,1},{9,5},{13,9},{2,14},{6,2},{... | collective-permute-start | bytes 12296 | tf_op jit(solution)/shard_map/ppermute | solution.py:39
  73.9 0.8 copy.144
  74.7 0.8 copy.143
  75.5 0.8 copy.142
  76.3 0.7 convert_element_type.135
  77.0 0.6 slice_multiply_fusion
  (48 shorter events, 2.5 us)
Async XLA Ops:
  0.6 0.7 copy-start.4
  1.3 2.2 %copy-start = (bf16[1,128,512]{2,1,0:T(8,128)(2,1)S(1)}, bf16[1,128,512]{2,1,0:T(8,128)(2,1)}, u32[]{:S(2)}) copy-start(bf16[1,128,512]{2,1,0:T(8,128)(2,1)} %param.17) | copy-start | bytes 393220
  1.3 2.2 %copy-start.1 = (bf16[1,128,512]{2,1,0:T(8,128)(2,1)S(1)}, bf16[1,128,512]{2,1,0:T(8,128)(2,1)}, u32[]{:S(2)}) copy-start(bf16[1,128,512]{2,1,0:T(8,128)(2,1)} %param.16) | copy-start | bytes 393220
  4.9 0.7 copy-start.3
  6.8 10.8 %collective-permute-start = (f32[4,136,128]{2,1,0:T(8,128)S(1)}, f32[4,136,128]{2,1,0:T(8,128)S(1)}, u32[]{:S(2)}, u32[]{:S(2)}) collective-permute-start(f32[4,136,128]{2,1,0:T(8,128)S(1)} %fusion.9), channel_id=1, source_target_pairs={{0,4},{4,8},{8,12},{1,5},{5,9},{9,13},{2,6},{6,10},{10,14},{3,7},{... | collective-permute-start | bytes 835592 | tf_op jit(solution)/shard_map/ppermute | solution.py:18
  17.8 10.1 %collective-permute-start.1 = (f32[4,128,128]{2,1,0:T(8,128)S(1)}, f32[4,128,128]{2,1,0:T(8,128)S(1)}, u32[]{:S(2)}, u32[]{:S(2)}) collective-permute-start(f32[4,128,128]{2,1,0:T(8,128)S(1)} %multiply_add_fusion.5), channel_id=1, source_target_pairs={{0,8},{4,12},{1,9},{5,13},{2,10},{6,14},{3,11},{7,15},{16,24},{20,... | collective-permute-start | bytes 786440 | tf_op jit(solution)/shard_map/ppermute | solution.py:18
  28.4 0.7 copy-start.2
  29.3 3.6 %collective-permute-start.2 = (f32[128]{0:T(128)S(1)}, f32[128]{0:T(128)S(1)}, u32[]{:S(2)}, u32[]{:S(2)}) collective-permute-start(f32[128]{0:T(128)S(1)} %convolution_bitcast_fusion.2), channel_id=1, source_target_pairs={{0,2},{2,0},{1,3},{3,1},{4,6},{6,4},{5,7},{7,5},{8,10},{10,8},{9,1... | collective-permute-start | bytes 1544 | tf_op jit(solution)/shard_map/ppermute | solution.py:28
  30.8 2.1 %copy-start.5 = (f32[1,128]{1,0:T(1,128)S(1)}, f32[1,128]{1,0:T(1,128)}, u32[]{:S(2)}) copy-start(f32[1,128]{1,0:T(1,128)} %param.20) | copy-start | bytes 1540
  34.7 14.6 %collective-permute-start.3 = (f32[4,136,128]{2,1,0:T(8,128)S(1)}, f32[4,136,128]{2,1,0:T(8,128)S(1)}, u32[]{:S(2)}, u32[]{:S(2)}) collective-permute-start(f32[4,136,128]{2,1,0:T(8,128)S(1)} %fusion.10), channel_id=1, source_target_pairs={{4,0},{8,4},{12,8},{5,1},{9,5},{13,9},{6,2},{10,6},{14,10},{7,3},{... | collective-permute-start | bytes 835592 | tf_op jit(solution)/shard_map/ppermute | solution.py:18
  49.5 14.8 %collective-permute-start.4 = (f32[4,128,128]{2,1,0:T(8,128)S(1)}, f32[4,128,128]{2,1,0:T(8,128)S(1)}, u32[]{:S(2)}, u32[]{:S(2)}) collective-permute-start(f32[4,128,128]{2,1,0:T(8,128)S(1)} %multiply_add_fusion.3), channel_id=1, source_target_pairs={{8,0},{12,4},{9,1},{13,5},{10,2},{14,6},{11,3},{15,7},{24,16},{28,... | collective-permute-start | bytes 786440 | tf_op jit(solution)/shard_map/ppermute | solution.py:18
  68.7 1.2 %collective-permute-start.5 = (f32[1024]{0:T(1024)S(1)}, f32[1024]{0:T(1024)S(1)}, u32[]{:S(2)}, u32[]{:S(2)}) collective-permute-start(f32[1024]{0:T(1024)S(1)} %pad_maximum_fusion.1), channel_id=1, source_target_pairs={{0,1},{1,0},{2,3},{3,2},{4,5},{5,4},{6,7},{7,6},{8,9},{9,8},{10,11... | collective-permute-start | bytes 12296 | tf_op jit(solution)/shard_map/ppermute | solution.py:28
  70.0 7.0 %collective-permute-start.8 = (f32[1024]{0:T(1024)S(1)}, f32[1024]{0:T(1024)S(1)}, u32[]{:S(2)}, u32[]{:S(2)}) collective-permute-start(f32[1024]{0:T(1024)S(1)} %fusion.61), channel_id=1, source_target_pairs={{0,4},{4,8},{8,12},{12,0},{1,5},{5,9},{9,13},{13,1},{2,6},{6,10},{... | collective-permute-start | bytes 12296 | tf_op jit(solution)/shard_map/ppermute | solution.py:39
  70.0 7.0 %collective-permute-start.7 = (f32[1024]{0:T(1024)S(1)}, f32[1024]{0:T(1024)S(1)}, u32[]{:S(2)}, u32[]{:S(2)}) collective-permute-start(f32[1024]{0:T(1024)S(1)} %fusion.61), channel_id=1, source_target_pairs={{0,8},{4,12},{8,0},{12,4},{1,9},{5,13},{9,1},{13,5},{2,10},{6,14},... | collective-permute-start | bytes 12296 | tf_op jit(solution)/shard_map/ppermute | solution.py:39
  70.0 6.9 %collective-permute-start.6 = (f32[1024]{0:T(1024)S(1)}, f32[1024]{0:T(1024)S(1)}, u32[]{:S(2)}, u32[]{:S(2)}) collective-permute-start(f32[1024]{0:T(1024)S(1)} %fusion.61), channel_id=1, source_target_pairs={{0,12},{4,0},{8,4},{12,8},{1,13},{5,1},{9,5},{13,9},{2,14},{6,2},{... | collective-permute-start | bytes 12296 | tf_op jit(solution)/shard_map/ppermute | solution.py:39

commit v11 on v10

--- a/solution.py
+++ b/solution.py
@@ -47,6 +47,18 @@
     total = from_member(0)
     for member in range(1, length):
         total = total + from_member(member)
+    return total
+
+
+def exchange_sum(value, axes):
+    members = 1
+    for axis in axes:
+        members *= lax.axis_size(axis)
+    tiled = jnp.broadcast_to(value[None], (members,) + value.shape)
+    terms = lax.all_to_all(tiled, axes, 0, 0, tiled=True)
+    total = terms[0]
+    for member in range(1, members):
+        total = total + terms[member]
     return total
 
 
@@ -199,9 +211,8 @@
     grad_logit = inner_grads[3] + summary_grads[2]
     grad_bias = inner_grads[4] + summary_grads[3]
     token_total = token_count * lax.axis_size("ctx") * lax.axis_size("rep")
-    both_total = direct_sum(
-        butterfly_sum(jnp.concatenate([grad_bias.reshape(-1), grad_weight.reshape(-1)]), "rep"),
-        "ctx",
+    both_total = exchange_sum(
+        jnp.concatenate([grad_bias.reshape(-1), grad_weight.reshape(-1)]), ("ctx", "rep")
     )
     bias_total, weight_total = jnp.split(both_total, 2)
 

time: 77.9 us -> 79.8 us (1.024)
  waiting for transfers between devices: 37.2 us -> 39.1 us
    ppermute x3 -> x0, starting transfers between devices: 3.81 us -> none  [direct_sum(): terms.append(lax.ppermute(value, axis, pairs))]
    all_to_all x0 -> x1, starting transfers between devices: none -> 3.33 us  [exchange_sum(): terms = lax.all_to_all(tiled, axes, 0, 0, tiled=True)]
    all_to_all x0 -> x1, waiting for transfers between devices: none -> 2.49 us  [exchange_sum(): terms = lax.all_to_all(tiled, axes, 0, 0, tiled=True)]
    ppermute x2 -> x1, waiting for transfers between devices: 2.71 us -> 2.05 us  [butterfly_sum(): value = value + lax.ppermute(value, axis, pairs)]
    ppermute x2 -> x1, starting transfers between devices: 1.62 us -> 1.54 us  [butterfly_sum(): value = value + lax.ppermute(value, axis, pairs)]
  transfers between devices with their start and end apart: 9 -> 6, of which waited for: 6 -> 6; matrix products, arithmetic and copies ran while one was open for 7% -> 7% of each run, Pallas kernels for 0% -> 0%
where the time goes in v11:
time: 79.8 us; the launch traced here: 79.5 us
  waiting for transfers between devices  39.1 us (49%)
  starting transfers between devices  17.8 us (22%)
  other arithmetic  8.04 us (10%)
  local copies, waits for them, and re-layouts  7.34 us (9%)
  matrix products  4.77 us (6%)
  between operations  2.38 us (3%)
    ppermute x4, waiting for transfers between devices, from_behind(): return lax.ppermute(value, axis, pairs)  34.6 us
    ppermute x4, starting transfers between devices, from_behind(): return lax.ppermute(value, axis, pairs)  12.9 us
    unnamed x15, local copies, waits for them, and re-layouts  4.2 us
    all_to_all x1, starting transfers between devices, exchange_sum(): terms = lax.all_to_all(tiled, axes, 0, 0, tiled=True)  3.33 us
    all_to_all x1, waiting for transfers between devices, exchange_sum(): terms = lax.all_to_all(tiled, axes, 0, 0, tiled=True)  2.49 us
    ppermute x1, waiting for transfers between devices, butterfly_sum(): value = value + lax.ppermute(value, axis, pairs)  2.05 us
  transfers between devices with their start and end apart: 6, of which 6 were waited for; matrix products, arithmetic and copies ran while one was open for 7% of the time, Pallas kernels for 0%

profile of v11, /device:TPU:0, one launch (start us, length us, event | category | flops | bytes accessed | tf_op | source)
XLA Modules:
  0.0 79.5 jit_solution(14845901968153944463)
XLA Ops:
  0.6 0.6 copy-done.4
  1.4 0.2 broadcast_in_dim.26
  1.6 0.5 slice.119
  2.9 0.6 compare_convert_fusion.1
  3.5 1.0 %pad_maximum_fusion = bf16[4,128,512]{2,1,0:T(8,128)(2,1)S(1)} fusion(bf16[1,128,512]{2,1,0:T(8,128)(2,1)S(1)} %copy-done, bf16[1,128,512]{2,1,0:T(8,128)(2,1)S(1)} %copy-done.1, bf16[1,128,512]{2,1,0:T(8,128)(2,1)} %param.15, bf16[1,128,512]{2,1,0:T(8,128)(2,1)} %param.14), kind=kLoop, calls=%fused_computation.22 | loop fusion | flops 786432 | bytes 1048576 | tf_op jit(solution)/shard_map/concatenate | solution.py:165
  5.0 0.6 copy-done.3
  5.6 0.3 fusion.16
  6.1 0.3 multiply_reduce_fusion.1
  6.4 0.3 fusion.46
  6.8 4.9 %collective-permute-start = (f32[4,136,128]{2,1,0:T(8,128)S(1)}, f32[4,136,128]{2,1,0:T(8,128)S(1)}, u32[]{:S(2)}, u32[]{:S(2)}) collective-permute-start(f32[4,136,128]{2,1,0:T(8,128)S(1)} %fusion.9), channel_id=1, source_target_pairs={{0,4},{4,8},{8,12},{1,5},{5,9},{9,13},{2,6},{6,10},{10,14},{3,7},{... | collective-permute-start | bytes 835592 | tf_op jit(solution)/shard_map/ppermute | solution.py:18
  12.7 0.4 fusion.4
  13.1 4.5 %collective-permute-done = f32[4,136,128]{2,1,0:T(8,128)S(1)} collective-permute-done((f32[4,136,128]{2,1,0:T(8,128)S(1)}, f32[4,136,128]{2,1,0:T(8,128)S(1)}, u32[]{:S(2)}, u32[]{:S(2)}) %collective-permute-start) | collective-permute-done | bytes 278560 | tf_op jit(solution)/shard_map/ppermute | solution.py:18
  17.8 5.4 %collective-permute-start.1 = (f32[4,128,128]{2,1,0:T(8,128)S(1)}, f32[4,128,128]{2,1,0:T(8,128)S(1)}, u32[]{:S(2)}, u32[]{:S(2)}) collective-permute-start(f32[4,128,128]{2,1,0:T(8,128)S(1)} %multiply_add_fusion.5), channel_id=1, source_target_pairs={{0,8},{4,12},{1,9},{5,13},{2,10},{6,14},{3,11},{7,15},{16,24},{20,... | collective-permute-start | bytes 786440 | tf_op jit(solution)/shard_map/ppermute | solution.py:18
  23.2 0.2 fusion.65
  23.4 4.5 %collective-permute-done.1 = f32[4,128,128]{2,1,0:T(8,128)S(1)} collective-permute-done((f32[4,128,128]{2,1,0:T(8,128)S(1)}, f32[4,128,128]{2,1,0:T(8,128)S(1)}, u32[]{:S(2)}, u32[]{:S(2)}) %collective-permute-start.1) | collective-permute-done | bytes 262176 | tf_op jit(solution)/shard_map/ppermute | solution.py:18
  28.0 0.4 fusion.15
  28.5 0.6 copy-done.2
  29.1 0.2 convolution_bitcast_fusion.2
  29.3 1.5 %collective-permute-start.2 = (f32[128]{0:T(128)S(1)}, f32[128]{0:T(128)S(1)}, u32[]{:S(2)}, u32[]{:S(2)}) collective-permute-start(f32[128]{0:T(128)S(1)} %convolution_bitcast_fusion.2), channel_id=1, source_target_pairs={{0,2},{2,0},{1,3},{3,1},{4,6},{6,4},{5,7},{7,5},{8,10},{10,8},{9,1... | collective-permute-start | bytes 1544 | tf_op jit(solution)/shard_map/ppermute | solution.py:28
  30.8 2.0 %collective-permute-done.2 = f32[128]{0:T(128)S(1)} collective-permute-done((f32[128]{0:T(128)S(1)}, f32[128]{0:T(128)S(1)}, u32[]{:S(2)}, u32[]{:S(2)}) %collective-permute-start.2) | collective-permute-done | bytes 544 | tf_op jit(solution)/shard_map/ppermute | solution.py:28
  32.9 0.5 bitcast_subtract_fusion
  33.6 0.5 fusion.17
  34.1 0.3 fusion.8
  34.4 0.3 convolution_bitcast_fusion
  34.7 1.3 %collective-permute-start.3 = (f32[4,136,128]{2,1,0:T(8,128)S(1)}, f32[4,136,128]{2,1,0:T(8,128)S(1)}, u32[]{:S(2)}, u32[]{:S(2)}) collective-permute-start(f32[4,136,128]{2,1,0:T(8,128)S(1)} %fusion.10), channel_id=1, source_target_pairs={{4,0},{8,4},{12,8},{5,1},{9,5},{13,9},{6,2},{10,6},{14,10},{7,3},{... | collective-permute-start | bytes 835592 | tf_op jit(solution)/shard_map/ppermute | solution.py:18
  36.0 0.3 fusion.6
  36.3 0.4 convolution_bitcast_fusion.1
  36.7 12.7 %collective-permute-done.3 = f32[4,136,128]{2,1,0:T(8,128)S(1)} collective-permute-done((f32[4,136,128]{2,1,0:T(8,128)S(1)}, f32[4,136,128]{2,1,0:T(8,128)S(1)}, u32[]{:S(2)}, u32[]{:S(2)}) %collective-permute-start.3) | collective-permute-done | bytes 278560 | tf_op jit(solution)/shard_map/ppermute | solution.py:18
  49.5 1.3 %collective-permute-start.4 = (f32[4,128,128]{2,1,0:T(8,128)S(1)}, f32[4,128,128]{2,1,0:T(8,128)S(1)}, u32[]{:S(2)}, u32[]{:S(2)}) collective-permute-start(f32[4,128,128]{2,1,0:T(8,128)S(1)} %multiply_add_fusion.3), channel_id=1, source_target_pairs={{8,0},{12,4},{9,1},{13,5},{10,2},{14,6},{11,3},{15,7},{24,16},{28,... | collective-permute-start | bytes 786440 | tf_op jit(solution)/shard_map/ppermute | solution.py:18
  50.8 0.2 fusion.55
  51.0 0.4 fusion.3
  51.4 12.9 %collective-permute-done.4 = f32[4,128,128]{2,1,0:T(8,128)S(1)} collective-permute-done((f32[4,128,128]{2,1,0:T(8,128)S(1)}, f32[4,128,128]{2,1,0:T(8,128)S(1)}, u32[]{:S(2)}, u32[]{:S(2)}) %collective-permute-start.4) | collective-permute-done | bytes 262176 | tf_op jit(solution)/shard_map/ppermute | solution.py:18
  64.3 0.2 multiply_reduce_fusion
  64.6 0.5 fusion.5
  65.1 0.5 fusion.62
  65.5 0.1 copy.140
  65.7 0.1 copy.139
  66.3 1.1 %fusion.64 = f32[128,4,128]{2,1,0:T(4,128)S(1)} fusion(f32[128,4,128]{2,1,0:T(4,128)S(1)} %copy.141), kind=kOutput, calls=%fused_computation.135 | output fusion | flops 8323072 | bytes 524288 | tf_op jit(solution)/shard_map/transpose(jvp(jit(cumsum)))/reduce_window_sum | solution.py:133
  67.5 1.1 %fusion.63 = f32[128,4,128]{2,1,0:T(4,128)S(1)} fusion(f32[128,4,128]{2,1,0:T(4,128)S(1)} %copy.138), kind=kOutput, calls=%fused_computation.134 | output fusion | flops 8323072 | bytes 524288 | tf_op jit(solution)/shard_map/transpose(jvp(jit(cumsum)))/reduce_window_sum | solution.py:109
  68.6 0.6 fusion.51
  69.2 0.6 broadcast_in_dim.49
  69.8 3.3 %all-to-all-start = ((f32[8,1,1024]{2,1,0:T(1,128)}), f32[8,1,1024]{2,1,0:T(1,128)S(1)}, u32[]{:S(2)}, u32[]{:S(2)}) async-start(f32[8,1,1024]{2,1,0:T(1,128)} %broadcast_in_dim.49), calls=%async_computation | async-start | bytes 65536 | tf_op jit(solution)/shard_map/all_to_all | solution.py:58
  73.3 0.8 copy.144
  74.1 0.8 copy.143
  74.9 0.8 copy.142
  75.7 0.7 convert_element_type.135
  76.4 2.5 %all-to-all-done = f32[8,1,1024]{2,1,0:T(1,128)S(1)} async-done(((f32[8,1,1024]{2,1,0:T(1,128)}), f32[8,1,1024]{2,1,0:T(1,128)S(1)}, u32[]{:S(2)}, u32[]{:S(2)}) %all-to-all-start) | async-done | bytes 32800 | tf_op jit(solution)/shard_map/all_to_all | solution.py:58
  78.9 0.6 slice_multiply_fusion
  (42 shorter events, 2.4 us)
Async XLA Ops:
  0.6 0.7 copy-start.4
  1.3 2.2 %copy-start = (bf16[1,128,512]{2,1,0:T(8,128)(2,1)S(1)}, bf16[1,128,512]{2,1,0:T(8,128)(2,1)}, u32[]{:S(2)}) copy-start(bf16[1,128,512]{2,1,0:T(8,128)(2,1)} %param.17) | copy-start | bytes 393220
  1.3 2.2 %copy-start.1 = (bf16[1,128,512]{2,1,0:T(8,128)(2,1)S(1)}, bf16[1,128,512]{2,1,0:T(8,128)(2,1)}, u32[]{:S(2)}) copy-start(bf16[1,128,512]{2,1,0:T(8,128)(2,1)} %param.16) | copy-start | bytes 393220
  4.9 0.7 copy-start.3
  6.8 10.8 %collective-permute-start = (f32[4,136,128]{2,1,0:T(8,128)S(1)}, f32[4,136,128]{2,1,0:T(8,128)S(1)}, u32[]{:S(2)}, u32[]{:S(2)}) collective-permute-start(f32[4,136,128]{2,1,0:T(8,128)S(1)} %fusion.9), channel_id=1, source_target_pairs={{0,4},{4,8},{8,12},{1,5},{5,9},{9,13},{2,6},{6,10},{10,14},{3,7},{... | collective-permute-start | bytes 835592 | tf_op jit(solution)/shard_map/ppermute | solution.py:18
  17.8 10.1 %collective-permute-start.1 = (f32[4,128,128]{2,1,0:T(8,128)S(1)}, f32[4,128,128]{2,1,0:T(8,128)S(1)}, u32[]{:S(2)}, u32[]{:S(2)}) collective-permute-start(f32[4,128,128]{2,1,0:T(8,128)S(1)} %multiply_add_fusion.5), channel_id=1, source_target_pairs={{0,8},{4,12},{1,9},{5,13},{2,10},{6,14},{3,11},{7,15},{16,24},{20,... | collective-permute-start | bytes 786440 | tf_op jit(solution)/shard_map/ppermute | solution.py:18
  28.4 0.7 copy-start.2
  29.1 3.8 %copy-start.5 = (f32[1,128]{1,0:T(1,128)S(1)}, f32[1,128]{1,0:T(1,128)}, u32[]{:S(2)}) copy-start(f32[1,128]{1,0:T(1,128)} %param.20) | copy-start | bytes 1540
  29.3 3.6 %collective-permute-start.2 = (f32[128]{0:T(128)S(1)}, f32[128]{0:T(128)S(1)}, u32[]{:S(2)}, u32[]{:S(2)}) collective-permute-start(f32[128]{0:T(128)S(1)} %convolution_bitcast_fusion.2), channel_id=1, source_target_pairs={{0,2},{2,0},{1,3},{3,1},{4,6},{6,4},{5,7},{7,5},{8,10},{10,8},{9,1... | collective-permute-start | bytes 1544 | tf_op jit(solution)/shard_map/ppermute | solution.py:28
  34.7 14.6 %collective-permute-start.3 = (f32[4,136,128]{2,1,0:T(8,128)S(1)}, f32[4,136,128]{2,1,0:T(8,128)S(1)}, u32[]{:S(2)}, u32[]{:S(2)}) collective-permute-start(f32[4,136,128]{2,1,0:T(8,128)S(1)} %fusion.10), channel_id=1, source_target_pairs={{4,0},{8,4},{12,8},{5,1},{9,5},{13,9},{6,2},{10,6},{14,10},{7,3},{... | collective-permute-start | bytes 835592 | tf_op jit(solution)/shard_map/ppermute | solution.py:18
  49.5 14.8 %collective-permute-start.4 = (f32[4,128,128]{2,1,0:T(8,128)S(1)}, f32[4,128,128]{2,1,0:T(8,128)S(1)}, u32[]{:S(2)}, u32[]{:S(2)}) collective-permute-start(f32[4,128,128]{2,1,0:T(8,128)S(1)} %multiply_add_fusion.3), channel_id=1, source_target_pairs={{8,0},{12,4},{9,1},{13,5},{10,2},{14,6},{11,3},{15,7},{24,16},{28,... | collective-permute-start | bytes 786440 | tf_op jit(solution)/shard_map/ppermute | solution.py:18
  69.8 9.0 %all-to-all-start = ((f32[8,1,1024]{2,1,0:T(1,128)}), f32[8,1,1024]{2,1,0:T(1,128)S(1)}, u32[]{:S(2)}, u32[]{:S(2)}) async-start(f32[8,1,1024]{2,1,0:T(1,128)} %broadcast_in_dim.49), calls=%async_computation | async-start | bytes 65536 | tf_op jit(solution)/shard_map/all_to_all | solution.py:58

commit v12 on v10

--- a/solution.py
+++ b/solution.py
@@ -83,6 +83,13 @@
     return near_a
 
 
+def running_sum(values):
+    length = values.shape[0]
+    positions = jnp.arange(length, dtype=jnp.int32)
+    lower = (positions[:, None] >= positions[None, :]).astype(values.dtype)
+    return jnp.einsum("ts,shc->thc", lower, values, precision=lax.Precision.HIGHEST)
+
+
 def log_decay(logit_in, bias_in):
     return jax.nn.log_sigmoid(logit_in + bias_in) / gate_scale
 
@@ -94,7 +101,7 @@
 def block_inner(query_in, key_in, value_in, logit_in, bias_in, start_flags, kind_id):
     block_len = query_in.shape[0]
     channels = query_in.shape[2]
-    log_cum = jnp.cumsum(log_decay(logit_in, bias_in), axis=0)
+    log_cum = running_sum(log_decay(logit_in, bias_in))
     segment = segment_ids(start_flags)
     alive_mask = (segment == 0).astype(jnp.float32)
     offsets = jnp.arange(block_len, dtype=jnp.int32)
@@ -118,7 +125,7 @@
 
 
 def block_summary(key_in, value_in, logit_in, bias_in, start_flags):
-    log_cum = jnp.cumsum(log_decay(logit_in, bias_in), axis=0)
+    log_cum = running_sum(log_decay(logit_in, bias_in))
     log_last = log_cum[-1]
     segment = segment_ids(start_flags)
     alive_last = (segment[-1] == 0).astype(jnp.float32)

time: 77.9 us -> 80.9 us (1.039)
  local copies, waits for them, and re-layouts: 6.72 us -> 9.6 us
  waiting for transfers between devices: 37.2 us -> 34.9 us
  other arithmetic: 8.05 us -> 9.25 us
  matrix products: 4.74 us -> 5.89 us
    ppermute x4, waiting for transfers between devices: 34.5 us -> 31.9 us  [from_behind(): return lax.ppermute(value, axis, pairs)]
    another operation x3 -> x0, other arithmetic: 2.5 us -> none  [the longest x2 1.43 us: block_inner(): log_cum = jnp.cumsum(log_decay(logit_in, bias_in), axis=0)]
    reduce_sum x0 -> x1, other arithmetic: none -> 1.47 us  [block_summary(): log_last[None] - log_cum]
    dot_general x0 -> x5, local copies, waits for them, and re-layouts: none -> 1.42 us  [the longest x1 0.83 us: block_summary(): jnp.einsum('jhc,jhd->hcd', key_tail, value_in, precision=highest)]
    add x2, other arithmetic: 0.26 us -> 1.66 us  [gather_scan(): run_a = far_a * run_b[..., None] + run_a]
    reduce_sum x1, other arithmetic: 0.25 us -> 1.27 us  [on_device(): grad_decay = jnp.sum(state_in * grad_state, axis=-1)]
    unnamed x15 -> x18, local copies, waits for them, and re-layouts: 4.2 us -> 4.32 us
  transfers between devices with their start and end apart: 9 -> 9, of which waited for: 6 -> 6; matrix products, arithmetic and copies ran while one was open for 7% -> 10% of each run, Pallas kernels for 0% -> 0%
where the time goes in v12:
time: 80.9 us; the launch traced here: 80.5 us
  waiting for transfers between devices  34.9 us (43%)
  starting transfers between devices  18.3 us (23%)
  local copies, waits for them, and re-layouts  9.6 us (12%)
  other arithmetic  9.25 us (11%)
  matrix products  5.89 us (7%)
  between operations  2.51 us (3%)
    ppermute x4, waiting for transfers between devices, from_behind(): return lax.ppermute(value, axis, pairs)  31.9 us
    ppermute x4, starting transfers between devices, from_behind(): return lax.ppermute(value, axis, pairs)  12.9 us
    unnamed x18, local copies, waits for them, and re-layouts  4.32 us
    ppermute x3, starting transfers between devices, direct_sum(): terms.append(lax.ppermute(value, axis, pairs))  3.81 us
    ppermute x2, waiting for transfers between devices, butterfly_sum(): value = value + lax.ppermute(value, axis, pairs)  2.95 us
    dot_general x3, matrix products, block_inner(): scores = jnp.einsum('ihc,jhc->hij', query_dec, key_dec, precision=highest)  1.74 us
    add x2, other arithmetic, gather_scan(): run_a = far_a * run_b[..., None] + run_a  1.66 us
  transfers between devices with their start and end apart: 9, of which 6 were waited for; matrix products, arithmetic and copies ran while one was open for 10% of the time, Pallas kernels for 0%

profile of v12, /device:TPU:0, one launch (start us, length us, event | category | flops | bytes accessed | tf_op | source)
XLA Modules:
  0.0 80.5 jit_solution(8090794217481185187)
XLA Ops:
  0.6 0.6 copy-done.6
  1.6 0.5 slice.77
  2.9 0.7 compare_convert_fusion.1
  3.6 1.0 %pad_maximum_fusion = bf16[4,128,512]{2,1,0:T(8,128)(2,1)S(1)} fusion(bf16[1,128,512]{2,1,0:T(8,128)(2,1)S(1)} %copy-done.2, bf16[1,128,512]{2,1,0:T(8,128)(2,1)S(1)} %copy-done.3, bf16[1,128,512]{2,1,0:T(8,128)(2,1)} %param.15, bf16[1,128,512]{2,1,0:T(8,128)(2,1)} %param.14), kind=kLoop, calls=%fused_computation.14 | loop fusion | flops 786432 | bytes 1048576 | tf_op jit(solution)/shard_map/concatenate | solution.py:160
  5.1 0.7 copy-done.5
  5.8 0.2 negate_multiply_fusion
  6.1 0.3 fusion.45
  6.5 0.4 broadcast_multiply_fusion
  6.9 0.3 fusion.19
  7.2 4.9 %collective-permute-start = (f32[4,136,128]{2,1,0:T(8,128)S(1)}, f32[4,136,128]{2,1,0:T(8,128)S(1)}, u32[]{:S(2)}, u32[]{:S(2)}) collective-permute-start(f32[4,136,128]{2,1,0:T(8,128)S(1)} %fusion.5), channel_id=1, source_target_pairs={{0,4},{4,8},{8,12},{1,5},{5,9},{9,13},{2,6},{6,10},{10,14},{3,7},{... | collective-permute-start | bytes 835592 | tf_op jit(solution)/shard_map/ppermute | solution.py:18
  13.3 4.8 %collective-permute-done = f32[4,136,128]{2,1,0:T(8,128)S(1)} collective-permute-done((f32[4,136,128]{2,1,0:T(8,128)S(1)}, f32[4,136,128]{2,1,0:T(8,128)S(1)}, u32[]{:S(2)}, u32[]{:S(2)}) %collective-permute-start) | collective-permute-done | bytes 278560 | tf_op jit(solution)/shard_map/ppermute | solution.py:18
  18.1 0.8 %multiply_add_fusion.3 = f32[4,128,128]{2,1,0:T(8,128)} fusion(f32[4,128,128]{2,1,0:T(8,128)S(1)} %fusion.19, f32[4,136,128]{2,1,0:T(8,128)S(1)} %collective-permute-done, f32[4,128]{1,0:T(4,128)S(1)} %exponential_multiply_fusion.1), kind=kLoop, calls=%fused_computation.54 | loop fusion | flops 131072 | bytes 788480 | tf_op jit(solution)/shard_map/add | solution.py:78
  18.9 5.4 %collective-permute-start.1 = (f32[4,128,128]{2,1,0:T(8,128)}, f32[4,128,128]{2,1,0:T(8,128)S(1)}, u32[]{:S(2)}, u32[]{:S(2)}) collective-permute-start(f32[4,128,128]{2,1,0:T(8,128)} %multiply_add_fusion.3), channel_id=1, source_target_pairs={{0,8},{4,12},{1,9},{5,13},{2,10},{6,14},{3,11},{7,15},{16,24},{20,... | collective-permute-start | bytes 786440 | tf_op jit(solution)/shard_map/ppermute | solution.py:18
  24.3 0.4 fusion
  25.1 4.2 %collective-permute-done.1 = f32[4,128,128]{2,1,0:T(8,128)S(1)} collective-permute-done((f32[4,128,128]{2,1,0:T(8,128)}, f32[4,128,128]{2,1,0:T(8,128)S(1)}, u32[]{:S(2)}, u32[]{:S(2)}) %collective-permute-start.1) | collective-permute-done | bytes 262176 | tf_op jit(solution)/shard_map/ppermute | solution.py:18
  29.5 0.4 fusion.18
  29.9 0.6 copy-done.4
  30.7 1.5 %collective-permute-start.2 = (f32[128]{0:T(128)S(1)}, f32[128]{0:T(128)S(1)}, u32[]{:S(2)}, u32[]{:S(2)}) collective-permute-start(f32[128]{0:T(128)S(1)} %convolution_bitcast_fusion), channel_id=1, source_target_pairs={{0,2},{2,0},{1,3},{3,1},{4,6},{6,4},{5,7},{7,5},{8,10},{10,8},{9,1... | collective-permute-start | bytes 1544 | tf_op jit(solution)/shard_map/ppermute | solution.py:28
  32.3 2.1 %collective-permute-done.2 = f32[128]{0:T(128)S(1)} collective-permute-done((f32[128]{0:T(128)S(1)}, f32[128]{0:T(128)S(1)}, u32[]{:S(2)}, u32[]{:S(2)}) %collective-permute-start.2) | collective-permute-done | bytes 544 | tf_op jit(solution)/shard_map/ppermute | solution.py:28
  34.3 0.5 bitcast_subtract_fusion
  35.0 0.5 fusion.22
  35.5 1.3 %collective-permute-start.3 = (f32[4,136,128]{2,1,0:T(8,128)S(1)}, f32[4,136,128]{2,1,0:T(8,128)S(1)}, u32[]{:S(2)}, u32[]{:S(2)}) collective-permute-start(f32[4,136,128]{2,1,0:T(8,128)S(1)} %fusion.6), channel_id=1, source_target_pairs={{4,0},{8,4},{12,8},{5,1},{9,5},{13,9},{6,2},{10,6},{14,10},{7,3},{... | collective-permute-start | bytes 835592 | tf_op jit(solution)/shard_map/ppermute | solution.py:18
  36.8 0.3 fusion.4
  37.2 1.0 %fusion.60 = f32[4,128,128]{1,2,0:T(8,128)} fusion(f32[4,128,128]{2,1,0:T(8,128)S(1)} %fusion.4, f32[128,4,128]{0,2,1:T(8,128)S(1)} %copy.107), kind=kOutput, calls=%fused_computation.127 | convolution fusion | flops 50331648 | bytes 786432 | tf_op jit(solution)/shard_map/transpose(jvp(ihc,jhc->hij))/dot_general | solution.py:115
  38.1 0.4 fusion.23
  38.5 11.7 %collective-permute-done.3 = f32[4,136,128]{2,1,0:T(8,128)S(1)} collective-permute-done((f32[4,136,128]{2,1,0:T(8,128)S(1)}, f32[4,136,128]{2,1,0:T(8,128)S(1)}, u32[]{:S(2)}, u32[]{:S(2)}) %collective-permute-start.3) | collective-permute-done | bytes 278560 | tf_op jit(solution)/shard_map/ppermute | solution.py:18
  50.2 0.8 %multiply_add_fusion.1 = f32[4,128,128]{2,1,0:T(8,128)} fusion(f32[4,128,128]{2,1,0:T(8,128)S(1)} %fusion.22, f32[4,136,128]{2,1,0:T(8,128)S(1)} %collective-permute-done.3, f32[4,128]{1,0:T(4,128)S(1)} %exponential_multiply_fusion.1), kind=kLoop, calls=%fused_computation.51 | loop fusion | flops 131072 | bytes 788480 | tf_op jit(solution)/shard_map/add | solution.py:78
  51.0 1.3 %collective-permute-start.4 = (f32[4,128,128]{2,1,0:T(8,128)}, f32[4,128,128]{2,1,0:T(8,128)}, u32[]{:S(2)}, u32[]{:S(2)}) collective-permute-start(f32[4,128,128]{2,1,0:T(8,128)} %multiply_add_fusion.1), channel_id=1, source_target_pairs={{8,0},{12,4},{9,1},{13,5},{10,2},{14,6},{11,3},{15,7},{24,16},{28,... | collective-permute-start | bytes 786440 | tf_op jit(solution)/shard_map/ppermute | solution.py:18
  52.3 0.4 fusion.59
  53.0 0.8 copy-done
  54.2 0.7 slice.81
  54.9 11.3 %collective-permute-done.4 = f32[4,128,128]{2,1,0:T(8,128)} collective-permute-done((f32[4,128,128]{2,1,0:T(8,128)}, f32[4,128,128]{2,1,0:T(8,128)}, u32[]{:S(2)}, u32[]{:S(2)}) %collective-permute-start.4) | collective-permute-done | bytes 262176 | tf_op jit(solution)/shard_map/ppermute | solution.py:18
  66.2 1.3 %multiply_reduce_fusion = (f32[4,128]{1,0:T(4,128)S(1)}, f32[4,128,128]{2,1,0:T(8,128)S(1)}) fusion(f32[4,128,128]{2,1,0:T(8,128)S(1)} %multiply_add_fusion.2, f32[4,136,128]{2,1,0:T(8,128)} %copy-done.1, f32[4,128,128]{2,1,0:T(8,128)} %collective-permute-done.4, f32[4,128]{1,0:T(4,128)S(1)} %bitcast.168), kind=kLoop, calls=%fused_computation.48 | loop fusion | flops 261632 | bytes 1052672 | tf_op jit(solution)/shard_map/reduce_sum | solution.py:200
  67.4 0.2 fusion.61
  67.7 0.8 %copy.112 = f32[4,128,128]{1,0,2:T(4,128)} copy(f32[4,128,128]{2,1,0:T(8,128)S(1)} %fusion.61) | data formatting | bytes 524288 | tf_op jit(solution)/shard_map/transpose(jvp(jhc,jhd->hcd))/dot_general | solution.py:134
  68.5 1.5 %fusion.56 = (f32[4,128]{1,0:T(4,128)S(1)}, f32[128,4,128]{2,1,0:T(4,128)S(1)}, bf16[128,4,128]{2,1,0:T(4,128)(2,1)S(1)}, bf16[128,4,128]{2,1,0:T(4,128)(2,1)S(1)}, f32[128,4,128]{2,1,0:T(4,128)S(1)}) fusion(f32[128,4,128]{2,1,0:T(4,128)S(1)} %copy.90, f32[4,128]{1,0:T(4,128)S(1)} %get-tuple-element.82, f32[128,4,128]{2,1,0:T(4,128)S(1)} %reshape.278, ...), kind=kLoop, calls=%fused_computation.124 | loop fusion | flops 1375744 | bytes 2626560 | tf_op jit(solution)/shard_map/transpose(jvp())/reduce_sum | solution.py:133
  70.2 0.3 fusion.43
  70.6 0.3 fusion.44
  70.9 0.5 fusion.41
  71.5 0.3 fusion.2
  71.8 0.9 %collective-permute-done.5 = f32[1024]{0:T(1024)S(1)} collective-permute-done((f32[1024]{0:T(1024)S(1)}, f32[1024]{0:T(1024)S(1)}, u32[]{:S(2)}, u32[]{:S(2)}) %collective-permute-start.5) | collective-permute-done | bytes 4128 | tf_op jit(solution)/shard_map/ppermute | solution.py:28
  72.7 3.7 %collective-permute-start.6 = (f32[1024]{0:T(1024)S(1)}, f32[1024]{0:T(1024)S(1)}, u32[]{:S(2)}, u32[]{:S(2)}) collective-permute-start(f32[1024]{0:T(1024)S(1)} %fusion.55), channel_id=1, source_target_pairs={{0,12},{4,0},{8,4},{12,8},{1,13},{5,1},{9,5},{13,9},{2,14},{6,2},{... | collective-permute-start | bytes 12296 | tf_op jit(solution)/shard_map/ppermute | solution.py:39
  76.5 0.4 fusion.1
  76.9 0.8 copy.117
  77.7 0.7 convert_element_type.130
  78.4 0.7 convert_element_type.128
  79.1 0.8 copy.118
  79.9 0.6 slice_multiply_fusion
  (57 shorter events, 3.5 us)
Async XLA Ops:
  0.6 0.7 copy-start.6
  1.3 2.3 %copy-start.2 = (bf16[1,128,512]{2,1,0:T(8,128)(2,1)S(1)}, bf16[1,128,512]{2,1,0:T(8,128)(2,1)}, u32[]{:S(2)}) copy-start(bf16[1,128,512]{2,1,0:T(8,128)(2,1)} %param.17) | copy-start | bytes 393220
  1.3 2.3 %copy-start.3 = (bf16[1,128,512]{2,1,0:T(8,128)(2,1)S(1)}, bf16[1,128,512]{2,1,0:T(8,128)(2,1)}, u32[]{:S(2)}) copy-start(bf16[1,128,512]{2,1,0:T(8,128)(2,1)} %param.16) | copy-start | bytes 393220
  5.1 0.7 copy-start.5
  7.2 10.8 %collective-permute-start = (f32[4,136,128]{2,1,0:T(8,128)S(1)}, f32[4,136,128]{2,1,0:T(8,128)S(1)}, u32[]{:S(2)}, u32[]{:S(2)}) collective-permute-start(f32[4,136,128]{2,1,0:T(8,128)S(1)} %fusion.5), channel_id=1, source_target_pairs={{0,4},{4,8},{8,12},{1,5},{5,9},{9,13},{2,6},{6,10},{10,14},{3,7},{... | collective-permute-start | bytes 835592 | tf_op jit(solution)/shard_map/ppermute | solution.py:18
  18.9 10.4 %collective-permute-start.1 = (f32[4,128,128]{2,1,0:T(8,128)}, f32[4,128,128]{2,1,0:T(8,128)S(1)}, u32[]{:S(2)}, u32[]{:S(2)}) collective-permute-start(f32[4,128,128]{2,1,0:T(8,128)} %multiply_add_fusion.3), channel_id=1, source_target_pairs={{0,8},{4,12},{1,9},{5,13},{2,10},{6,14},{3,11},{7,15},{16,24},{20,... | collective-permute-start | bytes 786440 | tf_op jit(solution)/shard_map/ppermute | solution.py:18
  29.9 0.7 copy-start.4
  30.7 3.6 %collective-permute-start.2 = (f32[128]{0:T(128)S(1)}, f32[128]{0:T(128)S(1)}, u32[]{:S(2)}, u32[]{:S(2)}) collective-permute-start(f32[128]{0:T(128)S(1)} %convolution_bitcast_fusion), channel_id=1, source_target_pairs={{0,2},{2,0},{1,3},{3,1},{4,6},{6,4},{5,7},{7,5},{8,10},{10,8},{9,1... | collective-permute-start | bytes 1544 | tf_op jit(solution)/shard_map/ppermute | solution.py:28
  32.3 2.1 %copy-start.7 = (f32[1,128]{1,0:T(1,128)S(1)}, f32[1,128]{1,0:T(1,128)}, u32[]{:S(2)}) copy-start(f32[1,128]{1,0:T(1,128)} %param.20) | copy-start | bytes 1540
  35.5 14.6 %collective-permute-start.3 = (f32[4,136,128]{2,1,0:T(8,128)S(1)}, f32[4,136,128]{2,1,0:T(8,128)S(1)}, u32[]{:S(2)}, u32[]{:S(2)}) collective-permute-start(f32[4,136,128]{2,1,0:T(8,128)S(1)} %fusion.6), channel_id=1, source_target_pairs={{4,0},{8,4},{12,8},{5,1},{9,5},{13,9},{6,2},{10,6},{14,10},{7,3},{... | collective-permute-start | bytes 835592 | tf_op jit(solution)/shard_map/ppermute | solution.py:18
  50.2 0.8 %copy-start.1 = (f32[4,136,128]{2,1,0:T(8,128)}, f32[4,136,128]{2,1,0:T(8,128)S(1)}, u32[]{:S(2)}) copy-start(f32[4,136,128]{2,1,0:T(8,128)S(1)} %collective-permute-done.3) | copy-start | bytes 835588
  51.0 15.1 %collective-permute-start.4 = (f32[4,128,128]{2,1,0:T(8,128)}, f32[4,128,128]{2,1,0:T(8,128)}, u32[]{:S(2)}, u32[]{:S(2)}) collective-permute-start(f32[4,128,128]{2,1,0:T(8,128)} %multiply_add_fusion.1), channel_id=1, source_target_pairs={{8,0},{12,4},{9,1},{13,5},{10,2},{14,6},{11,3},{15,7},{24,16},{28,... | collective-permute-start | bytes 786440 | tf_op jit(solution)/shard_map/ppermute | solution.py:18
  52.8 1.0 %copy-start = (f32[4,128,128]{1,2,0:T(8,128)S(1)}, f32[4,128,128]{1,2,0:T(8,128)}, u32[]{:S(2)}) copy-start(f32[4,128,128]{1,2,0:T(8,128)} %fusion.60) | copy-start | bytes 786436
  71.4 1.2 %collective-permute-start.5 = (f32[1024]{0:T(1024)S(1)}, f32[1024]{0:T(1024)S(1)}, u32[]{:S(2)}, u32[]{:S(2)}) collective-permute-start(f32[1024]{0:T(1024)S(1)} %pad_maximum_fusion.1), channel_id=1, source_target_pairs={{0,1},{1,0},{2,3},{3,2},{4,5},{5,4},{6,7},{7,6},{8,9},{9,8},{10,11... | collective-permute-start | bytes 12296 | tf_op jit(solution)/shard_map/ppermute | solution.py:28
  72.7 7.2 %collective-permute-start.8 = (f32[1024]{0:T(1024)S(1)}, f32[1024]{0:T(1024)S(1)}, u32[]{:S(2)}, u32[]{:S(2)}) collective-permute-start(f32[1024]{0:T(1024)S(1)} %fusion.55), channel_id=1, source_target_pairs={{0,4},{4,8},{8,12},{12,0},{1,5},{5,9},{9,13},{13,1},{2,6},{6,10},{... | collective-permute-start | bytes 12296 | tf_op jit(solution)/shard_map/ppermute | solution.py:39
  72.7 7.2 %collective-permute-start.7 = (f32[1024]{0:T(1024)S(1)}, f32[1024]{0:T(1024)S(1)}, u32[]{:S(2)}, u32[]{:S(2)}) collective-permute-start(f32[1024]{0:T(1024)S(1)} %fusion.55), channel_id=1, source_target_pairs={{0,8},{4,12},{8,0},{12,4},{1,9},{5,13},{9,1},{13,5},{2,10},{6,14},... | collective-permute-start | bytes 12296 | tf_op jit(solution)/shard_map/ppermute | solution.py:39
  72.7 7.1 %collective-permute-start.6 = (f32[1024]{0:T(1024)S(1)}, f32[1024]{0:T(1024)S(1)}, u32[]{:S(2)}, u32[]{:S(2)}) collective-permute-start(f32[1024]{0:T(1024)S(1)} %fusion.55), channel_id=1, source_target_pairs={{0,12},{4,0},{8,4},{12,8},{1,13},{5,1},{9,5},{13,9},{2,14},{6,2},{... | collective-permute-start | bytes 12296 | tf_op jit(solution)/shard_map/ppermute | solution.py:39

commit v13 on v10

--- a/solution.py
+++ b/solution.py
@@ -91,10 +91,9 @@
     return jnp.cumsum(start_flags, axis=0, dtype=jnp.int32)
 
 
-def block_inner(query_in, key_in, value_in, logit_in, bias_in, start_flags, kind_id):
+def block_inner(query_in, key_in, value_in, log_cum, start_flags, kind_id):
     block_len = query_in.shape[0]
     channels = query_in.shape[2]
-    log_cum = jnp.cumsum(log_decay(logit_in, bias_in), axis=0)
     segment = segment_ids(start_flags)
     alive_mask = (segment == 0).astype(jnp.float32)
     offsets = jnp.arange(block_len, dtype=jnp.int32)
@@ -117,8 +116,7 @@
     return inner_part, carried
 
 
-def block_summary(key_in, value_in, logit_in, bias_in, start_flags):
-    log_cum = jnp.cumsum(log_decay(logit_in, bias_in), axis=0)
+def block_summary(key_in, value_in, log_cum, start_flags):
     log_last = log_cum[-1]
     segment = segment_ids(start_flags)
     alive_last = (segment[-1] == 0).astype(jnp.float32)
@@ -158,18 +156,18 @@
     logit_f = to_heads(rows_in[3:4])
     bias_h = gate_bias.reshape(head_count, DK)
 
-    def inner_terms(query_in, key_in, value_in, logit_in, bias_in):
-        return block_inner(query_in, key_in, value_in, logit_in, bias_in, start_flags, kind_id)
-
-    def summary_terms(key_in, value_in, logit_in, bias_in):
-        return block_summary(key_in, value_in, logit_in, bias_in, start_flags)
-
-    (attended_local, carried), pull_inner = jax.vjp(
-        inner_terms, query_f, key_f, value_f, logit_f, bias_h
-    )
-    (state_local, decay_local), pull_summary = jax.vjp(
-        summary_terms, key_f, value_f, logit_f, bias_h
-    )
+    def inner_terms(query_in, key_in, value_in, log_cum):
+        return block_inner(query_in, key_in, value_in, log_cum, start_flags, kind_id)
+
+    def summary_terms(key_in, value_in, log_cum):
+        return block_summary(key_in, value_in, log_cum, start_flags)
+
+    def running_decay(logit_in, bias_in):
+        return jnp.cumsum(log_decay(logit_in, bias_in), axis=0)
+
+    log_cum, pull_decay = jax.vjp(running_decay, logit_f, bias_h)
+    (attended_local, carried), pull_inner = jax.vjp(inner_terms, query_f, key_f, value_f, log_cum)
+    (state_local, decay_local), pull_summary = jax.vjp(summary_terms, key_f, value_f, log_cum)
 
     span_count = lax.axis_size("ctx")
     state_in = gather_scan(state_local, decay_local, span_count, 1)
@@ -193,11 +191,10 @@
     grad_decay = jnp.sum(state_in * grad_state, axis=-1)
     summary_grads = pull_summary((grad_state, grad_decay))
 
+    grad_logit, grad_bias = pull_decay(inner_grads[3] + summary_grads[2])
     grad_query = inner_grads[0]
     grad_key = inner_grads[1] + summary_grads[0]
     grad_value = inner_grads[2] + summary_grads[1]
-    grad_logit = inner_grads[3] + summary_grads[2]
-    grad_bias = inner_grads[4] + summary_grads[3]
     token_total = token_count * lax.axis_size("ctx") * lax.axis_size("rep")
     both_total = direct_sum(
         butterfly_sum(jnp.concatenate([grad_bias.reshape(-1), grad_weight.reshape(-1)]), "rep"),

time: 77.9 us -> 79.8 us (1.024)
  other arithmetic: 8.05 us -> 10.4 us
  starting transfers between devices: 18.4 us -> 16.6 us
  matrix products: 4.74 us -> 6.06 us
    another operation x3 -> x2, other arithmetic: 2.5 us -> 4.76 us  [running_decay(): return jnp.cumsum(log_decay(logit_in, bias_in), axis=0)]
    ppermute x3, starting transfers between devices: 3.81 us -> 2.02 us  [direct_sum(): terms.append(lax.ppermute(value, axis, pairs))]
    ppermute x3, waiting for transfers between devices: 0.01 us -> 1 us  [direct_sum(): terms.append(lax.ppermute(value, axis, pairs))]
    ppermute x4, waiting for transfers between devices: 34.5 us -> 33.6 us  [from_behind(): return lax.ppermute(value, axis, pairs)]
    unnamed x15 -> x19, local copies, waits for them, and re-layouts: 4.2 us -> 5.11 us
  transfers between devices with their start and end apart: 9 -> 9, of which waited for: 6 -> 7; matrix products, arithmetic and copies ran while one was open for 7% -> 8% of each run, Pallas kernels for 0% -> 0%
where the time goes in v13:
time: 79.8 us; the launch traced here: 79.5 us
  waiting for transfers between devices  37.3 us (47%)
  starting transfers between devices  16.6 us (21%)
  other arithmetic  10.4 us (13%)
  local copies, waits for them, and re-layouts  6.74 us (8%)
  matrix products  6.06 us (8%)
  between operations  2.43 us (3%)
    ppermute x4, waiting for transfers between devices, from_behind(): return lax.ppermute(value, axis, pairs)  33.6 us
    ppermute x4, starting transfers between devices, from_behind(): return lax.ppermute(value, axis, pairs)  12.9 us
    unnamed x19, local copies, waits for them, and re-layouts  5.11 us
    another operation x2, other arithmetic, running_decay(): return jnp.cumsum(log_decay(logit_in, bias_in), axis=0)  4.76 us
    ppermute x2, waiting for transfers between devices, butterfly_sum(): value = value + lax.ppermute(value, axis, pairs)  2.71 us
    ppermute x3, starting transfers between devices, direct_sum(): terms.append(lax.ppermute(value, axis, pairs))  2.02 us
    dot_general x3, matrix products, block_inner(): scores = jnp.einsum('ihc,jhc->hij', query_dec, key_dec, precision=highest)  1.77 us
    dot_general x3, matrix products, block_summary(): jnp.einsum('jhc,jhd->hcd', key_tail, value_in, precision=highest)  1.76 us
  transfers between devices with their start and end apart: 9, of which 7 were waited for; matrix products, arithmetic and copies ran while one was open for 8% of the time, Pallas kernels for 0%

profile of v13, /device:TPU:0, one launch (start us, length us, event | category | flops | bytes accessed | tf_op | source)
XLA Modules:
  0.0 79.5 jit_solution(2011448535100357787)
XLA Ops:
  0.6 0.6 copy-done.6
  1.4 0.2 broadcast_in_dim.37
  1.6 0.5 slice.77
  2.3 1.0 %pad_maximum_fusion = bf16[4,128,512]{2,1,0:T(8,128)(2,1)S(1)} fusion(bf16[1,128,512]{2,1,0:T(8,128)(2,1)S(1)} %copy-done.2, bf16[1,128,512]{2,1,0:T(8,128)(2,1)S(1)} %copy-done.3, bf16[1,128,512]{2,1,0:T(8,128)(2,1)} %param.14, bf16[1,128,512]{2,1,0:T(8,128)(2,1)} %param.13), kind=kLoop, calls=%fused_computation.23 | loop fusion | flops 786432 | bytes 1048576 | tf_op jit(solution)/shard_map/concatenate | solution.py:151
  3.5 0.6 copy-done.5
  4.1 0.3 fusion.15
  5.3 0.7 compare_convert_fusion.1
  6.1 0.3 multiply_reduce_fusion.1
  6.5 0.3 fusion.61
  6.8 4.9 %collective-permute-start = (f32[4,136,128]{2,1,0:T(8,128)S(1)}, f32[4,136,128]{2,1,0:T(8,128)S(1)}, u32[]{:S(2)}, u32[]{:S(2)}) collective-permute-start(f32[4,136,128]{2,1,0:T(8,128)S(1)} %fusion.9), channel_id=1, source_target_pairs={{0,4},{4,8},{8,12},{1,5},{5,9},{9,13},{2,6},{6,10},{10,14},{3,7},{... | collective-permute-start | bytes 835592 | tf_op jit(solution)/shard_map/ppermute | solution.py:18
  12.7 0.4 fusion.4
  13.1 4.5 %collective-permute-done = f32[4,136,128]{2,1,0:T(8,128)S(1)} collective-permute-done((f32[4,136,128]{2,1,0:T(8,128)S(1)}, f32[4,136,128]{2,1,0:T(8,128)S(1)}, u32[]{:S(2)}, u32[]{:S(2)}) %collective-permute-start) | collective-permute-done | bytes 278560 | tf_op jit(solution)/shard_map/ppermute | solution.py:18
  17.8 5.4 %collective-permute-start.1 = (f32[4,128,128]{2,1,0:T(8,128)S(1)}, f32[4,128,128]{2,1,0:T(8,128)S(1)}, u32[]{:S(2)}, u32[]{:S(2)}) collective-permute-start(f32[4,128,128]{2,1,0:T(8,128)S(1)} %multiply_add_fusion.4), channel_id=1, source_target_pairs={{0,8},{4,12},{1,9},{5,13},{2,10},{6,14},{3,11},{7,15},{16,24},{20,... | collective-permute-start | bytes 786440 | tf_op jit(solution)/shard_map/ppermute | solution.py:18
  23.3 0.2 fusion.77
  23.5 4.4 %collective-permute-done.1 = f32[4,128,128]{2,1,0:T(8,128)S(1)} collective-permute-done((f32[4,128,128]{2,1,0:T(8,128)S(1)}, f32[4,128,128]{2,1,0:T(8,128)S(1)}, u32[]{:S(2)}, u32[]{:S(2)}) %collective-permute-start.1) | collective-permute-done | bytes 262176 | tf_op jit(solution)/shard_map/ppermute | solution.py:18
  28.0 0.4 fusion.20
  28.5 0.6 copy-done.4
  29.2 0.2 convolution_bitcast_fusion.2
  29.3 1.5 %collective-permute-start.2 = (f32[128]{0:T(128)S(1)}, f32[128]{0:T(128)S(1)}, u32[]{:S(2)}, u32[]{:S(2)}) collective-permute-start(f32[128]{0:T(128)S(1)} %convolution_bitcast_fusion.2), channel_id=1, source_target_pairs={{0,2},{2,0},{1,3},{3,1},{4,6},{6,4},{5,7},{7,5},{8,10},{10,8},{9,1... | collective-permute-start | bytes 1544 | tf_op jit(solution)/shard_map/ppermute | solution.py:28
  30.9 2.0 %collective-permute-done.2 = f32[128]{0:T(128)S(1)} collective-permute-done((f32[128]{0:T(128)S(1)}, f32[128]{0:T(128)S(1)}, u32[]{:S(2)}, u32[]{:S(2)}) %collective-permute-start.2) | collective-permute-done | bytes 544 | tf_op jit(solution)/shard_map/ppermute | solution.py:28
  32.9 0.5 bitcast_subtract_fusion
  33.4 0.1 fusion.11
  33.6 0.5 fusion.29
  34.1 1.3 %collective-permute-start.3 = (f32[4,136,128]{2,1,0:T(8,128)S(1)}, f32[4,136,128]{2,1,0:T(8,128)S(1)}, u32[]{:S(2)}, u32[]{:S(2)}) collective-permute-start(f32[4,136,128]{2,1,0:T(8,128)S(1)} %fusion.10), channel_id=1, source_target_pairs={{4,0},{8,4},{12,8},{5,1},{9,5},{13,9},{6,2},{10,6},{14,10},{7,3},{... | collective-permute-start | bytes 835592 | tf_op jit(solution)/shard_map/ppermute | solution.py:18
  35.4 0.3 fusion.8
  35.7 0.3 fusion.6
  36.0 0.3 convolution_bitcast_fusion
  36.3 12.5 %collective-permute-done.3 = f32[4,136,128]{2,1,0:T(8,128)S(1)} collective-permute-done((f32[4,136,128]{2,1,0:T(8,128)S(1)}, f32[4,136,128]{2,1,0:T(8,128)S(1)}, u32[]{:S(2)}, u32[]{:S(2)}) %collective-permute-start.3) | collective-permute-done | bytes 278560 | tf_op jit(solution)/shard_map/ppermute | solution.py:18
  48.9 1.3 %collective-permute-start.4 = (f32[4,128,128]{2,1,0:T(8,128)S(1)}, f32[4,128,128]{2,1,0:T(8,128)S(1)}, u32[]{:S(2)}, u32[]{:S(2)}) collective-permute-start(f32[4,128,128]{2,1,0:T(8,128)S(1)} %multiply_add_fusion.2), channel_id=1, source_target_pairs={{8,0},{12,4},{9,1},{13,5},{10,2},{14,6},{11,3},{15,7},{24,16},{28,... | collective-permute-start | bytes 786440 | tf_op jit(solution)/shard_map/ppermute | solution.py:18
  50.2 0.2 fusion.68
  50.4 1.1 %convolution_bitcast_fusion.1 = f32[128,4,128]{0,2,1:T(8,128)} fusion(f32[4,128,128]{2,1,0:T(8,128)S(1)} %fusion.8, f32[128,4,128]{0,2,1:T(8,128)S(1)} %bitcast.99, f32[128,4,128]{0,2,1:T(8,128)S(1)} %copy.118), kind=kOutput, calls=%fused_computation.4 | convolution fusion | flops 50462720 | bytes 1048576 | tf_op jit(solution)/shard_map/transpose(jvp(ihc,jhc->hij))/dot_general | solution.py:107
  51.5 12.2 %collective-permute-done.4 = f32[4,128,128]{2,1,0:T(8,128)S(1)} collective-permute-done((f32[4,128,128]{2,1,0:T(8,128)S(1)}, f32[4,128,128]{2,1,0:T(8,128)S(1)}, u32[]{:S(2)}, u32[]{:S(2)}) %collective-permute-start.4) | collective-permute-done | bytes 262176 | tf_op jit(solution)/shard_map/ppermute | solution.py:18
  63.7 0.2 multiply_reduce_fusion
  64.0 1.0 %fusion.35 = (f32[4,128]{1,0:T(4,128)S(1)}, f32[128,4,128]{0,2,1:T(8,128)}) fusion(f32[128,4,128]{0,2,1:T(8,128)S(1)} %copy.118, f32[128,4,128]{0,2,1:T(8,128)S(1)} %bitcast.100, f32[4,128]{1,0:T(4,128)S(1)} %get-tuple-element.63, f32[128]{0:T(128)S(1)} %get-tuple-element.82, f32[4,128,128]{2,1,0:T(8,128)S(1)} %get-tuple-element.67, ...), kind=kOutput, calls=%fused_computation.77 | convolution fusion | flops 50658816 | bytes 1184256 | tf_op jit(solution)/shard_map/transpose(jvp(jhc,jhd->hcd))/dot_general | solution.py:125
  64.9 0.1 copy.137
  65.4 0.8 copy-done
  66.3 0.5 add_add_fusion.2
  66.9 4.4 %reduce_window_sum.34 = f32[1,128,512]{2,1,0:T(8,128)S(1)} reduce-window(f32[1,128,512]{2,1,0:T(8,128)S(1)} %copy.138, f32[]{:T(128)} %constant.123.clone.1), window={size=1x128x1 pad=0_0x0_127x0_0}, to_apply=%region_6.7 | reduce-window | flops 8323072 | bytes 524292 | tf_op jit(solution)/shard_map/transpose(jvp(jit(cumsum)))/reduce_window_sum | solution.py:166
  71.3 0.3 fusion.75
  71.7 0.5 fusion.5
  72.2 0.7 collective-permute-done.5
  73.0 1.9 %collective-permute-start.8 = (f32[1024]{0:T(1024)S(1)}, f32[1024]{0:T(1024)S(1)}, u32[]{:S(2)}, u32[]{:S(2)}) collective-permute-start(f32[1024]{0:T(1024)S(1)} %fusion.74), channel_id=1, source_target_pairs={{0,4},{4,8},{8,12},{12,0},{1,5},{5,9},{9,13},{13,1},{2,6},{6,10},{... | collective-permute-start | bytes 12296 | tf_op jit(solution)/shard_map/ppermute | solution.py:39
  74.9 0.7 negate_convert_fusion
  75.6 0.8 copy.141
  76.4 0.8 copy.139
  77.1 0.8 copy.140
  77.9 1.0 %collective-permute-done.8 = f32[1024]{0:T(1024)S(1)} collective-permute-done((f32[1024]{0:T(1024)S(1)}, f32[1024]{0:T(1024)S(1)}, u32[]{:S(2)}, u32[]{:S(2)}) %collective-permute-start.8) | collective-permute-done | bytes 4128 | tf_op jit(solution)/shard_map/ppermute | solution.py:39
  78.9 0.6 slice_multiply_fusion
  (48 shorter events, 2.3 us)
Async XLA Ops:
  0.6 0.7 copy-start.6
  1.3 0.9 %copy-start.2 = (bf16[1,128,512]{2,1,0:T(8,128)(2,1)S(1)}, bf16[1,128,512]{2,1,0:T(8,128)(2,1)}, u32[]{:S(2)}) copy-start(bf16[1,128,512]{2,1,0:T(8,128)(2,1)} %param.16) | copy-start | bytes 393220
  1.3 1.0 %copy-start.3 = (bf16[1,128,512]{2,1,0:T(8,128)(2,1)S(1)}, bf16[1,128,512]{2,1,0:T(8,128)(2,1)}, u32[]{:S(2)}) copy-start(bf16[1,128,512]{2,1,0:T(8,128)(2,1)} %param.15) | copy-start | bytes 393220
  3.4 0.7 copy-start.5
  6.8 10.8 %collective-permute-start = (f32[4,136,128]{2,1,0:T(8,128)S(1)}, f32[4,136,128]{2,1,0:T(8,128)S(1)}, u32[]{:S(2)}, u32[]{:S(2)}) collective-permute-start(f32[4,136,128]{2,1,0:T(8,128)S(1)} %fusion.9), channel_id=1, source_target_pairs={{0,4},{4,8},{8,12},{1,5},{5,9},{9,13},{2,6},{6,10},{10,14},{3,7},{... | collective-permute-start | bytes 835592 | tf_op jit(solution)/shard_map/ppermute | solution.py:18
  17.8 10.1 %collective-permute-start.1 = (f32[4,128,128]{2,1,0:T(8,128)S(1)}, f32[4,128,128]{2,1,0:T(8,128)S(1)}, u32[]{:S(2)}, u32[]{:S(2)}) collective-permute-start(f32[4,128,128]{2,1,0:T(8,128)S(1)} %multiply_add_fusion.4), channel_id=1, source_target_pairs={{0,8},{4,12},{1,9},{5,13},{2,10},{6,14},{3,11},{7,15},{16,24},{20,... | collective-permute-start | bytes 786440 | tf_op jit(solution)/shard_map/ppermute | solution.py:18
  28.5 0.7 copy-start.4
  29.3 3.6 %collective-permute-start.2 = (f32[128]{0:T(128)S(1)}, f32[128]{0:T(128)S(1)}, u32[]{:S(2)}, u32[]{:S(2)}) collective-permute-start(f32[128]{0:T(128)S(1)} %convolution_bitcast_fusion.2), channel_id=1, source_target_pairs={{0,2},{2,0},{1,3},{3,1},{4,6},{6,4},{5,7},{7,5},{8,10},{10,8},{9,1... | collective-permute-start | bytes 1544 | tf_op jit(solution)/shard_map/ppermute | solution.py:28
  30.9 2.1 %copy-start.7 = (f32[1,128]{1,0:T(1,128)S(1)}, f32[1,128]{1,0:T(1,128)}, u32[]{:S(2)}) copy-start(f32[1,128]{1,0:T(1,128)} %param.19) | copy-start | bytes 1540
  34.1 14.6 %collective-permute-start.3 = (f32[4,136,128]{2,1,0:T(8,128)S(1)}, f32[4,136,128]{2,1,0:T(8,128)S(1)}, u32[]{:S(2)}, u32[]{:S(2)}) collective-permute-start(f32[4,136,128]{2,1,0:T(8,128)S(1)} %fusion.10), channel_id=1, source_target_pairs={{4,0},{8,4},{12,8},{5,1},{9,5},{13,9},{6,2},{10,6},{14,10},{7,3},{... | collective-permute-start | bytes 835592 | tf_op jit(solution)/shard_map/ppermute | solution.py:18
  48.9 14.8 %collective-permute-start.4 = (f32[4,128,128]{2,1,0:T(8,128)S(1)}, f32[4,128,128]{2,1,0:T(8,128)S(1)}, u32[]{:S(2)}, u32[]{:S(2)}) collective-permute-start(f32[4,128,128]{2,1,0:T(8,128)S(1)} %multiply_add_fusion.2), channel_id=1, source_target_pairs={{8,0},{12,4},{9,1},{13,5},{10,2},{14,6},{11,3},{15,7},{24,16},{28,... | collective-permute-start | bytes 786440 | tf_op jit(solution)/shard_map/ppermute | solution.py:18
  65.3 1.0 %copy-start = (f32[128,4,128]{0,2,1:T(8,128)S(1)}, f32[128,4,128]{0,2,1:T(8,128)}, u32[]{:S(2)}) copy-start(f32[128,4,128]{0,2,1:T(8,128)} %convolution_bitcast_fusion.1) | copy-start | bytes 786436
  65.3 1.0 %copy-start.1 = (f32[128,4,128]{0,2,1:T(8,128)S(1)}, f32[128,4,128]{0,2,1:T(8,128)}, u32[]{:S(2)}) copy-start(f32[128,4,128]{0,2,1:T(8,128)} %get-tuple-element.86) | copy-start | bytes 786436
  71.6 1.2 %collective-permute-start.5 = (f32[1024]{0:T(1024)S(1)}, f32[1024]{0:T(1024)S(1)}, u32[]{:S(2)}, u32[]{:S(2)}) collective-permute-start(f32[1024]{0:T(1024)S(1)} %pad_maximum_fusion.1), channel_id=1, source_target_pairs={{0,1},{1,0},{2,3},{3,2},{4,5},{5,4},{6,7},{7,6},{8,9},{9,8},{10,11... | collective-permute-start | bytes 12296 | tf_op jit(solution)/shard_map/ppermute | solution.py:28
  72.9 5.0 %collective-permute-start.6 = (f32[1024]{0:T(1024)S(1)}, f32[1024]{0:T(1024)S(1)}, u32[]{:S(2)}, u32[]{:S(2)}) collective-permute-start(f32[1024]{0:T(1024)S(1)} %fusion.74), channel_id=1, source_target_pairs={{0,12},{4,0},{8,4},{12,8},{1,13},{5,1},{9,5},{13,9},{2,14},{6,2},{... | collective-permute-start | bytes 12296 | tf_op jit(solution)/shard_map/ppermute | solution.py:39
  72.9 5.0 %collective-permute-start.7 = (f32[1024]{0:T(1024)S(1)}, f32[1024]{0:T(1024)S(1)}, u32[]{:S(2)}, u32[]{:S(2)}) collective-permute-start(f32[1024]{0:T(1024)S(1)} %fusion.74), channel_id=1, source_target_pairs={{0,8},{4,12},{8,0},{12,4},{1,9},{5,13},{9,1},{13,5},{2,10},{6,14},... | collective-permute-start | bytes 12296 | tf_op jit(solution)/shard_map/ppermute | solution.py:39
  73.0 5.9 %collective-permute-start.8 = (f32[1024]{0:T(1024)S(1)}, f32[1024]{0:T(1024)S(1)}, u32[]{:S(2)}, u32[]{:S(2)}) collective-permute-start(f32[1024]{0:T(1024)S(1)} %fusion.74), channel_id=1, source_target_pairs={{0,4},{4,8},{8,12},{12,0},{1,5},{5,9},{9,13},{13,1},{2,6},{6,10},{... | collective-permute-start | bytes 12296 | tf_op jit(solution)/shard_map/ppermute | solution.py:39

commit v14 on v10

--- a/solution.py
+++ b/solution.py
@@ -50,25 +50,27 @@
     return total
 
 
-def pack_state(state, factor):
-    rows = jnp.zeros((state.shape[0], 8, state.shape[2]), state.dtype)
-    rows = rows.at[:, 0, :].set(factor)
-    return jnp.concatenate([state, rows], axis=1)
-
-
-def gather_scan(state, factor, span_count, direction):
-    channels = state.shape[1]
+def factor_runs(factor, span_count, direction):
+    runs = []
+    run_b = factor
+    shift = 1
+    while 2 * shift < span_count:
+        far_b = from_behind(run_b, "ctx", direction * shift)
+        runs.append(far_b)
+        run_b = far_b * run_b
+        shift *= 2
+    return runs
+
+
+def gather_scan(state, factor, span_count, direction, far_factors):
     near_a, near_b = None, None
     run_a, run_b = state, factor
     shift = 1
+    round_index = 0
     while shift < span_count:
         last = 2 * shift >= span_count
-        if last:
-            far = from_behind(run_a, "ctx", direction * shift)
-            far_a, far_b = far, None
-        else:
-            far = from_behind(pack_state(run_a, factor=run_b), "ctx", direction * shift)
-            far_a, far_b = far[:, :channels], far[:, channels, :]
+        far_a = from_behind(run_a, "ctx", direction * shift)
+        far_b = None if last else far_factors[round_index]
         if near_a is None:
             near_a, near_b = far_a, far_b
         else:
@@ -78,6 +80,7 @@
             run_a = far_a * run_b[..., None] + run_a
             run_b = far_b * run_b
         shift *= 2
+        round_index += 1
     if near_a is None:
         return jnp.zeros_like(state)
     return near_a
@@ -172,7 +175,9 @@
     )
 
     span_count = lax.axis_size("ctx")
-    state_in = gather_scan(state_local, decay_local, span_count, 1)
+    forward_runs = factor_runs(decay_local, span_count, 1)
+    backward_runs = factor_runs(decay_local, span_count, -1)
+    state_in = gather_scan(state_local, decay_local, span_count, 1, forward_runs)
     attended = attended_local + jnp.einsum("thc,hcd->thd", carried, state_in, precision=highest)
 
     def value_head(attended_in, weight_in):
@@ -189,7 +194,7 @@
     grad_direct = jnp.einsum("thc,thd->hcd", carried, grad_attended, precision=highest)
     inner_grads = pull_inner((grad_attended, grad_carried))
 
-    grad_state = gather_scan(grad_direct, decay_local, span_count, -1)
+    grad_state = gather_scan(grad_direct, decay_local, span_count, -1, backward_runs)
     grad_decay = jnp.sum(state_in * grad_state, axis=-1)
     summary_grads = pull_summary((grad_state, grad_decay))
 

time: 77.9 us -> 82.1 us (1.054)
  waiting for transfers between devices: 37.2 us -> 26.4 us
  other arithmetic: 8.05 us -> 14 us
  starting transfers between devices: 18.4 us -> 24 us
  local copies, waits for them, and re-layouts: 6.72 us -> 8.96 us
  matrix products: 4.74 us -> 5.68 us
    ppermute x4 -> x6, waiting for transfers between devices: 34.5 us -> 23.5 us  [from_behind(): return lax.ppermute(value, axis, pairs)]
    ppermute x4 -> x6, starting transfers between devices: 12.9 us -> 18.5 us  [from_behind(): return lax.ppermute(value, axis, pairs)]
    reduce_sum x1, other arithmetic: 0.25 us -> 1.85 us  [on_device(): grad_decay = jnp.sum(state_in * grad_state, axis=-1)]
    convert_element_type x1 -> x3, local copies, waits for them, and re-layouts: 0.71 us -> 2.13 us  [to_rows(): return array.reshape(1, token_count, -1).astype(jnp.bfloat16)]
    add x2, other arithmetic: 0.26 us -> 1.68 us  [gather_scan(): run_a = far_a * run_b[..., None] + run_a]
    another operation x2, other arithmetic: 1.43 us -> 2.43 us  [block_inner(): log_cum = jnp.cumsum(log_decay(logit_in, bias_in), axis=0)]
    add x1, other arithmetic: 0.13 us -> 1.08 us  [gather_scan(): near_a = far_a * near_b[..., None] + near_a]
    unnamed x15 -> x35, local copies, waits for them, and re-layouts: 4.2 us -> 4.81 us
  transfers between devices with their start and end apart: 9 -> 11, of which waited for: 6 -> 5; matrix products, arithmetic and copies ran while one was open for 7% -> 15% of each run, Pallas kernels for 0% -> 0%
where the time goes in v14:
time: 82.1 us; the launch traced here: 81.6 us
  waiting for transfers between devices  26.4 us (32%)
  starting transfers between devices  24 us (29%)
  other arithmetic  14 us (17%)
  local copies, waits for them, and re-layouts  8.96 us (11%)
  matrix products  5.68 us (7%)
  between operations  2.49 us (3%)
    ppermute x6, waiting for transfers between devices, from_behind(): return lax.ppermute(value, axis, pairs)  23.5 us
    ppermute x6, starting transfers between devices, from_behind(): return lax.ppermute(value, axis, pairs)  18.5 us
    unnamed x35, local copies, waits for them, and re-layouts  4.81 us
    ppermute x3, starting transfers between devices, direct_sum(): terms.append(lax.ppermute(value, axis, pairs))  3.81 us
    ppermute x2, waiting for transfers between devices, butterfly_sum(): value = value + lax.ppermute(value, axis, pairs)  2.94 us
    another operation x2, other arithmetic, block_inner(): log_cum = jnp.cumsum(log_decay(logit_in, bias_in), axis=0)  2.43 us
    convert_element_type x3, local copies, waits for them, and re-layouts, to_rows(): return array.reshape(1, token_count, -1).astype(jnp.bfloat16)  2.13 us
    reduce_sum x1, other arithmetic, on_device(): grad_decay = jnp.sum(state_in * grad_state, axis=-1)  1.85 us
  transfers between devices with their start and end apart: 11, of which 5 were waited for; matrix products, arithmetic and copies ran while one was open for 15% of the time, Pallas kernels for 0%

profile of v14, /device:TPU:0, one launch (start us, length us, event | category | flops | bytes accessed | tf_op | source)
XLA Modules:
  0.0 81.6 jit_solution(7080431753242956504)
XLA Ops:
  0.6 0.6 copy-done.15
  1.6 0.5 slice.31
  2.2 1.2 %compare_convert_fusion.1 = (f32[128]{0:T(128)}, f32[128]{0:T(128)S(1)}) fusion(s32[128]{0:T(128)S(1)} %reduce, s32[]{:T(128)} %bitcast.6), kind=kLoop, calls=%fused_computation.113 | loop fusion | flops 512 | bytes 1540 | tf_op jit(solution)/shard_map/jvp()/convert_element_type | solution.py:102
  3.4 1.0 %pad_maximum_fusion = bf16[4,128,512]{2,1,0:T(8,128)(2,1)S(1)} fusion(bf16[1,128,512]{2,1,0:T(8,128)(2,1)S(1)} %copy-done.3, bf16[1,128,512]{2,1,0:T(8,128)(2,1)S(1)} %copy-done.4, bf16[1,128,512]{2,1,0:T(8,128)(2,1)} %param.11, bf16[1,128,512]{2,1,0:T(8,128)(2,1)} %param.10), kind=kLoop, calls=%fused_computation.14 | loop fusion | flops 786432 | bytes 1048576 | tf_op jit(solution)/shard_map/concatenate | solution.py:156
  4.8 0.6 copy-done.7
  5.4 0.3 fusion.19
  5.9 0.5 copy-done.9
  6.4 0.4 broadcast_multiply_fusion
  6.7 0.3 fusion.30
  7.0 4.9 %collective-permute-start = (f32[4,128,128]{2,1,0:T(8,128)S(1)}, f32[4,128,128]{2,1,0:T(8,128)S(1)}, u32[]{:S(2)}, u32[]{:S(2)}) collective-permute-start(f32[4,128,128]{2,1,0:T(8,128)S(1)} %fusion.30), channel_id=1, source_target_pairs={{0,4},{4,8},{8,12},{1,5},{5,9},{9,13},{2,6},{6,10},{10,14},{3,7},{... | collective-permute-start | bytes 786440 | tf_op jit(solution)/shard_map/ppermute | solution.py:18
  12.7 1.3 %collective-permute-start.6 = (f32[4,128]{1,0:T(4,128)S(1)}, f32[4,128]{1,0:T(4,128)S(1)}, u32[]{:S(2)}, u32[]{:S(2)}) collective-permute-start(f32[4,128]{1,0:T(4,128)S(1)} %exponential_multiply_fusion.1), channel_id=1, source_target_pairs={{4,0},{8,4},{12,8},{5,1},{9,5},{13,9},{6,2},{10,6},{14,10},{7,3},{... | collective-permute-start | bytes 6152 | tf_op jit(solution)/shard_map/ppermute | solution.py:18
  14.0 4.5 %collective-permute-start.2 = (f32[4,128]{1,0:T(4,128)S(1)}, f32[4,128]{1,0:T(4,128)S(1)}, u32[]{:S(2)}, u32[]{:S(2)}) collective-permute-start(f32[4,128]{1,0:T(4,128)S(1)} %exponential_multiply_fusion.1), channel_id=1, source_target_pairs={{0,4},{4,8},{8,12},{1,5},{5,9},{9,13},{2,6},{6,10},{10,14},{3,7},{... | collective-permute-start | bytes 6152 | tf_op jit(solution)/shard_map/ppermute | solution.py:18
  19.6 0.8 %multiply_add_fusion.3 = f32[4,128,128]{2,1,0:T(8,128)} fusion(f32[4,128,128]{2,1,0:T(8,128)S(1)} %fusion.30, f32[4,128,128]{2,1,0:T(8,128)S(1)} %collective-permute-done, f32[4,128]{1,0:T(4,128)S(1)} %exponential_multiply_fusion.1), kind=kLoop, calls=%fused_computation.57 | loop fusion | flops 131072 | bytes 788480 | tf_op jit(solution)/shard_map/add | solution.py:80
  20.4 5.2 %collective-permute-start.1 = (f32[4,128,128]{2,1,0:T(8,128)}, f32[4,128,128]{2,1,0:T(8,128)}, u32[]{:S(2)}, u32[]{:S(2)}) collective-permute-start(f32[4,128,128]{2,1,0:T(8,128)} %multiply_add_fusion.3), channel_id=1, source_target_pairs={{0,8},{4,12},{1,9},{5,13},{2,10},{6,14},{3,11},{7,15},{16,24},{20,... | collective-permute-start | bytes 786440 | tf_op jit(solution)/shard_map/ppermute | solution.py:18
  25.6 0.4 fusion
  26.4 3.5 %collective-permute-done.1 = f32[4,128,128]{2,1,0:T(8,128)} collective-permute-done((f32[4,128,128]{2,1,0:T(8,128)}, f32[4,128,128]{2,1,0:T(8,128)}, u32[]{:S(2)}, u32[]{:S(2)}) %collective-permute-start.1) | collective-permute-done | bytes 262176 | tf_op jit(solution)/shard_map/ppermute | solution.py:18
  30.0 1.1 %multiply_add_fusion.2 = f32[4,128,128]{2,1,0:T(8,128)S(1)} fusion(f32[4,128,128]{2,1,0:T(8,128)S(1)} %collective-permute-done, f32[4,128,128]{2,1,0:T(8,128)} %collective-permute-done.1, f32[4,128]{1,0:T(4,128)S(1)} %collective-permute-done.2), kind=kLoop, calls=%fused_computation.56 | loop fusion | flops 131072 | bytes 788480 | tf_op jit(solution)/shard_map/add | solution.py:77
  31.0 0.4 fusion.18
  31.5 0.6 copy-done.5
  32.3 1.5 %collective-permute-start.3 = (f32[128]{0:T(128)S(1)}, f32[128]{0:T(128)S(1)}, u32[]{:S(2)}, u32[]{:S(2)}) collective-permute-start(f32[128]{0:T(128)S(1)} %convolution_bitcast_fusion), channel_id=1, source_target_pairs={{0,2},{2,0},{1,3},{3,1},{4,6},{6,4},{5,7},{7,5},{8,10},{10,8},{9,1... | collective-permute-start | bytes 1544 | tf_op jit(solution)/shard_map/ppermute | solution.py:28
  33.9 2.0 %collective-permute-done.3 = f32[128]{0:T(128)S(1)} collective-permute-done((f32[128]{0:T(128)S(1)}, f32[128]{0:T(128)S(1)}, u32[]{:S(2)}, u32[]{:S(2)}) %collective-permute-start.3) | collective-permute-done | bytes 544 | tf_op jit(solution)/shard_map/ppermute | solution.py:28
  35.9 0.5 bitcast_subtract_fusion
  36.6 0.5 fusion.34
  37.1 1.3 %collective-permute-start.4 = (f32[4,128,128]{2,1,0:T(8,128)S(1)}, f32[4,128,128]{2,1,0:T(8,128)S(1)}, u32[]{:S(2)}, u32[]{:S(2)}) collective-permute-start(f32[4,128,128]{2,1,0:T(8,128)S(1)} %fusion.34), channel_id=1, source_target_pairs={{4,0},{8,4},{12,8},{5,1},{9,5},{13,9},{6,2},{10,6},{14,10},{7,3},{... | collective-permute-start | bytes 786440 | tf_op jit(solution)/shard_map/ppermute | solution.py:18
  38.4 0.3 fusion.4
  38.7 0.3 fusion.72
  39.0 1.1 %fusion.35 = f32[4,128,128]{2,1,0:T(8,128)} fusion(f32[4,128,128]{2,1,0:T(8,128)S(1)} %multiply_add_fusion.2, f32[4,128,128]{2,1,0:T(8,128)S(1)} %get-tuple-element.67, f32[128,4]{0,1:T(4,128)S(1)} %multiply_multiply_fusion.3, f32[4,128]{1,0:T(4,128)S(1)} %bitcast.144, f32[128]{0:T(128)S(1)} %get-tuple-element.62, f32[128,4]{0,1:T(4,128)S(1)} %fusion.59), kind=kOutput, calls=%fused_computation.68 | convolution fusion | flops 50659328 | bytes 793088 | tf_op jit(solution)/shard_map/thd,hcd->thc/dot_general | solution.py:193
  40.1 9.3 %collective-permute-done.4 = f32[4,128,128]{2,1,0:T(8,128)S(1)} collective-permute-done((f32[4,128,128]{2,1,0:T(8,128)S(1)}, f32[4,128,128]{2,1,0:T(8,128)S(1)}, u32[]{:S(2)}, u32[]{:S(2)}) %collective-permute-start.4) | collective-permute-done | bytes 262176 | tf_op jit(solution)/shard_map/ppermute | solution.py:18
  49.3 0.8 %multiply_add_fusion.1 = f32[4,128,128]{2,1,0:T(8,128)} fusion(f32[4,128,128]{2,1,0:T(8,128)S(1)} %fusion.34, f32[4,128,128]{2,1,0:T(8,128)S(1)} %collective-permute-done.4, f32[4,128]{1,0:T(4,128)S(1)} %exponential_multiply_fusion.1), kind=kLoop, calls=%fused_computation.54 | loop fusion | flops 131072 | bytes 788480 | tf_op jit(solution)/shard_map/add | solution.py:80
  50.2 1.3 %collective-permute-start.5 = (f32[4,128,128]{2,1,0:T(8,128)}, f32[4,128,128]{2,1,0:T(8,128)}, u32[]{:S(2)}, u32[]{:S(2)}) collective-permute-start(f32[4,128,128]{2,1,0:T(8,128)} %multiply_add_fusion.1), channel_id=1, source_target_pairs={{8,0},{12,4},{9,1},{13,5},{10,2},{14,6},{11,3},{15,7},{24,16},{28,... | collective-permute-start | bytes 786440 | tf_op jit(solution)/shard_map/ppermute | solution.py:18
  51.5 0.4 fusion.71
  51.9 0.8 fusion.60
  53.3 10.7 %collective-permute-done.5 = f32[4,128,128]{2,1,0:T(8,128)} collective-permute-done((f32[4,128,128]{2,1,0:T(8,128)}, f32[4,128,128]{2,1,0:T(8,128)}, u32[]{:S(2)}, u32[]{:S(2)}) %collective-permute-start.5) | collective-permute-done | bytes 262176 | tf_op jit(solution)/shard_map/ppermute | solution.py:18
  64.0 1.9 %multiply_reduce_fusion = (f32[4,128]{1,0:T(4,128)}, f32[4,128,128]{2,1,0:T(8,128)S(1)}) fusion(f32[4,128,128]{2,1,0:T(8,128)S(1)} %multiply_add_fusion.2, f32[4,128,128]{2,1,0:T(8,128)} %copy-done, f32[4,128,128]{2,1,0:T(8,128)} %collective-permute-done.5, f32[4,128]{1,0:T(4,128)S(1)} %collective-permute-done.6), kind=kLoop, calls=%fused_computation.48 | loop fusion | flops 261632 | bytes 1052672 | tf_op jit(solution)/shard_map/reduce_sum | solution.py:198
  66.2 0.5 copy-done.10
  66.9 1.0 %fusion.67 = (f32[4,128]{1,0:T(4,128)S(1)}, f32[128,4,128]{2,1,0:T(4,128)S(1)}, bf16[128,4,128]{2,1,0:T(4,128)(2,1)}, bf16[128,4,128]{2,1,0:T(4,128)(2,1)S(1)}) fusion(f32[128,4,128]{2,1,0:T(4,128)S(1)} %fusion.19, f32[4,128]{1,0:T(4,128)S(1)} %copy-done.10, f32[128,4,128]{2,1,0:T(4,128)S(1)} %reshape.219, f32[4,128,128]{1,0,2:T(4,128)S(1)} %copy.114, ...), kind=kLoop, calls=%fused_computation.124 | loop fusion | flops 982528 | bytes 2102272 | tf_op jit(solution)/shard_map/transpose(jvp())/reduce_sum | solution.py:129
  67.9 0.7 copy-done.11
  68.6 1.6 %negate_multiply_fusion.2 = f32[128,4,128]{2,1,0:T(4,128)S(1)} fusion(f32[1,4,128]{2,1,0:T(4,128)S(1)} %bitcast_add_fusion.1, f32[128,4,128]{2,1,0:T(4,128)S(1)} %get-tuple-element.42, f32[128,4,128]{2,1,0:T(4,128)S(1)} %reshape.218, f32[4,128]{1,0:T(4,128)S(1)} %bitcast.149), kind=kOutput, calls=%fused_computation.44 | output fusion | flops 9502720 | bytes 790528 | tf_op jit(solution)/shard_map/transpose(jvp(jit(cumsum)))/reduce_window_sum | solution.py:124
  70.3 2.1 %fusion.69 = (f32[4,128]{1,0:T(4,128)S(1)}, bf16[128,4,128]{2,1,0:T(4,128)(2,1)S(1)}, f32[4,128]{1,0:T(4,128)S(1)}) fusion(f32[128,4,128]{2,1,0:T(4,128)S(1)} %negate_multiply_fusion.2, f32[128,4,128]{2,1,0:T(4,128)S(1)} %reshape.218, f32[4,128]{1,0:T(4,128)S(1)} %bitcast.150, f32[128,4,128]{2,1,0:T(4,128)S(1)} %reshape.219, ...), kind=kOutput, calls=%fused_computation.125 | output fusion | flops 10419200 | bytes 2234880 | tf_op jit(solution)/shard_map/transpose(jvp(jit(cumsum)))/reduce_window_sum | solution.py:100
  72.5 0.3 fusion.2
  72.7 0.9 %collective-permute-done.7 = f32[1024]{0:T(1024)S(1)} collective-permute-done((f32[1024]{0:T(1024)S(1)}, f32[1024]{0:T(1024)S(1)}, u32[]{:S(2)}, u32[]{:S(2)}) %collective-permute-start.7) | collective-permute-done | bytes 4128 | tf_op jit(solution)/shard_map/ppermute | solution.py:28
  73.7 3.7 %collective-permute-start.8 = (f32[1024]{0:T(1024)S(1)}, f32[1024]{0:T(1024)S(1)}, u32[]{:S(2)}, u32[]{:S(2)}) collective-permute-start(f32[1024]{0:T(1024)S(1)} %fusion.65), channel_id=1, source_target_pairs={{0,12},{4,0},{8,4},{12,8},{1,13},{5,1},{9,5},{13,9},{2,14},{6,2},{... | collective-permute-start | bytes 12296 | tf_op jit(solution)/shard_map/ppermute | solution.py:39
  77.5 0.4 fusion.1
  77.8 0.8 copy.117
  78.6 0.7 convert_element_type.135
  79.5 0.7 convert_element_type.128
  80.2 0.7 convert_element_type.126
  81.0 0.6 slice_multiply_fusion
  (69 shorter events, 3.5 us)
Async XLA Ops:
  0.6 0.7 copy-start.15
  1.3 2.1 %copy-start.3 = (bf16[1,128,512]{2,1,0:T(8,128)(2,1)S(1)}, bf16[1,128,512]{2,1,0:T(8,128)(2,1)}, u32[]{:S(2)}) copy-start(bf16[1,128,512]{2,1,0:T(8,128)(2,1)} %param.13) | copy-start | bytes 393220
  1.3 2.1 %copy-start.4 = (bf16[1,128,512]{2,1,0:T(8,128)(2,1)S(1)}, bf16[1,128,512]{2,1,0:T(8,128)(2,1)}, u32[]{:S(2)}) copy-start(bf16[1,128,512]{2,1,0:T(8,128)(2,1)} %param.12) | copy-start | bytes 393220
  3.4 2.5 %copy-start.13 = (f32[128]{0:T(128)}, f32[128]{0:T(128)S(1)}, u32[]{:S(2)}) copy-start(f32[128]{0:T(128)S(1)} %get-tuple-element.65) | copy-start | bytes 1540
  4.7 0.7 copy-start.7
  5.8 0.6 copy-start.9
  7.0 12.5 %collective-permute-start = (f32[4,128,128]{2,1,0:T(8,128)S(1)}, f32[4,128,128]{2,1,0:T(8,128)S(1)}, u32[]{:S(2)}, u32[]{:S(2)}) collective-permute-start(f32[4,128,128]{2,1,0:T(8,128)S(1)} %fusion.30), channel_id=1, source_target_pairs={{0,4},{4,8},{8,12},{1,5},{5,9},{9,13},{2,6},{6,10},{10,14},{3,7},{... | collective-permute-start | bytes 786440 | tf_op jit(solution)/shard_map/ppermute | solution.py:18
  12.7 40.6 %collective-permute-start.6 = (f32[4,128]{1,0:T(4,128)S(1)}, f32[4,128]{1,0:T(4,128)S(1)}, u32[]{:S(2)}, u32[]{:S(2)}) collective-permute-start(f32[4,128]{1,0:T(4,128)S(1)} %exponential_multiply_fusion.1), channel_id=1, source_target_pairs={{4,0},{8,4},{12,8},{5,1},{9,5},{13,9},{6,2},{10,6},{14,10},{7,3},{... | collective-permute-start | bytes 6152 | tf_op jit(solution)/shard_map/ppermute | solution.py:18
  14.0 12.5 %collective-permute-start.2 = (f32[4,128]{1,0:T(4,128)S(1)}, f32[4,128]{1,0:T(4,128)S(1)}, u32[]{:S(2)}, u32[]{:S(2)}) collective-permute-start(f32[4,128]{1,0:T(4,128)S(1)} %exponential_multiply_fusion.1), channel_id=1, source_target_pairs={{0,4},{4,8},{8,12},{1,5},{5,9},{9,13},{2,6},{6,10},{10,14},{3,7},{... | collective-permute-start | bytes 6152 | tf_op jit(solution)/shard_map/ppermute | solution.py:18
  20.4 9.5 %collective-permute-start.1 = (f32[4,128,128]{2,1,0:T(8,128)}, f32[4,128,128]{2,1,0:T(8,128)}, u32[]{:S(2)}, u32[]{:S(2)}) collective-permute-start(f32[4,128,128]{2,1,0:T(8,128)} %multiply_add_fusion.3), channel_id=1, source_target_pairs={{0,8},{4,12},{1,9},{5,13},{2,10},{6,14},{3,11},{7,15},{16,24},{20,... | collective-permute-start | bytes 786440 | tf_op jit(solution)/shard_map/ppermute | solution.py:18
  31.5 0.7 copy-start.5
  32.3 3.6 %collective-permute-start.3 = (f32[128]{0:T(128)S(1)}, f32[128]{0:T(128)S(1)}, u32[]{:S(2)}, u32[]{:S(2)}) collective-permute-start(f32[128]{0:T(128)S(1)} %convolution_bitcast_fusion), channel_id=1, source_target_pairs={{0,2},{2,0},{1,3},{3,1},{4,6},{6,4},{5,7},{7,5},{8,10},{10,8},{9,1... | collective-permute-start | bytes 1544 | tf_op jit(solution)/shard_map/ppermute | solution.py:28
  33.9 2.1 %copy-start.16 = (f32[1,128]{1,0:T(1,128)S(1)}, f32[1,128]{1,0:T(1,128)}, u32[]{:S(2)}) copy-start(f32[1,128]{1,0:T(1,128)} %param.16) | copy-start | bytes 1540
  37.1 12.2 %collective-permute-start.4 = (f32[4,128,128]{2,1,0:T(8,128)S(1)}, f32[4,128,128]{2,1,0:T(8,128)S(1)}, u32[]{:S(2)}, u32[]{:S(2)}) collective-permute-start(f32[4,128,128]{2,1,0:T(8,128)S(1)} %fusion.34), channel_id=1, source_target_pairs={{4,0},{8,4},{12,8},{5,1},{9,5},{13,9},{6,2},{10,6},{14,10},{7,3},{... | collective-permute-start | bytes 786440 | tf_op jit(solution)/shard_map/ppermute | solution.py:18
  49.3 0.8 %copy-start = (f32[4,128,128]{2,1,0:T(8,128)}, f32[4,128,128]{2,1,0:T(8,128)S(1)}, u32[]{:S(2)}) copy-start(f32[4,128,128]{2,1,0:T(8,128)S(1)} %collective-permute-done.4) | copy-start | bytes 786436
  50.2 13.8 %collective-permute-start.5 = (f32[4,128,128]{2,1,0:T(8,128)}, f32[4,128,128]{2,1,0:T(8,128)}, u32[]{:S(2)}, u32[]{:S(2)}) collective-permute-start(f32[4,128,128]{2,1,0:T(8,128)} %multiply_add_fusion.1), channel_id=1, source_target_pairs={{8,0},{12,4},{9,1},{13,5},{10,2},{14,6},{11,3},{15,7},{24,16},{28,... | collective-permute-start | bytes 786440 | tf_op jit(solution)/shard_map/ppermute | solution.py:18
  51.8 1.0 %copy-start.1 = (f32[4,128,128]{2,1,0:T(8,128)S(1)}, f32[4,128,128]{2,1,0:T(8,128)}, u32[]{:S(2)}) copy-start(f32[4,128,128]{2,1,0:T(8,128)} %fusion.35) | copy-start | bytes 786436
  66.0 0.7 copy-start.10
  66.2 0.7 copy-start.12
  66.2 0.7 copy-start.14
  66.9 1.7 %copy-start.8 = (f32[512]{0:T(512)S(1)}, f32[512]{0:T(512)}, u32[]{:S(2)}) copy-start(f32[512]{0:T(512)} %param.14) | copy-start | bytes 6148
  67.9 0.7 copy-start.11
  70.2 2.1 %copy-start.6 = (f32[1,512]{1,0:T(1,128)S(1)}, f32[1,512]{1,0:T(1,128)}, u32[]{:S(2)}) copy-start(f32[1,512]{1,0:T(1,128)} %fusion.60) | copy-start | bytes 6148
  72.4 1.2 %collective-permute-start.7 = (f32[1024]{0:T(1024)S(1)}, f32[1024]{0:T(1024)S(1)}, u32[]{:S(2)}, u32[]{:S(2)}) collective-permute-start(f32[1024]{0:T(1024)S(1)} %pad_maximum_fusion.1), channel_id=1, source_target_pairs={{0,1},{1,0},{2,3},{3,2},{4,5},{5,4},{6,7},{7,6},{8,9},{9,8},{10,11... | collective-permute-start | bytes 12296 | tf_op jit(solution)/shard_map/ppermute | solution.py:28
  73.6 7.3 %collective-permute-start.10 = (f32[1024]{0:T(1024)S(1)}, f32[1024]{0:T(1024)S(1)}, u32[]{:S(2)}, u32[]{:S(2)}) collective-permute-start(f32[1024]{0:T(1024)S(1)} %fusion.65), channel_id=1, source_target_pairs={{0,4},{4,8},{8,12},{12,0},{1,5},{5,9},{9,13},{13,1},{2,6},{6,10},{... | collective-permute-start | bytes 12296 | tf_op jit(solution)/shard_map/ppermute | solution.py:39
  73.6 7.3 %collective-permute-start.9 = (f32[1024]{0:T(1024)S(1)}, f32[1024]{0:T(1024)S(1)}, u32[]{:S(2)}, u32[]{:S(2)}) collective-permute-start(f32[1024]{0:T(1024)S(1)} %fusion.65), channel_id=1, source_target_pairs={{0,8},{4,12},{8,0},{12,4},{1,9},{5,13},{9,1},{13,5},{2,10},{6,14},... | collective-permute-start | bytes 12296 | tf_op jit(solution)/shard_map/ppermute | solution.py:39
  73.7 7.2 %collective-permute-start.8 = (f32[1024]{0:T(1024)S(1)}, f32[1024]{0:T(1024)S(1)}, u32[]{:S(2)}, u32[]{:S(2)}) collective-permute-start(f32[1024]{0:T(1024)S(1)} %fusion.65), channel_id=1, source_target_pairs={{0,12},{4,0},{8,4},{12,8},{1,13},{5,1},{9,5},{13,9},{2,14},{6,2},{... | collective-permute-start | bytes 12296 | tf_op jit(solution)/shard_map/ppermute | solution.py:39
  78.6 0.9 %copy-start.2 = (bf16[128,4,128]{2,1,0:T(4,128)(2,1)S(1)}, bf16[128,4,128]{2,1,0:T(4,128)(2,1)}, u32[]{:S(2)}) copy-start(bf16[128,4,128]{2,1,0:T(4,128)(2,1)} %get-tuple-element.43) | copy-start | bytes 393220

commit v15 on v10

--- a/solution.py
+++ b/solution.py
@@ -121,8 +121,9 @@
     log_cum = jnp.cumsum(log_decay(logit_in, bias_in), axis=0)
     log_last = log_cum[-1]
     segment = segment_ids(start_flags)
-    alive_last = (segment[-1] == 0).astype(jnp.float32)
-    tail_mask = (segment == segment[-1]).astype(jnp.float32)
+    last_segment = jnp.sum(start_flags)
+    alive_last = (last_segment == 0).astype(jnp.float32)
+    tail_mask = (segment == last_segment).astype(jnp.float32)
     key_tail = key_in * jnp.exp(log_last[None] - log_cum) * tail_mask[:, None, None]
     block_state = jnp.einsum("jhc,jhd->hcd", key_tail, value_in, precision=highest)
     block_decay = jnp.exp(log_last) * alive_last

time: 77.9 us -> 78.7 us (1.010)
  other arithmetic: 8.05 us -> 9.35 us
    reduce_sum x0 -> x1, other arithmetic: none -> 1.3 us  [block_summary(): last_segment = jnp.sum(start_flags)]
where the time goes in v15:
time: 78.7 us; the launch traced here: 78.4 us
  waiting for transfers between devices  37.2 us (47%)
  starting transfers between devices  18.4 us (23%)
  other arithmetic  9.35 us (12%)
  local copies, waits for them, and re-layouts  6.21 us (8%)
  matrix products  4.75 us (6%)
  between operations  2.46 us (3%)
    ppermute x4, waiting for transfers between devices, from_behind(): return lax.ppermute(value, axis, pairs)  34.5 us
    ppermute x4, starting transfers between devices, from_behind(): return lax.ppermute(value, axis, pairs)  12.9 us
    unnamed x15, local copies, waits for them, and re-layouts  4.2 us
    ppermute x3, starting transfers between devices, direct_sum(): terms.append(lax.ppermute(value, axis, pairs))  3.81 us
    ppermute x2, waiting for transfers between devices, butterfly_sum(): value = value + lax.ppermute(value, axis, pairs)  2.7 us
    ppermute x2, starting transfers between devices, butterfly_sum(): value = value + lax.ppermute(value, axis, pairs)  1.62 us
  transfers between devices with their start and end apart: 9, of which 6 were waited for; matrix products, arithmetic and copies ran while one was open for 7% of the time, Pallas kernels for 0%

profile of v15, /device:TPU:0, one launch (start us, length us, event | category | flops | bytes accessed | tf_op | source)
XLA Modules:
  0.0 78.4 jit_solution(6790993763823974882)
XLA Ops:
  0.6 1.3 %reduce_sum.64 = s32[]{:T(128)} reduce(s32[1,128]{1,0:T(1,128)} %param.22, s32[]{:T(128)} %constant.121.clone.1), dimensions={0,1}, to_apply=%region_2.4 | reduce | flops 127 | bytes 520 | tf_op jit(solution)/shard_map/jvp()/reduce_sum | solution.py:124
  2.6 0.6 copy-done.4
  3.4 0.2 reduce-window.7
  3.6 0.7 compare_convert_fusion.1
  4.3 1.0 %pad_maximum_fusion = bf16[4,128,512]{2,1,0:T(8,128)(2,1)S(1)} fusion(bf16[1,128,512]{2,1,0:T(8,128)(2,1)S(1)} %copy-done, bf16[1,128,512]{2,1,0:T(8,128)(2,1)S(1)} %copy-done.1, bf16[1,128,512]{2,1,0:T(8,128)(2,1)} %param.15, bf16[1,128,512]{2,1,0:T(8,128)(2,1)} %param.14), kind=kLoop, calls=%fused_computation.22 | loop fusion | flops 786432 | bytes 1048576 | tf_op jit(solution)/shard_map/concatenate | solution.py:154
  5.8 0.6 copy-done.3
  6.4 0.3 fusion.16
  6.9 0.3 multiply_reduce_fusion.1
  7.2 0.3 fusion.46
  7.6 4.9 %collective-permute-start = (f32[4,136,128]{2,1,0:T(8,128)S(1)}, f32[4,136,128]{2,1,0:T(8,128)S(1)}, u32[]{:S(2)}, u32[]{:S(2)}) collective-permute-start(f32[4,136,128]{2,1,0:T(8,128)S(1)} %fusion.9), channel_id=1, source_target_pairs={{0,4},{4,8},{8,12},{1,5},{5,9},{9,13},{2,6},{6,10},{10,14},{3,7},{... | collective-permute-start | bytes 835592 | tf_op jit(solution)/shard_map/ppermute | solution.py:18
  13.5 0.4 fusion.4
  13.9 4.5 %collective-permute-done = f32[4,136,128]{2,1,0:T(8,128)S(1)} collective-permute-done((f32[4,136,128]{2,1,0:T(8,128)S(1)}, f32[4,136,128]{2,1,0:T(8,128)S(1)}, u32[]{:S(2)}, u32[]{:S(2)}) %collective-permute-start) | collective-permute-done | bytes 278560 | tf_op jit(solution)/shard_map/ppermute | solution.py:18
  18.5 5.4 %collective-permute-start.1 = (f32[4,128,128]{2,1,0:T(8,128)S(1)}, f32[4,128,128]{2,1,0:T(8,128)S(1)}, u32[]{:S(2)}, u32[]{:S(2)}) collective-permute-start(f32[4,128,128]{2,1,0:T(8,128)S(1)} %multiply_add_fusion.5), channel_id=1, source_target_pairs={{0,8},{4,12},{1,9},{5,13},{2,10},{6,14},{3,11},{7,15},{16,24},{20,... | collective-permute-start | bytes 786440 | tf_op jit(solution)/shard_map/ppermute | solution.py:18
  24.0 0.2 fusion.66
  24.3 4.4 %collective-permute-done.1 = f32[4,128,128]{2,1,0:T(8,128)S(1)} collective-permute-done((f32[4,128,128]{2,1,0:T(8,128)S(1)}, f32[4,128,128]{2,1,0:T(8,128)S(1)}, u32[]{:S(2)}, u32[]{:S(2)}) %collective-permute-start.1) | collective-permute-done | bytes 262176 | tf_op jit(solution)/shard_map/ppermute | solution.py:18
  28.8 0.4 fusion.15
  29.3 0.6 copy-done.2
  29.9 0.2 convolution_bitcast_fusion.2
  30.1 1.6 %collective-permute-start.2 = (f32[128]{0:T(128)S(1)}, f32[128]{0:T(128)S(1)}, u32[]{:S(2)}, u32[]{:S(2)}) collective-permute-start(f32[128]{0:T(128)S(1)} %convolution_bitcast_fusion.2), channel_id=1, source_target_pairs={{0,2},{2,0},{1,3},{3,1},{4,6},{6,4},{5,7},{7,5},{8,10},{10,8},{9,1... | collective-permute-start | bytes 1544 | tf_op jit(solution)/shard_map/ppermute | solution.py:28
  31.6 2.0 %collective-permute-done.2 = f32[128]{0:T(128)S(1)} collective-permute-done((f32[128]{0:T(128)S(1)}, f32[128]{0:T(128)S(1)}, u32[]{:S(2)}, u32[]{:S(2)}) %collective-permute-start.2) | collective-permute-done | bytes 544 | tf_op jit(solution)/shard_map/ppermute | solution.py:28
  33.7 0.5 bitcast_subtract_fusion
  34.4 0.5 fusion.17
  34.8 0.3 fusion.8
  35.2 0.3 convolution_bitcast_fusion
  35.5 1.3 %collective-permute-start.3 = (f32[4,136,128]{2,1,0:T(8,128)S(1)}, f32[4,136,128]{2,1,0:T(8,128)S(1)}, u32[]{:S(2)}, u32[]{:S(2)}) collective-permute-start(f32[4,136,128]{2,1,0:T(8,128)S(1)} %fusion.10), channel_id=1, source_target_pairs={{4,0},{8,4},{12,8},{5,1},{9,5},{13,9},{6,2},{10,6},{14,10},{7,3},{... | collective-permute-start | bytes 835592 | tf_op jit(solution)/shard_map/ppermute | solution.py:18
  36.8 0.3 fusion.6
  37.0 0.4 convolution_bitcast_fusion.1
  37.4 12.7 %collective-permute-done.3 = f32[4,136,128]{2,1,0:T(8,128)S(1)} collective-permute-done((f32[4,136,128]{2,1,0:T(8,128)S(1)}, f32[4,136,128]{2,1,0:T(8,128)S(1)}, u32[]{:S(2)}, u32[]{:S(2)}) %collective-permute-start.3) | collective-permute-done | bytes 278560 | tf_op jit(solution)/shard_map/ppermute | solution.py:18
  50.2 1.3 %collective-permute-start.4 = (f32[4,128,128]{2,1,0:T(8,128)S(1)}, f32[4,128,128]{2,1,0:T(8,128)S(1)}, u32[]{:S(2)}, u32[]{:S(2)}) collective-permute-start(f32[4,128,128]{2,1,0:T(8,128)S(1)} %multiply_add_fusion.3), channel_id=1, source_target_pairs={{8,0},{12,4},{9,1},{13,5},{10,2},{14,6},{11,3},{15,7},{24,16},{28,... | collective-permute-start | bytes 786440 | tf_op jit(solution)/shard_map/ppermute | solution.py:18
  51.5 0.2 fusion.55
  51.7 0.4 fusion.3
  52.2 12.9 %collective-permute-done.4 = f32[4,128,128]{2,1,0:T(8,128)S(1)} collective-permute-done((f32[4,128,128]{2,1,0:T(8,128)S(1)}, f32[4,128,128]{2,1,0:T(8,128)S(1)}, u32[]{:S(2)}, u32[]{:S(2)}) %collective-permute-start.4) | collective-permute-done | bytes 262176 | tf_op jit(solution)/shard_map/ppermute | solution.py:18
  65.1 0.2 multiply_reduce_fusion
  65.3 0.5 fusion.63
  65.8 0.1 copy.140
  65.9 0.1 copy.139
  66.1 0.1 multiply_add_fusion
  66.6 1.1 %fusion.65 = f32[128,4,128]{2,1,0:T(4,128)S(1)} fusion(f32[128,4,128]{2,1,0:T(4,128)S(1)} %copy.141), kind=kOutput, calls=%fused_computation.130 | output fusion | flops 8323072 | bytes 524288 | tf_op jit(solution)/shard_map/transpose(jvp(jit(cumsum)))/reduce_window_sum | solution.py:121
  67.8 1.1 %fusion.64 = f32[128,4,128]{2,1,0:T(4,128)S(1)} fusion(f32[128,4,128]{2,1,0:T(4,128)S(1)} %copy.138), kind=kOutput, calls=%fused_computation.129 | output fusion | flops 8323072 | bytes 524288 | tf_op jit(solution)/shard_map/transpose(jvp(jit(cumsum)))/reduce_window_sum | solution.py:97
  68.9 0.6 fusion.51
  69.6 0.5 fusion.5
  70.1 0.7 collective-permute-done.5
  70.8 3.7 %collective-permute-start.6 = (f32[1024]{0:T(1024)S(1)}, f32[1024]{0:T(1024)S(1)}, u32[]{:S(2)}, u32[]{:S(2)}) collective-permute-start(f32[1024]{0:T(1024)S(1)} %fusion.61), channel_id=1, source_target_pairs={{0,12},{4,0},{8,4},{12,8},{1,13},{5,1},{9,5},{13,9},{2,14},{6,2},{... | collective-permute-start | bytes 12296 | tf_op jit(solution)/shard_map/ppermute | solution.py:39
  74.7 0.8 copy.144
  75.5 0.8 copy.143
  76.2 0.8 copy.142
  77.0 0.7 convert_element_type.135
  77.8 0.6 slice_multiply_fusion
  (48 shorter events, 2.5 us)
Async XLA Ops:
  2.6 0.7 copy-start.4
  3.2 1.1 %copy-start = (bf16[1,128,512]{2,1,0:T(8,128)(2,1)S(1)}, bf16[1,128,512]{2,1,0:T(8,128)(2,1)}, u32[]{:S(2)}) copy-start(bf16[1,128,512]{2,1,0:T(8,128)(2,1)} %param.17) | copy-start | bytes 393220
  3.2 1.1 %copy-start.1 = (bf16[1,128,512]{2,1,0:T(8,128)(2,1)S(1)}, bf16[1,128,512]{2,1,0:T(8,128)(2,1)}, u32[]{:S(2)}) copy-start(bf16[1,128,512]{2,1,0:T(8,128)(2,1)} %param.16) | copy-start | bytes 393220
  5.7 0.7 copy-start.3
  7.6 10.8 %collective-permute-start = (f32[4,136,128]{2,1,0:T(8,128)S(1)}, f32[4,136,128]{2,1,0:T(8,128)S(1)}, u32[]{:S(2)}, u32[]{:S(2)}) collective-permute-start(f32[4,136,128]{2,1,0:T(8,128)S(1)} %fusion.9), channel_id=1, source_target_pairs={{0,4},{4,8},{8,12},{1,5},{5,9},{9,13},{2,6},{6,10},{10,14},{3,7},{... | collective-permute-start | bytes 835592 | tf_op jit(solution)/shard_map/ppermute | solution.py:18
  18.5 10.1 %collective-permute-start.1 = (f32[4,128,128]{2,1,0:T(8,128)S(1)}, f32[4,128,128]{2,1,0:T(8,128)S(1)}, u32[]{:S(2)}, u32[]{:S(2)}) collective-permute-start(f32[4,128,128]{2,1,0:T(8,128)S(1)} %multiply_add_fusion.5), channel_id=1, source_target_pairs={{0,8},{4,12},{1,9},{5,13},{2,10},{6,14},{3,11},{7,15},{16,24},{20,... | collective-permute-start | bytes 786440 | tf_op jit(solution)/shard_map/ppermute | solution.py:18
  29.2 0.7 copy-start.2
  30.1 3.6 %collective-permute-start.2 = (f32[128]{0:T(128)S(1)}, f32[128]{0:T(128)S(1)}, u32[]{:S(2)}, u32[]{:S(2)}) collective-permute-start(f32[128]{0:T(128)S(1)} %convolution_bitcast_fusion.2), channel_id=1, source_target_pairs={{0,2},{2,0},{1,3},{3,1},{4,6},{6,4},{5,7},{7,5},{8,10},{10,8},{9,1... | collective-permute-start | bytes 1544 | tf_op jit(solution)/shard_map/ppermute | solution.py:28
  31.6 2.0 %copy-start.5 = (f32[1,128]{1,0:T(1,128)S(1)}, f32[1,128]{1,0:T(1,128)}, u32[]{:S(2)}) copy-start(f32[1,128]{1,0:T(1,128)} %param.20) | copy-start | bytes 1540
  35.5 14.6 %collective-permute-start.3 = (f32[4,136,128]{2,1,0:T(8,128)S(1)}, f32[4,136,128]{2,1,0:T(8,128)S(1)}, u32[]{:S(2)}, u32[]{:S(2)}) collective-permute-start(f32[4,136,128]{2,1,0:T(8,128)S(1)} %fusion.10), channel_id=1, source_target_pairs={{4,0},{8,4},{12,8},{5,1},{9,5},{13,9},{6,2},{10,6},{14,10},{7,3},{... | collective-permute-start | bytes 835592 | tf_op jit(solution)/shard_map/ppermute | solution.py:18
  50.2 14.8 %collective-permute-start.4 = (f32[4,128,128]{2,1,0:T(8,128)S(1)}, f32[4,128,128]{2,1,0:T(8,128)S(1)}, u32[]{:S(2)}, u32[]{:S(2)}) collective-permute-start(f32[4,128,128]{2,1,0:T(8,128)S(1)} %multiply_add_fusion.3), channel_id=1, source_target_pairs={{8,0},{12,4},{9,1},{13,5},{10,2},{14,6},{11,3},{15,7},{24,16},{28,... | collective-permute-start | bytes 786440 | tf_op jit(solution)/shard_map/ppermute | solution.py:18
  69.5 1.2 %collective-permute-start.5 = (f32[1024]{0:T(1024)S(1)}, f32[1024]{0:T(1024)S(1)}, u32[]{:S(2)}, u32[]{:S(2)}) collective-permute-start(f32[1024]{0:T(1024)S(1)} %pad_maximum_fusion.1), channel_id=1, source_target_pairs={{0,1},{1,0},{2,3},{3,2},{4,5},{5,4},{6,7},{7,6},{8,9},{9,8},{10,11... | collective-permute-start | bytes 12296 | tf_op jit(solution)/shard_map/ppermute | solution.py:28
  70.7 7.0 %collective-permute-start.8 = (f32[1024]{0:T(1024)S(1)}, f32[1024]{0:T(1024)S(1)}, u32[]{:S(2)}, u32[]{:S(2)}) collective-permute-start(f32[1024]{0:T(1024)S(1)} %fusion.61), channel_id=1, source_target_pairs={{0,4},{4,8},{8,12},{12,0},{1,5},{5,9},{9,13},{13,1},{2,6},{6,10},{... | collective-permute-start | bytes 12296 | tf_op jit(solution)/shard_map/ppermute | solution.py:39
  70.7 7.0 %collective-permute-start.7 = (f32[1024]{0:T(1024)S(1)}, f32[1024]{0:T(1024)S(1)}, u32[]{:S(2)}, u32[]{:S(2)}) collective-permute-start(f32[1024]{0:T(1024)S(1)} %fusion.61), channel_id=1, source_target_pairs={{0,8},{4,12},{8,0},{12,4},{1,9},{5,13},{9,1},{13,5},{2,10},{6,14},... | collective-permute-start | bytes 12296 | tf_op jit(solution)/shard_map/ppermute | solution.py:39
  70.8 6.9 %collective-permute-start.6 = (f32[1024]{0:T(1024)S(1)}, f32[1024]{0:T(1024)S(1)}, u32[]{:S(2)}, u32[]{:S(2)}) collective-permute-start(f32[1024]{0:T(1024)S(1)} %fusion.61), channel_id=1, source_target_pairs={{0,12},{4,0},{8,4},{12,8},{1,13},{5,1},{9,5},{13,9},{2,14},{6,2},{... | collective-permute-start | bytes 12296 | tf_op jit(solution)/shard_map/ppermute | solution.py:39

commit v16 on v7

--- a/solution.py
+++ b/solution.py
@@ -149,10 +149,13 @@
 
     start_flags = segment_starts[0]
     kind_id = mask_ids[0, 0]
+    rows_in = lax.optimization_barrier(
+        jnp.concatenate([per_head_keys, value_rows, gate_logits], axis=0)
+    )
     query_f = to_heads(queries)
-    key_f = to_heads(per_head_keys)
-    value_f = to_heads(value_rows)
-    logit_f = to_heads(gate_logits)
+    key_f = to_heads(rows_in[0:1])
+    value_f = to_heads(rows_in[1:2])
+    logit_f = to_heads(rows_in[2:3])
     bias_h = gate_bias.reshape(head_count, DK)
 
     def inner_terms(query_in, key_in, value_in, logit_in, bias_in):

time: 78.4 us -> 77.9 us (level)
  local copies, waits for them, and re-layouts: 8.22 us -> 6.71 us
  other arithmetic: 6.94 us -> 7.93 us
    unnamed x19 -> x17, local copies, waits for them, and re-layouts: 5.84 us -> 4.2 us
    concatenate x0 -> x1, other arithmetic: none -> 0.95 us  [on_device(): jnp.concatenate([per_head_keys, value_rows, gate_logits], axis=0)]
where the time goes in v16:
time: 77.9 us; the launch traced here: 77.6 us
  waiting for transfers between devices  37.2 us (48%)
  starting transfers between devices  18.5 us (24%)
  other arithmetic  7.93 us (10%)
  local copies, waits for them, and re-layouts  6.71 us (9%)
  matrix products  4.75 us (6%)
  between operations  2.49 us (3%)
    ppermute x4, waiting for transfers between devices, from_behind(): return lax.ppermute(value, axis, pairs)  34.5 us
    ppermute x4, starting transfers between devices, from_behind(): return lax.ppermute(value, axis, pairs)  13.1 us
    unnamed x17, local copies, waits for them, and re-layouts  4.2 us
    ppermute x3, starting transfers between devices, direct_sum(): terms.append(lax.ppermute(value, axis, pairs))  3.81 us
    ppermute x2, waiting for transfers between devices, butterfly_sum(): value = value + lax.ppermute(value, axis, pairs)  2.7 us
    ppermute x2, starting transfers between devices, butterfly_sum(): value = value + lax.ppermute(value, axis, pairs)  1.62 us
  transfers between devices with their start and end apart: 9, of which 6 were waited for; matrix products, arithmetic and copies ran while one was open for 7% of the time, Pallas kernels for 0%

profile of v16, /device:TPU:0, one launch (start us, length us, event | category | flops | bytes accessed | tf_op | source)
XLA Modules:
  0.0 77.6 jit_solution(5214729700405948230)
XLA Ops:
  0.6 0.6 copy-done.5
  1.4 0.2 broadcast_in_dim.37
  1.6 0.5 slice.72
  2.9 0.6 compare_convert_fusion.1
  3.5 1.0 %pad_maximum_fusion = bf16[3,128,512]{2,1,0:T(8,128)(2,1)S(1)} fusion(bf16[1,128,512]{2,1,0:T(8,128)(2,1)S(1)} %copy-done.1, bf16[1,128,512]{2,1,0:T(8,128)(2,1)S(1)} %copy-done.2, bf16[1,128,512]{2,1,0:T(8,128)(2,1)} %param.15), kind=kLoop, calls=%fused_computation.25 | loop fusion | flops 393216 | bytes 786432 | tf_op jit(solution)/shard_map/concatenate | solution.py:153
  4.9 0.6 copy-done.4
  5.5 0.3 fusion.16
  6.0 0.3 multiply_reduce_fusion.1
  6.3 0.3 fusion.46
  6.7 5.1 %collective-permute-start = (f32[4,136,128]{2,1,0:T(8,128)S(1)}, f32[4,136,128]{2,1,0:T(8,128)S(1)}, u32[]{:S(2)}, u32[]{:S(2)}) collective-permute-start(f32[4,136,128]{2,1,0:T(8,128)S(1)} %fusion.9), channel_id=1, source_target_pairs={{0,4},{4,8},{8,12},{1,5},{5,9},{9,13},{2,6},{6,10},{10,14},{3,7},{... | collective-permute-start | bytes 835592 | tf_op jit(solution)/shard_map/ppermute | solution.py:18
  12.7 0.4 fusion.4
  13.1 4.5 %collective-permute-done = f32[4,136,128]{2,1,0:T(8,128)S(1)} collective-permute-done((f32[4,136,128]{2,1,0:T(8,128)S(1)}, f32[4,136,128]{2,1,0:T(8,128)S(1)}, u32[]{:S(2)}, u32[]{:S(2)}) %collective-permute-start) | collective-permute-done | bytes 278560 | tf_op jit(solution)/shard_map/ppermute | solution.py:18
  17.8 5.4 %collective-permute-start.1 = (f32[4,128,128]{2,1,0:T(8,128)S(1)}, f32[4,128,128]{2,1,0:T(8,128)S(1)}, u32[]{:S(2)}, u32[]{:S(2)}) collective-permute-start(f32[4,128,128]{2,1,0:T(8,128)S(1)} %multiply_add_fusion.5), channel_id=1, source_target_pairs={{0,8},{4,12},{1,9},{5,13},{2,10},{6,14},{3,11},{7,15},{16,24},{20,... | collective-permute-start | bytes 786440 | tf_op jit(solution)/shard_map/ppermute | solution.py:18
  23.3 0.2 fusion.66
  23.5 4.4 %collective-permute-done.1 = f32[4,128,128]{2,1,0:T(8,128)S(1)} collective-permute-done((f32[4,128,128]{2,1,0:T(8,128)S(1)}, f32[4,128,128]{2,1,0:T(8,128)S(1)}, u32[]{:S(2)}, u32[]{:S(2)}) %collective-permute-start.1) | collective-permute-done | bytes 262176 | tf_op jit(solution)/shard_map/ppermute | solution.py:18
  28.0 0.4 fusion.15
  28.5 0.6 copy-done.3
  29.1 0.2 convolution_bitcast_fusion.2
  29.3 1.6 %collective-permute-start.2 = (f32[128]{0:T(128)S(1)}, f32[128]{0:T(128)S(1)}, u32[]{:S(2)}, u32[]{:S(2)}) collective-permute-start(f32[128]{0:T(128)S(1)} %convolution_bitcast_fusion.2), channel_id=1, source_target_pairs={{0,2},{2,0},{1,3},{3,1},{4,6},{6,4},{5,7},{7,5},{8,10},{10,8},{9,1... | collective-permute-start | bytes 1544 | tf_op jit(solution)/shard_map/ppermute | solution.py:28
  30.9 2.0 %collective-permute-done.2 = f32[128]{0:T(128)S(1)} collective-permute-done((f32[128]{0:T(128)S(1)}, f32[128]{0:T(128)S(1)}, u32[]{:S(2)}, u32[]{:S(2)}) %collective-permute-start.2) | collective-permute-done | bytes 544 | tf_op jit(solution)/shard_map/ppermute | solution.py:28
  32.9 0.5 bitcast_subtract_fusion
  33.6 0.5 fusion.17
  34.1 0.3 fusion.8
  34.4 0.3 convolution_bitcast_fusion
  34.7 1.3 %collective-permute-start.3 = (f32[4,136,128]{2,1,0:T(8,128)S(1)}, f32[4,136,128]{2,1,0:T(8,128)S(1)}, u32[]{:S(2)}, u32[]{:S(2)}) collective-permute-start(f32[4,136,128]{2,1,0:T(8,128)S(1)} %fusion.10), channel_id=1, source_target_pairs={{4,0},{8,4},{12,8},{5,1},{9,5},{13,9},{6,2},{10,6},{14,10},{7,3},{... | collective-permute-start | bytes 835592 | tf_op jit(solution)/shard_map/ppermute | solution.py:18
  36.0 0.3 fusion.6
  36.3 0.4 convolution_bitcast_fusion.1
  36.7 12.7 %collective-permute-done.3 = f32[4,136,128]{2,1,0:T(8,128)S(1)} collective-permute-done((f32[4,136,128]{2,1,0:T(8,128)S(1)}, f32[4,136,128]{2,1,0:T(8,128)S(1)}, u32[]{:S(2)}, u32[]{:S(2)}) %collective-permute-start.3) | collective-permute-done | bytes 278560 | tf_op jit(solution)/shard_map/ppermute | solution.py:18
  49.5 1.3 %collective-permute-start.4 = (f32[4,128,128]{2,1,0:T(8,128)S(1)}, f32[4,128,128]{2,1,0:T(8,128)S(1)}, u32[]{:S(2)}, u32[]{:S(2)}) collective-permute-start(f32[4,128,128]{2,1,0:T(8,128)S(1)} %multiply_add_fusion.3), channel_id=1, source_target_pairs={{8,0},{12,4},{9,1},{13,5},{10,2},{14,6},{11,3},{15,7},{24,16},{28,... | collective-permute-start | bytes 786440 | tf_op jit(solution)/shard_map/ppermute | solution.py:18
  50.8 0.2 fusion.55
  51.0 0.4 fusion.3
  51.4 12.9 %collective-permute-done.4 = f32[4,128,128]{2,1,0:T(8,128)S(1)} collective-permute-done((f32[4,128,128]{2,1,0:T(8,128)S(1)}, f32[4,128,128]{2,1,0:T(8,128)S(1)}, u32[]{:S(2)}, u32[]{:S(2)}) %collective-permute-start.4) | collective-permute-done | bytes 262176 | tf_op jit(solution)/shard_map/ppermute | solution.py:18
  64.3 0.2 multiply_reduce_fusion
  64.6 0.5 fusion.63
  65.0 0.1 copy.140
  65.2 0.1 copy.139
  65.4 0.1 multiply_add_fusion
  65.8 1.1 %fusion.65 = f32[128,4,128]{2,1,0:T(4,128)S(1)} fusion(f32[128,4,128]{2,1,0:T(4,128)S(1)} %copy.141), kind=kOutput, calls=%fused_computation.129 | output fusion | flops 8323072 | bytes 524288 | tf_op jit(solution)/shard_map/transpose(jvp(jit(cumsum)))/reduce_window_sum | solution.py:121
  67.0 1.1 %fusion.64 = f32[128,4,128]{2,1,0:T(4,128)S(1)} fusion(f32[128,4,128]{2,1,0:T(4,128)S(1)} %copy.138), kind=kOutput, calls=%fused_computation.128 | output fusion | flops 8323072 | bytes 524288 | tf_op jit(solution)/shard_map/transpose(jvp(jit(cumsum)))/reduce_window_sum | solution.py:97
  68.1 0.6 fusion.51
  68.8 0.5 fusion.5
  69.3 0.7 collective-permute-done.5
  70.1 3.7 %collective-permute-start.6 = (f32[1024]{0:T(1024)S(1)}, f32[1024]{0:T(1024)S(1)}, u32[]{:S(2)}, u32[]{:S(2)}) collective-permute-start(f32[1024]{0:T(1024)S(1)} %fusion.61), channel_id=1, source_target_pairs={{0,12},{4,0},{8,4},{12,8},{1,13},{5,1},{9,5},{13,9},{2,14},{6,2},{... | collective-permute-start | bytes 12296 | tf_op jit(solution)/shard_map/ppermute | solution.py:39
  74.0 0.8 copy.144
  74.7 0.8 copy.143
  75.5 0.8 copy.142
  76.3 0.7 convert_element_type.135
  77.0 0.6 slice_multiply_fusion
  (50 shorter events, 2.4 us)
Async XLA Ops:
  0.6 0.7 copy-start.5
  1.3 2.2 %copy-start.1 = (bf16[1,128,512]{2,1,0:T(8,128)(2,1)S(1)}, bf16[1,128,512]{2,1,0:T(8,128)(2,1)}, u32[]{:S(2)}) copy-start(bf16[1,128,512]{2,1,0:T(8,128)(2,1)} %param.17) | copy-start | bytes 393220
  1.3 2.2 %copy-start.2 = (bf16[1,128,512]{2,1,0:T(8,128)(2,1)S(1)}, bf16[1,128,512]{2,1,0:T(8,128)(2,1)}, u32[]{:S(2)}) copy-start(bf16[1,128,512]{2,1,0:T(8,128)(2,1)} %param.16) | copy-start | bytes 393220
  4.8 0.7 copy-start.4
  6.6 5.9 %copy-start = (bf16[1,128,512]{2,1,0:T(8,128)(2,1)S(1)}, bf16[1,128,512]{2,1,0:T(8,128)(2,1)}, u32[]{:S(2)}) copy-start(bf16[1,128,512]{2,1,0:T(8,128)(2,1)} %param.14) | copy-start | bytes 393220
  6.7 11.0 %collective-permute-start = (f32[4,136,128]{2,1,0:T(8,128)S(1)}, f32[4,136,128]{2,1,0:T(8,128)S(1)}, u32[]{:S(2)}, u32[]{:S(2)}) collective-permute-start(f32[4,136,128]{2,1,0:T(8,128)S(1)} %fusion.9), channel_id=1, source_target_pairs={{0,4},{4,8},{8,12},{1,5},{5,9},{9,13},{2,6},{6,10},{10,14},{3,7},{... | collective-permute-start | bytes 835592 | tf_op jit(solution)/shard_map/ppermute | solution.py:18
  17.8 10.1 %collective-permute-start.1 = (f32[4,128,128]{2,1,0:T(8,128)S(1)}, f32[4,128,128]{2,1,0:T(8,128)S(1)}, u32[]{:S(2)}, u32[]{:S(2)}) collective-permute-start(f32[4,128,128]{2,1,0:T(8,128)S(1)} %multiply_add_fusion.5), channel_id=1, source_target_pairs={{0,8},{4,12},{1,9},{5,13},{2,10},{6,14},{3,11},{7,15},{16,24},{20,... | collective-permute-start | bytes 786440 | tf_op jit(solution)/shard_map/ppermute | solution.py:18
  28.5 0.7 copy-start.3
  29.3 3.6 %collective-permute-start.2 = (f32[128]{0:T(128)S(1)}, f32[128]{0:T(128)S(1)}, u32[]{:S(2)}, u32[]{:S(2)}) collective-permute-start(f32[128]{0:T(128)S(1)} %convolution_bitcast_fusion.2), channel_id=1, source_target_pairs={{0,2},{2,0},{1,3},{3,1},{4,6},{6,4},{5,7},{7,5},{8,10},{10,8},{9,1... | collective-permute-start | bytes 1544 | tf_op jit(solution)/shard_map/ppermute | solution.py:28
  30.9 2.0 %copy-start.6 = (f32[1,128]{1,0:T(1,128)S(1)}, f32[1,128]{1,0:T(1,128)}, u32[]{:S(2)}) copy-start(f32[1,128]{1,0:T(1,128)} %param.20) | copy-start | bytes 1540
  34.7 14.6 %collective-permute-start.3 = (f32[4,136,128]{2,1,0:T(8,128)S(1)}, f32[4,136,128]{2,1,0:T(8,128)S(1)}, u32[]{:S(2)}, u32[]{:S(2)}) collective-permute-start(f32[4,136,128]{2,1,0:T(8,128)S(1)} %fusion.10), channel_id=1, source_target_pairs={{4,0},{8,4},{12,8},{5,1},{9,5},{13,9},{6,2},{10,6},{14,10},{7,3},{... | collective-permute-start | bytes 835592 | tf_op jit(solution)/shard_map/ppermute | solution.py:18
  49.5 14.8 %collective-permute-start.4 = (f32[4,128,128]{2,1,0:T(8,128)S(1)}, f32[4,128,128]{2,1,0:T(8,128)S(1)}, u32[]{:S(2)}, u32[]{:S(2)}) collective-permute-start(f32[4,128,128]{2,1,0:T(8,128)S(1)} %multiply_add_fusion.3), channel_id=1, source_target_pairs={{8,0},{12,4},{9,1},{13,5},{10,2},{14,6},{11,3},{15,7},{24,16},{28,... | collective-permute-start | bytes 786440 | tf_op jit(solution)/shard_map/ppermute | solution.py:18
  68.7 1.2 %collective-permute-start.5 = (f32[1024]{0:T(1024)S(1)}, f32[1024]{0:T(1024)S(1)}, u32[]{:S(2)}, u32[]{:S(2)}) collective-permute-start(f32[1024]{0:T(1024)S(1)} %pad_maximum_fusion.1), channel_id=1, source_target_pairs={{0,1},{1,0},{2,3},{3,2},{4,5},{5,4},{6,7},{7,6},{8,9},{9,8},{10,11... | collective-permute-start | bytes 12296 | tf_op jit(solution)/shard_map/ppermute | solution.py:28
  70.0 7.0 %collective-permute-start.8 = (f32[1024]{0:T(1024)S(1)}, f32[1024]{0:T(1024)S(1)}, u32[]{:S(2)}, u32[]{:S(2)}) collective-permute-start(f32[1024]{0:T(1024)S(1)} %fusion.61), channel_id=1, source_target_pairs={{0,4},{4,8},{8,12},{12,0},{1,5},{5,9},{9,13},{13,1},{2,6},{6,10},{... | collective-permute-start | bytes 12296 | tf_op jit(solution)/shard_map/ppermute | solution.py:39
  70.0 7.0 %collective-permute-start.7 = (f32[1024]{0:T(1024)S(1)}, f32[1024]{0:T(1024)S(1)}, u32[]{:S(2)}, u32[]{:S(2)}) collective-permute-start(f32[1024]{0:T(1024)S(1)} %fusion.61), channel_id=1, source_target_pairs={{0,8},{4,12},{8,0},{12,4},{1,9},{5,13},{9,1},{13,5},{2,10},{6,14},... | collective-permute-start | bytes 12296 | tf_op jit(solution)/shard_map/ppermute | solution.py:39
  70.1 6.9 %collective-permute-start.6 = (f32[1024]{0:T(1024)S(1)}, f32[1024]{0:T(1024)S(1)}, u32[]{:S(2)}, u32[]{:S(2)}) collective-permute-start(f32[1024]{0:T(1024)S(1)} %fusion.61), channel_id=1, source_target_pairs={{0,12},{4,0},{8,4},{12,8},{1,13},{5,1},{9,5},{13,9},{2,14},{6,2},{... | collective-permute-start | bytes 12296 | tf_op jit(solution)/shard_map/ppermute | solution.py:39

commit v17 on v10

--- a/solution.py
+++ b/solution.py
@@ -200,7 +200,9 @@
     grad_bias = inner_grads[4] + summary_grads[3]
     token_total = token_count * lax.axis_size("ctx") * lax.axis_size("rep")
     both_total = direct_sum(
-        butterfly_sum(jnp.concatenate([grad_bias.reshape(-1), grad_weight.reshape(-1)]), "rep"),
+        butterfly_sum(
+            jnp.concatenate([grad_bias.reshape(-1), grad_weight.reshape(-1)]) / token_total, "rep"
+        ),
         "ctx",
     )
     bias_total, weight_total = jnp.split(both_total, 2)
@@ -214,8 +216,8 @@
         to_rows(grad_key),
         to_rows(grad_value),
         to_rows(grad_logit),
-        bias_total / token_total,
-        weight_total / token_total,
+        bias_total,
+        weight_total,
     )
 
 

time: 77.9 us -> 77.9 us (level)
  no operation moved by 1% of the time
where the time goes in v17:
time: 77.9 us; the launch traced here: 77.6 us
  waiting for transfers between devices  37.2 us (48%)
  starting transfers between devices  18.4 us (24%)
  other arithmetic  7.46 us (10%)
  local copies, waits for them, and re-layouts  7.31 us (9%)
  matrix products  4.74 us (6%)
  between operations  2.48 us (3%)
    ppermute x4, waiting for transfers between devices, from_behind(): return lax.ppermute(value, axis, pairs)  34.5 us
    ppermute x4, starting transfers between devices, from_behind(): return lax.ppermute(value, axis, pairs)  12.9 us
    unnamed x15, local copies, waits for them, and re-layouts  4.2 us
    ppermute x3, starting transfers between devices, direct_sum(): terms.append(lax.ppermute(value, axis, pairs))  3.86 us
    ppermute x2, waiting for transfers between devices, butterfly_sum(): value = value + lax.ppermute(value, axis, pairs)  2.71 us
    ppermute x2, starting transfers between devices, butterfly_sum(): value = value + lax.ppermute(value, axis, pairs)  1.62 us
  transfers between devices with their start and end apart: 9, of which 6 were waited for; matrix products, arithmetic and copies ran while one was open for 7% of the time, Pallas kernels for 0%

profile of v17, /device:TPU:0, one launch (start us, length us, event | category | flops | bytes accessed | tf_op | source)
XLA Modules:
  0.0 77.6 jit_solution(12974660413449102322)
XLA Ops:
  0.6 0.6 copy-done.4
  1.4 0.2 broadcast_in_dim.37
  1.6 0.5 slice.77
  2.9 0.6 compare_convert_fusion.1
  3.5 1.0 %pad_maximum_fusion = bf16[4,128,512]{2,1,0:T(8,128)(2,1)S(1)} fusion(bf16[1,128,512]{2,1,0:T(8,128)(2,1)S(1)} %copy-done, bf16[1,128,512]{2,1,0:T(8,128)(2,1)S(1)} %copy-done.1, bf16[1,128,512]{2,1,0:T(8,128)(2,1)} %param.15, bf16[1,128,512]{2,1,0:T(8,128)(2,1)} %param.14), kind=kLoop, calls=%fused_computation.22 | loop fusion | flops 786432 | bytes 1048576 | tf_op jit(solution)/shard_map/concatenate | solution.py:153
  5.0 0.6 copy-done.3
  5.6 0.3 fusion.16
  6.1 0.3 multiply_reduce_fusion.1
  6.4 0.3 fusion.46
  6.8 4.9 %collective-permute-start = (f32[4,136,128]{2,1,0:T(8,128)S(1)}, f32[4,136,128]{2,1,0:T(8,128)S(1)}, u32[]{:S(2)}, u32[]{:S(2)}) collective-permute-start(f32[4,136,128]{2,1,0:T(8,128)S(1)} %fusion.9), channel_id=1, source_target_pairs={{0,4},{4,8},{8,12},{1,5},{5,9},{9,13},{2,6},{6,10},{10,14},{3,7},{... | collective-permute-start | bytes 835592 | tf_op jit(solution)/shard_map/ppermute | solution.py:18
  12.7 0.4 fusion.4
  13.1 4.5 %collective-permute-done = f32[4,136,128]{2,1,0:T(8,128)S(1)} collective-permute-done((f32[4,136,128]{2,1,0:T(8,128)S(1)}, f32[4,136,128]{2,1,0:T(8,128)S(1)}, u32[]{:S(2)}, u32[]{:S(2)}) %collective-permute-start) | collective-permute-done | bytes 278560 | tf_op jit(solution)/shard_map/ppermute | solution.py:18
  17.8 5.4 %collective-permute-start.1 = (f32[4,128,128]{2,1,0:T(8,128)S(1)}, f32[4,128,128]{2,1,0:T(8,128)S(1)}, u32[]{:S(2)}, u32[]{:S(2)}) collective-permute-start(f32[4,128,128]{2,1,0:T(8,128)S(1)} %multiply_add_fusion.5), channel_id=1, source_target_pairs={{0,8},{4,12},{1,9},{5,13},{2,10},{6,14},{3,11},{7,15},{16,24},{20,... | collective-permute-start | bytes 786440 | tf_op jit(solution)/shard_map/ppermute | solution.py:18
  23.3 0.2 fusion.67
  23.5 4.4 %collective-permute-done.1 = f32[4,128,128]{2,1,0:T(8,128)S(1)} collective-permute-done((f32[4,128,128]{2,1,0:T(8,128)S(1)}, f32[4,128,128]{2,1,0:T(8,128)S(1)}, u32[]{:S(2)}, u32[]{:S(2)}) %collective-permute-start.1) | collective-permute-done | bytes 262176 | tf_op jit(solution)/shard_map/ppermute | solution.py:18
  28.0 0.4 fusion.15
  28.5 0.6 copy-done.2
  29.1 0.2 convolution_bitcast_fusion.2
  29.3 1.5 %collective-permute-start.2 = (f32[128]{0:T(128)S(1)}, f32[128]{0:T(128)S(1)}, u32[]{:S(2)}, u32[]{:S(2)}) collective-permute-start(f32[128]{0:T(128)S(1)} %convolution_bitcast_fusion.2), channel_id=1, source_target_pairs={{0,2},{2,0},{1,3},{3,1},{4,6},{6,4},{5,7},{7,5},{8,10},{10,8},{9,1... | collective-permute-start | bytes 1544 | tf_op jit(solution)/shard_map/ppermute | solution.py:28
  30.8 2.0 %collective-permute-done.2 = f32[128]{0:T(128)S(1)} collective-permute-done((f32[128]{0:T(128)S(1)}, f32[128]{0:T(128)S(1)}, u32[]{:S(2)}, u32[]{:S(2)}) %collective-permute-start.2) | collective-permute-done | bytes 544 | tf_op jit(solution)/shard_map/ppermute | solution.py:28
  32.9 0.5 bitcast_subtract_fusion
  33.6 0.5 fusion.17
  34.1 0.3 fusion.8
  34.4 0.3 convolution_bitcast_fusion
  34.7 1.3 %collective-permute-start.3 = (f32[4,136,128]{2,1,0:T(8,128)S(1)}, f32[4,136,128]{2,1,0:T(8,128)S(1)}, u32[]{:S(2)}, u32[]{:S(2)}) collective-permute-start(f32[4,136,128]{2,1,0:T(8,128)S(1)} %fusion.10), channel_id=1, source_target_pairs={{4,0},{8,4},{12,8},{5,1},{9,5},{13,9},{6,2},{10,6},{14,10},{7,3},{... | collective-permute-start | bytes 835592 | tf_op jit(solution)/shard_map/ppermute | solution.py:18
  36.0 0.3 fusion.6
  36.2 0.4 convolution_bitcast_fusion.1
  36.6 12.7 %collective-permute-done.3 = f32[4,136,128]{2,1,0:T(8,128)S(1)} collective-permute-done((f32[4,136,128]{2,1,0:T(8,128)S(1)}, f32[4,136,128]{2,1,0:T(8,128)S(1)}, u32[]{:S(2)}, u32[]{:S(2)}) %collective-permute-start.3) | collective-permute-done | bytes 278560 | tf_op jit(solution)/shard_map/ppermute | solution.py:18
  49.5 1.3 %collective-permute-start.4 = (f32[4,128,128]{2,1,0:T(8,128)S(1)}, f32[4,128,128]{2,1,0:T(8,128)S(1)}, u32[]{:S(2)}, u32[]{:S(2)}) collective-permute-start(f32[4,128,128]{2,1,0:T(8,128)S(1)} %multiply_add_fusion.3), channel_id=1, source_target_pairs={{8,0},{12,4},{9,1},{13,5},{10,2},{14,6},{11,3},{15,7},{24,16},{28,... | collective-permute-start | bytes 786440 | tf_op jit(solution)/shard_map/ppermute | solution.py:18
  50.8 0.2 fusion.55
  51.0 0.4 fusion.3
  51.4 12.9 %collective-permute-done.4 = f32[4,128,128]{2,1,0:T(8,128)S(1)} collective-permute-done((f32[4,128,128]{2,1,0:T(8,128)S(1)}, f32[4,128,128]{2,1,0:T(8,128)S(1)}, u32[]{:S(2)}, u32[]{:S(2)}) %collective-permute-start.4) | collective-permute-done | bytes 262176 | tf_op jit(solution)/shard_map/ppermute | solution.py:18
  64.3 0.2 multiply_reduce_fusion
  64.6 0.5 fusion.63
  65.0 0.1 copy.140
  65.2 0.1 copy.139
  65.3 0.1 multiply_add_fusion
  65.8 1.1 %fusion.66 = f32[128,4,128]{2,1,0:T(4,128)S(1)} fusion(f32[128,4,128]{2,1,0:T(4,128)S(1)} %copy.141), kind=kOutput, calls=%fused_computation.129 | output fusion | flops 8323072 | bytes 524288 | tf_op jit(solution)/shard_map/transpose(jvp(jit(cumsum)))/reduce_window_sum | solution.py:121
  67.0 1.1 %fusion.65 = f32[128,4,128]{2,1,0:T(4,128)S(1)} fusion(f32[128,4,128]{2,1,0:T(4,128)S(1)} %copy.138), kind=kOutput, calls=%fused_computation.128 | output fusion | flops 8323072 | bytes 524288 | tf_op jit(solution)/shard_map/transpose(jvp(jit(cumsum)))/reduce_window_sum | solution.py:97
  68.1 0.6 fusion.51
  68.8 0.5 fusion.5
  69.3 0.7 collective-permute-done.5
  70.1 3.7 %collective-permute-start.6 = (f32[1024]{0:T(1024)S(1)}, f32[1024]{0:T(1024)S(1)}, u32[]{:S(2)}, u32[]{:S(2)}) collective-permute-start(f32[1024]{0:T(1024)S(1)} %fusion.61), channel_id=1, source_target_pairs={{0,12},{4,0},{8,4},{12,8},{1,13},{5,1},{9,5},{13,9},{2,14},{6,2},{... | collective-permute-start | bytes 12296 | tf_op jit(solution)/shard_map/ppermute | solution.py:39
  74.0 0.8 copy.144
  74.8 0.8 copy.143
  75.5 0.8 copy.142
  76.3 0.7 convert_element_type.135
  77.0 0.6 fusion.64
  (48 shorter events, 2.5 us)
Async XLA Ops:
  0.6 0.7 copy-start.4
  1.3 2.2 %copy-start = (bf16[1,128,512]{2,1,0:T(8,128)(2,1)S(1)}, bf16[1,128,512]{2,1,0:T(8,128)(2,1)}, u32[]{:S(2)}) copy-start(bf16[1,128,512]{2,1,0:T(8,128)(2,1)} %param.17) | copy-start | bytes 393220
  1.3 2.2 %copy-start.1 = (bf16[1,128,512]{2,1,0:T(8,128)(2,1)S(1)}, bf16[1,128,512]{2,1,0:T(8,128)(2,1)}, u32[]{:S(2)}) copy-start(bf16[1,128,512]{2,1,0:T(8,128)(2,1)} %param.16) | copy-start | bytes 393220
  4.9 0.7 copy-start.3
  6.8 10.8 %collective-permute-start = (f32[4,136,128]{2,1,0:T(8,128)S(1)}, f32[4,136,128]{2,1,0:T(8,128)S(1)}, u32[]{:S(2)}, u32[]{:S(2)}) collective-permute-start(f32[4,136,128]{2,1,0:T(8,128)S(1)} %fusion.9), channel_id=1, source_target_pairs={{0,4},{4,8},{8,12},{1,5},{5,9},{9,13},{2,6},{6,10},{10,14},{3,7},{... | collective-permute-start | bytes 835592 | tf_op jit(solution)/shard_map/ppermute | solution.py:18
  17.8 10.1 %collective-permute-start.1 = (f32[4,128,128]{2,1,0:T(8,128)S(1)}, f32[4,128,128]{2,1,0:T(8,128)S(1)}, u32[]{:S(2)}, u32[]{:S(2)}) collective-permute-start(f32[4,128,128]{2,1,0:T(8,128)S(1)} %multiply_add_fusion.5), channel_id=1, source_target_pairs={{0,8},{4,12},{1,9},{5,13},{2,10},{6,14},{3,11},{7,15},{16,24},{20,... | collective-permute-start | bytes 786440 | tf_op jit(solution)/shard_map/ppermute | solution.py:18
  28.4 0.7 copy-start.2
  29.3 3.6 %collective-permute-start.2 = (f32[128]{0:T(128)S(1)}, f32[128]{0:T(128)S(1)}, u32[]{:S(2)}, u32[]{:S(2)}) collective-permute-start(f32[128]{0:T(128)S(1)} %convolution_bitcast_fusion.2), channel_id=1, source_target_pairs={{0,2},{2,0},{1,3},{3,1},{4,6},{6,4},{5,7},{7,5},{8,10},{10,8},{9,1... | collective-permute-start | bytes 1544 | tf_op jit(solution)/shard_map/ppermute | solution.py:28
  30.8 2.1 %copy-start.5 = (f32[1,128]{1,0:T(1,128)S(1)}, f32[1,128]{1,0:T(1,128)}, u32[]{:S(2)}) copy-start(f32[1,128]{1,0:T(1,128)} %param.20) | copy-start | bytes 1540
  34.7 14.6 %collective-permute-start.3 = (f32[4,136,128]{2,1,0:T(8,128)S(1)}, f32[4,136,128]{2,1,0:T(8,128)S(1)}, u32[]{:S(2)}, u32[]{:S(2)}) collective-permute-start(f32[4,136,128]{2,1,0:T(8,128)S(1)} %fusion.10), channel_id=1, source_target_pairs={{4,0},{8,4},{12,8},{5,1},{9,5},{13,9},{6,2},{10,6},{14,10},{7,3},{... | collective-permute-start | bytes 835592 | tf_op jit(solution)/shard_map/ppermute | solution.py:18
  49.5 14.8 %collective-permute-start.4 = (f32[4,128,128]{2,1,0:T(8,128)S(1)}, f32[4,128,128]{2,1,0:T(8,128)S(1)}, u32[]{:S(2)}, u32[]{:S(2)}) collective-permute-start(f32[4,128,128]{2,1,0:T(8,128)S(1)} %multiply_add_fusion.3), channel_id=1, source_target_pairs={{8,0},{12,4},{9,1},{13,5},{10,2},{14,6},{11,3},{15,7},{24,16},{28,... | collective-permute-start | bytes 786440 | tf_op jit(solution)/shard_map/ppermute | solution.py:18
  68.7 1.2 %collective-permute-start.5 = (f32[1024]{0:T(1024)S(1)}, f32[1024]{0:T(1024)S(1)}, u32[]{:S(2)}, u32[]{:S(2)}) collective-permute-start(f32[1024]{0:T(1024)S(1)} %maximum_multiply_fusion), channel_id=1, source_target_pairs={{0,1},{1,0},{2,3},{3,2},{4,5},{5,4},{6,7},{7,6},{8,9},{9,8},{10,11... | collective-permute-start | bytes 12296 | tf_op jit(solution)/shard_map/ppermute | solution.py:28
  70.0 7.0 %collective-permute-start.8 = (f32[1024]{0:T(1024)S(1)}, f32[1024]{0:T(1024)S(1)}, u32[]{:S(2)}, u32[]{:S(2)}) collective-permute-start(f32[1024]{0:T(1024)S(1)} %fusion.61), channel_id=1, source_target_pairs={{0,4},{4,8},{8,12},{12,0},{1,5},{5,9},{9,13},{13,1},{2,6},{6,10},{... | collective-permute-start | bytes 12296 | tf_op jit(solution)/shard_map/ppermute | solution.py:39
  70.0 7.0 %collective-permute-start.7 = (f32[1024]{0:T(1024)S(1)}, f32[1024]{0:T(1024)S(1)}, u32[]{:S(2)}, u32[]{:S(2)}) collective-permute-start(f32[1024]{0:T(1024)S(1)} %fusion.61), channel_id=1, source_target_pairs={{0,8},{4,12},{8,0},{12,4},{1,9},{5,13},{9,1},{13,5},{2,10},{6,14},... | collective-permute-start | bytes 12296 | tf_op jit(solution)/shard_map/ppermute | solution.py:39
  70.1 6.9 %collective-permute-start.6 = (f32[1024]{0:T(1024)S(1)}, f32[1024]{0:T(1024)S(1)}, u32[]{:S(2)}, u32[]{:S(2)}) collective-permute-start(f32[1024]{0:T(1024)S(1)} %fusion.61), channel_id=1, source_target_pairs={{0,12},{4,0},{8,4},{12,8},{1,13},{5,1},{9,5},{13,9},{2,14},{6,2},{... | collective-permute-start | bytes 12296 | tf_op jit(solution)/shard_map/ppermute | solution.py:39
